TPU v7x, 32 devices: a whole 2x2x4 slice. The times are simulated.
32 devices in a mesh: row: 2 (over x), col: 4 (over z), tok: 4 (over y, core).
Axes of the slice: x: 2, y: 2, z: 4, core: 2. Of those that a mesh axis runs over, the one named last changes fastest.
Arguments:
- activations: bfloat16 [4096, 2048], P(('row', 'col', 'tok')), may hold values from -6 to 6
- norm_gain: float32 [2048], replicated, may hold values from 0.1 to 1.9
- routes: int32 [4096, 8], P(('row', 'col', 'tok')), may hold values from 0 to 127, all different within a row; in each aligned block of 128 rows (0 to 127, 128 to 255, ...) at most 10 rows name the same one
- route_weights: float32 [4096, 8], P(('row', 'col', 'tok')), may hold values from 0.05 to 1
- gate_up_weight: bfloat16 [128, 2, 768, 2048], P(('row', 'col'), None, 'tok'), may hold values from -0.125 to 0.125
- down_weight: bfloat16 [128, 768, 2048], P(('row', 'col'), 'tok'), may hold values from -0.21875 to 0.21875
Outputs:
- expert_mix: bfloat16 [4096, 2048], P(('row', 'col', 'tok'))
Inputs may be any that keep to these rules, and one draw needn't show every extreme that they name: `routes`: within the rows of one device no expert is named by more than 10 rows, a bound that some block reaches.
All inputs are finite; a program needn't handle non-finite values.
Results may differ from a plain program's by a relative error of at most 0.0085.
Values may be sent and summed in bfloat16 or wider, within the bound.
No kernel may reach another device: no remote copies, remote signals or barrier semaphores. Data moves between devices by JAX's collectives and lax.ppermute only.
A program may use at most 384 MiB of HBM per device.

v0:
```python
import jax
import jax.numpy as jnp
from jax import lax
from jax.sharding import PartitionSpec as P

CAP = 10


EPSILON = 1e-06


def rank_in_block(block_routes, experts):
    onehot = (block_routes[:, None] == jnp.arange(experts, dtype=jnp.int32)[None, :]).astype(
        jnp.int32
    )
    before = jnp.cumsum(onehot, axis=0) - onehot
    return jnp.sum(before * onehot, axis=1)


def rms_normed(activations, norm_gain):
    values = activations.astype(jnp.float32)
    scale = lax.rsqrt(jnp.mean(values * values, axis=-1, keepdims=True) + EPSILON)
    return (values * scale * norm_gain).astype(jnp.bfloat16)


def apply_experts(received, gate_up_weight, down_weight):
    both = jnp.einsum(
        "sjcd,jgfd->sjcgf",
        received,
        lax.all_gather(gate_up_weight, "tok", axis=2, tiled=True),
        preferred_element_type=jnp.float32,
    )
    hidden = (jax.nn.silu(both[:, :, :, 0, :]) * both[:, :, :, 1, :]).astype(jnp.bfloat16)
    summed = jnp.einsum(
        "sjcf,jfd->sjcd",
        hidden,
        lax.all_gather(down_weight, "tok", axis=1, tiled=True),
        preferred_element_type=jnp.float32,
    )
    return summed.astype(jnp.bfloat16)


def local(activations, norm_gain, routes, route_weights, gate_up_weight, down_weight):
    count, features = activations.shape
    chosen = routes.shape[1]
    holding = gate_up_weight.shape[0]
    row_count = lax.axis_size("row")
    col_count = lax.axis_size("col")
    owners = row_count * col_count
    experts = holding * owners
    normed = rms_normed(activations, norm_gain)
    gates = route_weights / jnp.sum(route_weights, axis=1, keepdims=True)
    flat_routes = routes.reshape(-1)
    target = flat_routes * CAP + rank_in_block(flat_routes, experts)
    token_ids = jnp.arange(count * chosen, dtype=jnp.int32) // chosen
    source = jnp.full((experts * CAP,), count, jnp.int32).at[target].set(token_ids)
    outbound = jnp.take(normed, source, axis=0, mode="fill", fill_value=0)
    outbound = outbound.reshape(owners, holding, CAP, features)
    arrived = lax.all_to_all(outbound, ("row", "col"), split_axis=0, concat_axis=0, tiled=True)
    results = apply_experts(arrived, gate_up_weight, down_weight)
    returned = lax.all_to_all(results, ("row", "col"), split_axis=0, concat_axis=0, tiled=True)
    picked = jnp.take(returned.reshape(experts * CAP, features), target, axis=0)
    picked = picked.reshape(count, chosen, features)
    mixed = jnp.einsum("tk,tkd->td", gates, picked.astype(jnp.float32))
    return mixed.astype(jnp.bfloat16)


def solution(mesh):
    in_specs = (
        P(("row", "col", "tok"), None),
        P(),
        P(("row", "col", "tok"), None),
        P(("row", "col", "tok"), None),
        P(("row", "col"), None, "tok", None),
        P(("row", "col"), "tok", None),
    )
    out_specs = P(("row", "col", "tok"), None)
    return jax.shard_map(local, mesh=mesh, in_specs=in_specs, out_specs=out_specs, check_vma=False)
```

profile of v0, /device:TPU:0, one launch (start us, length us, event | category | flops | bytes accessed | tf_op | source)
XLA Modules:
  0.0 1096.7 jit_solution(4971576280621673986)
XLA Ops:
  6.5 0.0 all-gather.3.cloned.1.call-start
  6.5 0.7 all-gather.3.cloned.1.call-update
  7.3 0.0 copy-start.3
  7.3 0.0 copy-start
  7.3 0.0 copy-start.8
  7.3 0.0 all-gather.5.cloned.1.call-start
  7.3 0.7 all-gather.5.cloned.1.call-update
  8.0 0.0 copy-done.3
  8.0 0.1 copy.28
  8.1 0.1 eq.26
  8.2 0.1 reshape.87
  8.3 0.1 copy.30
  8.4 0.2 fusion.24
  8.7 0.1 copy.31
  8.9 0.1 copy.34
  9.0 0.1 mul.51
  9.1 0.4 fusion.23
  9.4 0.0 copy-start.1
  9.5 0.6 copy-done.1
  10.0 4.3 scatter_custom_fusion
  14.3 0.0 copy-done.5
  14.4 0.0 copy-done
  14.4 0.2 fusion.19
  14.6 0.0 copy-done.8
  14.6 0.2 fusion.21
  14.8 6.2 gather_fusion
  21.0 10.5 gather.13
  31.6 0.2 broadcast_in_dim.34
  31.8 12.9 %broadcast_select_fusion = bf16[8,16,10,2048]{3,2,1,0:T(8,128)(2,1)} fusion(bf16[8,16,10,2048]{3,2,1,0:T(8,128)(2,1)} %gather.13, pred[8,16,10]{2,1,0:T(8,128)(4,1)S(1)} %broadcast_in_dim.34), kind=kLoop, calls=%fused_computation.9 | loop fusion | flops 2621440 | bytes 10487040 | tf_op jit(solution)/shard_map/jit(_take)/select_n | solution.py:57
  44.6 8.0 copy.35
  52.6 123.2 %all_to_all.10 = bf16[8,16,10,2048]{3,1,2,0:T(8,128)(2,1)} all-to-all(bf16[8,16,10,2048]{3,1,2,0:T(8,128)(2,1)S(1)} %copy.35), channel_id=1, replica_groups=mesh['row'=2,'col'=4,'tok'=4] {'row','col'}, dimensions={0} | all-to-all | bytes 10485760 | tf_op jit(solution)/shard_map/all_to_all | solution.py:59
  175.9 421.0 %all-gather.3.cloned.1.call-done = bf16[16,2,768,2048]{3,2,1,0:T(8,128)(2,1)} async-done(((bf16[16,2,192,2048]{3,2,1,0:T(8,128)(2,1)}), bf16[16,2,768,2048]{3,2,1,0:T(8,128)(2,1)}) %all-gather.3.cloned.1.call-update) | async-done | bytes 100663312 | tf_op jit(solution)/shard_map/all_gather | solution.py:30
  596.9 58.9 %fusion.9 = f32[8,16,10,2,768]{4,2,3,0,1:T(8,128)} fusion(bf16[16,2,768,2048]{3,2,1,0:T(8,128)(2,1)} %all-gather.3.cloned.1.call-done, bf16[8,16,10,2048,1]{3,1,2,0,4:T(8,128)(2,1)} %bitcast.54), kind=kOutput, calls=%fused_computation.14 | convolution fusion | flops 8053063680 | bytes 113770496 | tf_op jit(solution)/shard_map/sjcd,jgfd->sjcgf/dot_general | solution.py:27
  655.8 241.6 %all-gather.5.cloned.1.call-done = bf16[16,768,2048]{2,1,0:T(8,128)(2,1)} async-done(((bf16[16,192,2048]{2,1,0:T(8,128)(2,1)}), bf16[16,768,2048]{2,1,0:T(8,128)(2,1)}) %all-gather.5.cloned.1.call-update) | async-done | bytes 50331664 | tf_op jit(solution)/shard_map/all_gather | solution.py:37
  897.5 24.4 %convert_bitcast_fusion = bf16[8,16,10,2048]{3,2,0,1:T(8,128)(2,1)} fusion(bf16[16,768,2048]{2,1,0:T(8,128)(2,1)} %all-gather.5.cloned.1.call-done, f32[8,16,10,2,768]{4,2,3,0,1:T(8,128)} %fusion.9), kind=kOutput, calls=%fused_computation.8 | convolution fusion | flops 4035051520 | bytes 63438848 | tf_op jit(solution)/shard_map/sjcf,jfd->sjcd/dot_general | solution.py:34
  921.9 9.1 copy.38
  931.0 5.6 all-to-all-start.1
  936.6 0.0 copy-done.2
  936.6 0.1 reduce_sum.33
  936.7 0.0 copy-done.4
  936.8 0.1 copy.33
  936.9 0.1 copy.43
  937.1 116.6 %all-to-all-done.1 = bf16[8,16,10,2048]{3,1,2,0:T(8,128)(2,1)} async-done(((bf16[8,16,10,2048]{3,1,2,0:T(8,128)(2,1)}), bf16[8,16,10,2048]{3,1,2,0:T(8,128)(2,1)}, u32[]{:S(2)}, u32[]{:S(2)}) %all-to-all-start.1) | async-done | bytes 5242912 | tf_op jit(solution)/shard_map/all_to_all | solution.py:61
  1053.6 9.7 copy.39
  1063.4 9.8 reshape.89
  1073.2 12.0 %gather_fusion.1 = bf16[1024,2048]{1,0:T(8,128)(2,1)} fusion(bf16[1280,2048]{1,0:T(8,128)(2,1)} %reshape.89, s32[1024]{0:T(1024)S(1)} %broadcast_clamp_fusion), kind=kCustom, calls=%fused_computation.1 | custom fusion | bytes 8392704 | tf_op jit(solution)/shard_map/jit(_take)/gather | solution.py:62
  1085.2 3.5 fusion.14
  1088.7 1.1 copy.53
  (23 shorter events, 0.2 us)
Async XLA Ops:
  6.5 590.4 %all-gather.3.cloned.1.call-start = ((), (), s32[]{:S(2)}) async-start(), calls=%async_computation.2 | async-start | bytes 125829120 | tf_op jit(solution)/shard_map/all_gather | solution.py:30
  7.3 0.8 copy-start.3
  7.3 7.1 copy-start
  7.3 7.3 copy-start.8
  7.3 890.2 %all-gather.5.cloned.1.call-start = ((), (), s32[]{:S(2)}) async-start(), calls=%async_computation.3 | async-start | bytes 62914560 | tf_op jit(solution)/shard_map/all_gather | solution.py:37
  9.4 0.6 copy-start.1
  10.0 4.3 copy-start.5
  930.9 5.6 copy-start.2
  930.9 5.8 copy-start.4
  930.9 5.9 copy-start.7
  930.9 6.1 copy-start.6
  931.0 122.7 %all-to-all-start.1 = ((bf16[8,16,10,2048]{3,1,2,0:T(8,128)(2,1)}), bf16[8,16,10,2048]{3,1,2,0:T(8,128)(2,1)}, u32[]{:S(2)}, u32[]{:S(2)}) async-start(bf16[8,16,10,2048]{3,1,2,0:T(8,128)(2,1)} %copy.38), calls=%async_computation.1 | async-start | bytes 10485760 | tf_op jit(solution)/shard_map/all_to_all | solution.py:61
Sparse Core Ops, SparseCore 0:
  8.9 587.9 all-gather.2
  598.5 298.9 all-gather.4
where the time goes:
time: 1100 us
  waiting for transfers between devices  781 us (71%)
  blocking collectives  123 us (11%)
  matrix products  86.8 us (8%)
  local copies, waits for them, and re-layouts  72.7 us (7%)
  other arithmetic  14 us (1%)
  between operations  13.6 us (1%)
    all_gather x1, waiting for transfers between devices, apply_experts(): lax.all_gather(gate_up_weight, 'tok', axis=2, tiled=True)  421 us
    all_gather x1, waiting for transfers between devices, apply_experts(): lax.all_gather(down_weight, 'tok', axis=1, tiled=True)  242 us
    all_to_all x1, blocking collectives, local(): lax.all_to_all(outbound, ('row', 'col'), split_axis=0, concat_axis=0, til...  123 us
    all_to_all x1, waiting for transfers between devices, local(): lax.all_to_all(results, ('row', 'col'), split_axis=0, concat_axis=0, tile...  117 us
    dot_general x1, matrix products, apply_experts(): jnp.einsum('sjcd,jgfd->sjcgf', received, lax.all_gather(gate_up_weight, '...  58.9 us
    dot_general x1, matrix products, apply_experts(): jnp.einsum('sjcf,jfd->sjcd', hidden, lax.all_gather(down_weight, 'tok', a...  24.4 us
  transfers between devices with their start and end apart: 3, of which 3 were waited for; matrix products, arithmetic and copies ran while one was open for 9% of the time, Pallas kernels for 0%

commit v1 on v0

v1 whole, which is shorter than its diff:
```python
import jax
import jax.numpy as jnp
from jax import lax
from jax.sharding import PartitionSpec as P

CAP = 10


EPSILON = 1e-06

ALL = ("row", "col", "tok")


def rank_in_block(block_routes, experts):
    onehot = (block_routes[:, None] == jnp.arange(experts, dtype=jnp.int32)[None, :]).astype(
        jnp.int32
    )
    before = jnp.cumsum(onehot, axis=0) - onehot
    return jnp.sum(before * onehot, axis=1)


def rms_normed(activations, norm_gain):
    values = activations.astype(jnp.float32)
    scale = lax.rsqrt(jnp.mean(values * values, axis=-1, keepdims=True) + EPSILON)
    return (values * scale * norm_gain).astype(jnp.bfloat16)


def local(activations, norm_gain, routes, route_weights, gate_up_weight, down_weight):
    count, features = activations.shape
    chosen = routes.shape[1]
    holding = gate_up_weight.shape[0]
    row_count = lax.axis_size("row")
    col_count = lax.axis_size("col")
    tok_count = lax.axis_size("tok")
    owners = row_count * col_count
    experts = holding * owners
    devices = owners * tok_count
    owner = lax.axis_index("row") * col_count + lax.axis_index("col")

    normed = rms_normed(activations, norm_gain)
    gates = route_weights / jnp.sum(route_weights, axis=1, keepdims=True)
    flat_routes = routes.reshape(-1)
    target = flat_routes * CAP + rank_in_block(flat_routes, experts)

    every_normed = lax.all_gather(normed, ALL, axis=0, tiled=True)
    every_target = lax.all_gather(target, ALL, axis=0, tiled=False)

    source = jnp.arange(devices, dtype=jnp.int32)[:, None]
    pair = jnp.arange(count * chosen, dtype=jnp.int32)[None, :]
    expert = every_target // CAP
    rank = every_target % CAP
    mine = expert // holding == owner
    slot = (
        ((source % tok_count) * owners + source // tok_count) * holding + expert % holding
    ) * CAP + rank
    slots = tok_count * owners * holding * CAP
    slot = jnp.where(mine, slot, slots)
    token = source * count + pair // chosen
    table = jnp.full((slots,), devices * count, jnp.int32).at[slot.reshape(-1)].set(
        token.reshape(-1), mode="drop"
    )
    picked = jnp.take(every_normed, table, axis=0, mode="fill", fill_value=0)
    picked = picked.reshape(tok_count * owners, holding, CAP, features)

    both = jnp.einsum(
        "sjcd,jgfd->sjcgf", picked, gate_up_weight, preferred_element_type=jnp.float32
    )
    hidden = (jax.nn.silu(both[:, :, :, 0, :]) * both[:, :, :, 1, :]).astype(jnp.bfloat16)
    partial = jnp.einsum(
        "sjcf,jfd->sjcd", hidden, down_weight, preferred_element_type=jnp.float32
    )
    summed = lax.psum_scatter(partial, "tok", scatter_dimension=0, tiled=True)
    results = summed.astype(jnp.bfloat16)

    returned = lax.all_to_all(results, ("row", "col"), split_axis=0, concat_axis=0, tiled=True)
    picked_back = jnp.take(returned.reshape(experts * CAP, features), target, axis=0)
    picked_back = picked_back.reshape(count, chosen, features)
    mixed = jnp.einsum("tk,tkd->td", gates, picked_back.astype(jnp.float32))
    return mixed.astype(jnp.bfloat16)


def solution(mesh):
    in_specs = (
        P(("row", "col", "tok"), None),
        P(),
        P(("row", "col", "tok"), None),
        P(("row", "col", "tok"), None),
        P(("row", "col"), None, "tok", None),
        P(("row", "col"), "tok", None),
    )
    out_specs = P(("row", "col", "tok"), None)
    return jax.shard_map(local, mesh=mesh, in_specs=in_specs, out_specs=out_specs, check_vma=False)
```

time: 1100 us -> 801 us (0.73)
  waiting for transfers between devices: 781 us -> 401 us
  local copies, waits for them, and re-layouts: 72.7 us -> 241 us
  blocking collectives: 123 us -> 44.2 us
  matrix products: 86.8 us -> 60.4 us
  other arithmetic: 14 us -> 33 us
    all_gather x2 -> x1, waiting for transfers between devices: 663 us -> 0.02 us  [local(): every_normed = lax.all_gather(normed, ALL, axis=0, tiled=True)]
    reduce_scatter x0 -> x1, waiting for transfers between devices: none -> 285 us  [local(): summed = lax.psum_scatter(partial, 'tok', scatter_dimension=0, tiled=True)]
    all_to_all x1 -> x0, blocking collectives: 123 us -> none  [local(): lax.all_to_all(outbound, ('row', 'col'), split_axis=0, concat_axis=0, til...]
    scatter x1, local copies, waits for them, and re-layouts: 4.31 us -> 120 us  [local(): jnp.full((slots,), devices * count, jnp.int32).at[slot.reshape(-1)]]
    gather x3, local copies, waits for them, and re-layouts: 28.8 us -> 92.8 us  [the longest x2 80.8 us: local(): picked = jnp.take(every_normed, table, axis=0, mode='fill', fill_value=0)]
    all_gather x0 -> x1, blocking collectives: none -> 44.2 us  [local(): every_target = lax.all_gather(target, ALL, axis=0, tiled=False)]
    dot_general x3, matrix products: 86.8 us -> 60.4 us  [the longest x1 34.1 us: local(): jnp.einsum('sjcd,jgfd->sjcgf', picked, gate_up_weight, preferred_element_...]
  transfers between devices with their start and end apart: 3 -> 3, of which waited for: 3 -> 2; matrix products, arithmetic and copies ran while one was open for 9% -> 16% of each run, Pallas kernels for 0% -> 0%
where the time goes in v1:
time: 801 us; the launch traced here: 800 us
  waiting for transfers between devices  401 us (50%)
  local copies, waits for them, and re-layouts  241 us (30%)
  matrix products  60.4 us (8%)
  blocking collectives  44.2 us (6%)
  other arithmetic  33 us (4%)
  between operations  13.7 us (2%)
    reduce_scatter x1, waiting for transfers between devices, local(): summed = lax.psum_scatter(partial, 'tok', scatter_dimension=0, tiled=True)  285 us
    scatter x1, local copies, waits for them, and re-layouts, local(): jnp.full((slots,), devices * count, jnp.int32).at[slot.reshape(-1)]  120 us
    all_to_all x1, waiting for transfers between devices, local(): lax.all_to_all(results, ('row', 'col'), split_axis=0, concat_axis=0, tile...  116 us
    gather x2, local copies, waits for them, and re-layouts, local(): picked = jnp.take(every_normed, table, axis=0, mode='fill', fill_value=0)  80.8 us
    all_gather x1, blocking collectives, local(): every_target = lax.all_gather(target, ALL, axis=0, tiled=False)  44.2 us
    dot_general x1, matrix products, local(): jnp.einsum('sjcd,jgfd->sjcgf', picked, gate_up_weight, preferred_element_...  34.1 us
    dot_general x1, matrix products, local(): jnp.einsum('sjcf,jfd->sjcd', hidden, down_weight, preferred_element_type=...  22.9 us
    select_n x1, other arithmetic, local(): picked = jnp.take(every_normed, table, axis=0, mode='fill', fill_value=0)  22.7 us
  transfers between devices with their start and end apart: 3, of which 2 were waited for; matrix products, arithmetic and copies ran while one was open for 16% of the time, Pallas kernels for 0%

profile of v1, /device:TPU:0, one launch (start us, length us, event | category | flops | bytes accessed | tf_op | source)
XLA Modules:
  0.0 799.6 jit_solution(5752293919866283598)
XLA Ops:
  6.5 0.0 all-gather.3.cloned.1.call-start
  6.5 1.2 fusion.16
  7.8 2.0 fusion.18
  9.8 0.0 all-gather.3.cloned.1.call-update
  9.8 0.0 reduce-scatter.2.cloned.1.call-start
  9.9 0.8 copy.47
  10.7 0.1 eq.37
  10.8 0.1 reshape.240
  10.9 0.1 copy.49
  11.0 0.2 fusion.21
  11.3 0.1 copy.50
  11.4 0.7 broadcast_multiply_fusion
  12.1 0.1 copy.53
  12.2 0.1 mul.101
  12.3 0.4 fusion.20
  12.6 0.0 copy-start.2
  12.7 44.2 %all-gather = s32[32,1,1024]{2,1,0:T(1,128)S(1)} all-gather(s32[1,1,1024]{2,1,0:T(1,128)S(1)} %add_bitcast_fusion.1), channel_id=1, replica_groups=mesh['row'=2,'col'=4,'tok'=4] {'row','col','tok'}, dimensions={0}, use_global_device_ids=true | all-gather | bytes 135168 | tf_op jit(solution)/shard_map/all_gather | solution.py:46
  56.9 0.3 broadcast_remainder_fusion
  57.2 0.3 fusion.29
  57.5 0.1 copy.71
  57.6 0.1 add_bitcast_fusion
  57.7 0.1 compare_select_fusion
  57.9 120.3 %scatter_custom_fusion = s32[5120]{0:T(1024)S(1)} fusion(s32[32768]{0:T(1024)S(1)} %bitcast.89, s32[32768]{0:T(1024)S(1)} %bitcast.88, s32[]{:T(128)} %constant.127.clone.1), kind=kCustom, calls=%fused_computation.64 | custom fusion | bytes 20484 | tf_op jit(solution)/shard_map/scatter | solution.py:59
  178.2 0.3 broadcast_in_dim.41
  178.5 0.0 all-gather.3.cloned.1.call-done
  178.5 46.8 %gather_fusion = bf16[5120,2048]{1,0:T(8,128)(2,1)} fusion(bf16[4096,2048]{1,0:T(8,128)(2,1)} %all-gather.3.cloned.1.call-done, s32[5120]{0:T(1024)S(1)} %fusion.35), kind=kCustom, calls=%fused_computation | custom fusion | bytes 41963520 | tf_op jit(solution)/shard_map/jit(_take)/gather | solution.py:62
  225.3 34.0 %gather.13 = bf16[32,16,10,2048]{3,2,1,0:T(8,128)(2,1)} reshape(bf16[5120,2048]{1,0:T(8,128)(2,1)} %gather_fusion) | data formatting | bytes 41943040 | tf_op jit(solution)/shard_map/jit(_take)/gather | solution.py:62
  259.3 22.7 %select_bitcast_fusion = bf16[32,16,10,2048,1]{3,2,1,0,4:T(8,128)(2,1)} fusion(bf16[32,16,10,2048]{3,2,1,0:T(8,128)(2,1)} %gather.13, pred[32,16,10]{2,1,0:T(8,128)(4,1)S(1)} %broadcast_in_dim.41), kind=kLoop, calls=%fused_computation.3 | loop fusion | flops 10485760 | bytes 41948160 | tf_op jit(solution)/shard_map/jit(_take)/select_n | solution.py:62
  282.1 34.1 %fusion.8 = f32[32,16,10,2,192]{4,0,3,2,1:T(8,128)} fusion(bf16[16,2,192,2048]{3,2,1,0:T(8,128)(2,1)} %param.10, bf16[32,16,10,2048,1]{3,2,1,0,4:T(8,128)(2,1)} %select_bitcast_fusion), kind=kOutput, calls=%fused_computation.16 | convolution fusion | flops 8053063680 | bytes 54001664 | tf_op jit(solution)/shard_map/sjcd,jgfd->sjcgf/dot_general | solution.py:65
  316.2 22.9 %convolution_bitcast_fusion = f32[32,16,10,2048]{3,0,2,1:T(8,128)} fusion(bf16[16,192,2048]{2,1,0:T(8,128)(2,1)} %param.11, f32[32,16,10,2,192]{4,0,3,2,1:T(8,128)} %fusion.8), kind=kOutput, calls=%fused_computation.7 | convolution fusion | flops 4032430080 | bytes 62390272 | tf_op jit(solution)/shard_map/sjcf,jfd->sjcd/dot_general | solution.py:69
  339.0 0.0 reduce-scatter.2.cloned.1.call-update
  339.0 285.4 %reduce-scatter.2.cloned.1.call-done = f32[8,16,10,2048]{3,0,2,1:T(8,128)} async-done(((f32[32,16,10,2048]{3,0,2,1:T(8,128)}), f32[8,16,10,2048]{3,0,2,1:T(8,128)}) %reduce-scatter.2.cloned.1.call-update) | async-done | bytes 10485776 | tf_op jit(solution)/shard_map/reduce_scatter | solution.py:72
  624.4 4.8 convert_element_type.28
  629.2 0.0 copy-start.4
  629.2 0.0 copy-start.5
  629.2 5.2 copy.59
  634.4 5.5 all-to-all-start
  639.9 0.1 mul.117
  640.0 0.0 copy-done.3
  640.0 0.1 reduce_sum.35
  640.2 0.1 copy.52
  640.4 0.1 copy.65
  640.5 116.0 %all-to-all-done = bf16[8,16,10,2048]{3,1,2,0:T(8,128)(2,1)} async-done(((bf16[8,16,10,2048]{3,1,2,0:T(8,128)(2,1)}), bf16[8,16,10,2048]{3,1,2,0:T(8,128)(2,1)}, u32[]{:S(2)}, u32[]{:S(2)}) %all-to-all-start) | async-done | bytes 5242912 | tf_op jit(solution)/shard_map/all_to_all | solution.py:75
  756.6 9.7 %copy.60 = bf16[8,16,10,2048]{3,2,1,0:T(8,128)(2,1)} copy(bf16[8,16,10,2048]{3,1,2,0:T(8,128)(2,1)} %all-to-all-done) | data formatting | bytes 10485760 | tf_op jit(solution)/shard_map/all_to_all | solution.py:75
  766.3 9.8 %reshape.243 = bf16[1280,2048]{1,0:T(8,128)(2,1)} reshape(bf16[8,16,10,2048]{3,2,1,0:T(8,128)(2,1)} %copy.60) | data formatting | bytes 10485760 | tf_op jit(solution)/shard_map/reshape | solution.py:76
  776.1 12.0 %gather_fusion.1 = bf16[1024,2048]{1,0:T(8,128)(2,1)} fusion(bf16[1280,2048]{1,0:T(8,128)(2,1)} %reshape.243, s32[1024]{0:T(1024)S(1)} %broadcast_clamp_fusion), kind=kCustom, calls=%fused_computation.1 | custom fusion | bytes 8392704 | tf_op jit(solution)/shard_map/jit(_take)/gather | solution.py:76
  788.1 3.5 fusion.6
  791.6 1.1 copy.82
  (26 shorter events, 0.3 us)
Async XLA Ops:
  6.5 172.0 %all-gather.3.cloned.1.call-start = ((), (), s32[]{:S(2)}) async-start(), calls=%async_computation.2 | async-start | bytes 17301504 | tf_op jit(solution)/shard_map/all_gather | solution.py:45
  9.8 614.6 %reduce-scatter.2.cloned.1.call-start = ((), (), s32[]{:S(2)}) async-start(), calls=%async_computation.3 | async-start | bytes 52428800 | tf_op jit(solution)/shard_map/reduce_scatter | solution.py:72
  12.2 213.1 %copy-start = (s32[128,8]{1,0:T(8,128)}, s32[128,8]{1,0:T(8,128)S(1)}, u32[]{:S(2)}) copy-start(s32[128,8]{1,0:T(8,128)S(1)} %copy.53) | copy-start | bytes 12292
  12.6 45.3 %copy-start.2 = (s32[1024]{0:T(1024)}, s32[1024]{0:T(1024)S(1)}, u32[]{:S(2)}) copy-start(s32[1024]{0:T(1024)S(1)} %fusion.20) | copy-start | bytes 12292
  629.2 10.7 %copy-start.1 = (s32[128,8]{1,0:T(8,128)S(1)}, s32[128,8]{1,0:T(8,128)}, u32[]{:S(2)}) copy-start(s32[128,8]{1,0:T(8,128)} %copy-done) | copy-start | bytes 12292
  629.2 10.8 %copy-start.3 = (s32[1024]{0:T(1024)S(1)}, s32[1024]{0:T(1024)}, u32[]{:S(2)}) copy-start(s32[1024]{0:T(1024)} %copy-done.2) | copy-start | bytes 12292
  629.2 11.0 %copy-start.4 = (s32[128,8]{0,1:T(8,128)S(1)}, s32[128,8]{0,1:T(8,128)}, u32[]{:S(2)}) copy-start(s32[128,8]{0,1:T(8,128)} %param.8) | copy-start | bytes 12292
  629.2 11.1 %copy-start.5 = (f32[128,8]{0,1:T(8,128)S(1)}, f32[128,8]{0,1:T(8,128)}, u32[]{:S(2)}) copy-start(f32[128,8]{0,1:T(8,128)} %param.9) | copy-start | bytes 12292
  634.4 122.1 %all-to-all-start = ((bf16[8,16,10,2048]{3,1,2,0:T(8,128)(2,1)}), bf16[8,16,10,2048]{3,1,2,0:T(8,128)(2,1)}, u32[]{:S(2)}, u32[]{:S(2)}) async-start(bf16[8,16,10,2048]{3,1,2,0:T(8,128)(2,1)} %copy.59), calls=%async_computation.1 | async-start | bytes 10485760 | tf_op jit(solution)/shard_map/all_to_all | solution.py:75
Sparse Core Ops, SparseCore 0:
  10.2 117.7 all-gather.2
  339.1 285.1 reduce-scatter.1

commit v2 on v1

v2 whole, which is shorter than its diff:
```python
import jax
import jax.numpy as jnp
from jax import lax
from jax.sharding import PartitionSpec as P

CAP = 10


EPSILON = 1e-06

ALL = ("row", "col", "tok")


def rank_in_block(block_routes, experts):
    onehot = (block_routes[:, None] == jnp.arange(experts, dtype=jnp.int32)[None, :]).astype(
        jnp.int32
    )
    before = jnp.cumsum(onehot, axis=0) - onehot
    return jnp.sum(before * onehot, axis=1)


def rms_normed(activations, norm_gain):
    values = activations.astype(jnp.float32)
    scale = lax.rsqrt(jnp.mean(values * values, axis=-1, keepdims=True) + EPSILON)
    return (values * scale * norm_gain).astype(jnp.bfloat16)


def local(activations, norm_gain, routes, route_weights, gate_up_weight, down_weight):
    count, features = activations.shape
    chosen = routes.shape[1]
    holding = gate_up_weight.shape[0]
    row_count = lax.axis_size("row")
    col_count = lax.axis_size("col")
    tok_count = lax.axis_size("tok")
    owners = row_count * col_count
    experts = holding * owners
    devices = owners * tok_count
    owner = lax.axis_index("row") * col_count + lax.axis_index("col")
    assert count < 256

    normed = rms_normed(activations, norm_gain)
    gates = route_weights / jnp.sum(route_weights, axis=1, keepdims=True)
    flat_routes = routes.reshape(-1)
    target = flat_routes * CAP + rank_in_block(flat_routes, experts)
    token_ids = jnp.arange(count * chosen, dtype=jnp.int32) // chosen
    source = jnp.full((experts * CAP,), count, jnp.int32).at[target].set(token_ids)

    extra = -(-(experts * CAP) // features)
    extra = -(-extra // 8) * 8
    stride = count + extra
    table_rows = jnp.zeros((extra * features,), jnp.bfloat16)
    table_rows = table_rows.at[: experts * CAP].set(source.astype(jnp.bfloat16))
    packed = jnp.concatenate([normed, table_rows.reshape(extra, features)], axis=0)
    every = lax.all_gather(packed, ALL, axis=0, tiled=True)

    tables = every.reshape(devices, stride, features)[:, count:, :].reshape(devices, -1)
    tables = lax.dynamic_slice_in_dim(
        tables[:, : experts * CAP], owner * holding * CAP, holding * CAP, axis=1
    ).astype(jnp.int32)
    rows = tables + (jnp.arange(devices, dtype=jnp.int32) * stride)[:, None]
    rows = rows.reshape(owners, tok_count, holding, CAP).transpose(2, 1, 0, 3).reshape(-1)
    picked = jnp.take(every, rows, axis=0, mode="clip")
    picked = picked.reshape(holding, tok_count * owners * CAP, features)

    both = jnp.einsum(
        "jrd,jgfd->jrgf", picked, gate_up_weight, preferred_element_type=jnp.float32
    )
    hidden = (jax.nn.silu(both[:, :, 0, :]) * both[:, :, 1, :]).astype(jnp.bfloat16)
    partial = jnp.einsum(
        "jrf,jfd->rjd", hidden, down_weight, preferred_element_type=jnp.float32
    )
    partial = partial.astype(jnp.bfloat16).reshape(tok_count * owners, CAP, holding, features)
    summed = lax.psum_scatter(partial, "tok", scatter_dimension=0, tiled=True)

    returned = lax.all_to_all(summed, ("row", "col"), split_axis=0, concat_axis=0, tiled=True)
    expert = target // CAP
    back = (expert // holding) * (CAP * holding) + (target % CAP) * holding + expert % holding
    picked_back = jnp.take(returned.reshape(experts * CAP, features), back, axis=0)
    picked_back = picked_back.reshape(count, chosen, features)
    mixed = jnp.einsum("tk,tkd->td", gates, picked_back.astype(jnp.float32))
    return mixed.astype(jnp.bfloat16)


def solution(mesh):
    in_specs = (
        P(("row", "col", "tok"), None),
        P(),
        P(("row", "col", "tok"), None),
        P(("row", "col", "tok"), None),
        P(("row", "col"), None, "tok", None),
        P(("row", "col"), "tok", None),
    )
    out_specs = P(("row", "col", "tok"), None)
    return jax.shard_map(local, mesh=mesh, in_specs=in_specs, out_specs=out_specs, check_vma=False)
```

time: 801 us -> 555 us (0.69)
  local copies, waits for them, and re-layouts: 241 us -> 91.6 us
  blocking collectives: 44.2 us -> 0 us
  other arithmetic: 33 us -> 4.9 us
  matrix products: 60.4 us -> 48.1 us
  waiting for transfers between devices: 401 us -> 390 us
    reduce_scatter x1, waiting for transfers between devices: 285 us -> 151 us  [local(): summed = lax.psum_scatter(partial, 'tok', scatter_dimension=0, tiled=True)]
    all_gather x1, waiting for transfers between devices: 0.02 us -> 122 us  [local(): every = lax.all_gather(packed, ALL, axis=0, tiled=True)]
    scatter x1 -> x2, local copies, waits for them, and re-layouts: 120 us -> 4.32 us  [the longest x1 4.32 us: local(): jnp.full((experts * CAP,), count, jnp.int32).at[target].set(token_ids)]
    all_gather x1 -> x0, blocking collectives: 44.2 us -> none  [local(): every_target = lax.all_gather(target, ALL, axis=0, tiled=False)]
    gather x3 -> x2, local copies, waits for them, and re-layouts: 92.8 us -> 59.3 us  [the longest x1 47.2 us: local(): picked = jnp.take(every, rows, axis=0, mode='clip')]
    select_n x4 -> x2, other arithmetic: 22.9 us -> 0.09 us  [the longest x1 0.08 us: local(): jnp.take(returned.reshape(experts * CAP, features), back, axis=0)]
    convert_element_type x1, local copies, waits for them, and re-layouts: 5.18 us -> 22.7 us  [local(): partial.astype(jnp.bfloat16)]
    dot_general x2, matrix products: 56.9 us -> 44.6 us  [the longest x1 27.3 us: local(): jnp.einsum('jrd,jgfd->jrgf', picked, gate_up_weight, preferred_element_ty...]
  transfers between devices with their start and end apart: 3 -> 3, of which waited for: 2 -> 3; matrix products, arithmetic and copies ran while one was open for 16% -> 0% of each run, Pallas kernels for 0% -> 0%
where the time goes in v2:
time: 555 us; the launch traced here: 554 us
  waiting for transfers between devices  390 us (70%)
  local copies, waits for them, and re-layouts  91.6 us (17%)
  matrix products  48.1 us (9%)
  between operations  13.6 us (2%)
  starting transfers between devices  5.75 us (1%)
    reduce_scatter x1, waiting for transfers between devices, local(): summed = lax.psum_scatter(partial, 'tok', scatter_dimension=0, tiled=True)  151 us
    all_gather x1, waiting for transfers between devices, local(): every = lax.all_gather(packed, ALL, axis=0, tiled=True)  122 us
    all_to_all x1, waiting for transfers between devices, local(): lax.all_to_all(summed, ('row', 'col'), split_axis=0, concat_axis=0, tiled...  116 us
    gather x1, local copies, waits for them, and re-layouts, local(): picked = jnp.take(every, rows, axis=0, mode='clip')  47.2 us
    dot_general x1, matrix products, local(): jnp.einsum('jrd,jgfd->jrgf', picked, gate_up_weight, preferred_element_ty...  27.3 us
    convert_element_type x1, local copies, waits for them, and re-layouts, local(): partial.astype(jnp.bfloat16)  22.7 us
    dot_general x1, matrix products, local(): jnp.einsum('jrf,jfd->rjd', hidden, down_weight, preferred_element_type=jn...  17.3 us
    gather x1, local copies, waits for them, and re-layouts, local(): jnp.take(returned.reshape(experts * CAP, features), back, axis=0)  12 us
  transfers between devices with their start and end apart: 3, of which 3 were waited for; matrix products, arithmetic and copies ran while one was open for 0% of the time, Pallas kernels for 0%

profile of v2, /device:TPU:0, one launch (start us, length us, event | category | flops | bytes accessed | tf_op | source)
XLA Modules:
  0.0 553.9 jit_solution(12133837299108921005)
XLA Ops:
  6.5 0.0 all-gather.2.cloned.1.call-start
  6.5 0.8 copy.18
  7.3 0.1 eq.29
  7.4 0.1 reshape.250
  7.5 0.7 broadcast_multiply_fusion
  8.2 0.1 copy.20
  8.3 0.2 fusion.12
  8.6 0.1 copy.21
  8.7 0.1 copy.24
  8.8 0.1 mul.118
  8.9 0.4 fusion.11
  9.3 0.1 compare_select_fusion
  9.4 4.3 scatter_custom_fusion
  13.7 1.2 fusion.7
  15.0 1.2 fusion.9
  16.2 0.8 pad_maximum_fusion
  17.1 0.0 all-gather.2.cloned.1.call-update
  17.1 0.2 reduce-scatter.2.cloned.1.call-start
  17.3 122.4 %all-gather.2.cloned.1.call-done = bf16[4352,2048]{1,0:T(8,128)(2,1)} async-done(((bf16[136,2048]{1,0:T(8,128)(2,1)}), bf16[4352,2048]{1,0:T(8,128)(2,1)}) %all-gather.2.cloned.1.call-update) | async-done | bytes 17825808 | tf_op jit(solution)/shard_map/all_gather | solution.py:54
  139.8 1.3 slice.41
  141.1 0.6 copy.32
  141.7 0.1 convert_add_fusion
  141.8 0.2 reshape.255
  142.0 0.2 copy.25
  142.1 0.2 reshape.261
  142.3 47.2 %gather_fusion = bf16[5120,2048]{1,0:T(8,128)(2,1)} fusion(bf16[4352,2048]{1,0:T(8,128)(2,1)} %all-gather.2.cloned.1.call-done, s32[5120]{0:T(1024)S(1)} %broadcast_clamp_fusion), kind=kCustom, calls=%fused_computation | custom fusion | bytes 41963520 | tf_op jit(solution)/shard_map/jit(_take)/gather | solution.py:62
  189.5 27.3 %fusion.34 = f32[16,320,2,192]{1,3,2,0:T(8,128)} fusion(bf16[16,320,2048,1]{2,1,3,0:T(8,128)(2,1)} %bitcast.56, bf16[16,2,192,2048]{3,2,1,0:T(8,128)(2,1)} %param.12), kind=kOutput, calls=%fused_computation.81 | convolution fusion | flops 8053063680 | bytes 54001664 | tf_op jit(solution)/shard_map/jrd,jgfd->jrgf/dot_general | solution.py:65
  216.8 17.3 %convert_bitcast_fusion = bf16[320,16,2048]{2,0,1:T(8,128)(2,1)} fusion(bf16[16,192,2048]{2,1,0:T(8,128)(2,1)} %param.13, f32[16,320,2,192]{1,3,2,0:T(8,128)} %fusion.34), kind=kOutput, calls=%fused_computation.3 | convolution fusion | flops 4042915840 | bytes 41418752 | tf_op jit(solution)/shard_map/jrf,jfd->rjd/dot_general | solution.py:69
  234.1 22.7 %copy.27 = bf16[320,16,2048]{2,1,0:T(8,128)(2,1)} copy(bf16[320,16,2048]{2,0,1:T(8,128)(2,1)} %convert_bitcast_fusion) | data formatting | bytes 41943040 | tf_op jit(solution)/shard_map/convert_element_type | solution.py:72
  256.8 0.0 reduce-scatter.2.cloned.1.call-update
  256.8 0.0 copy-start
  256.8 0.0 copy-start.1
  256.8 151.4 %reduce-scatter.2.cloned.1.call-done = bf16[8,10,16,2048]{3,2,1,0:T(8,128)(2,1)} async-done(((bf16[32,10,16,2048]{3,2,1,0:T(8,128)(2,1)}), bf16[8,10,16,2048]{3,2,1,0:T(8,128)(2,1)}) %reduce-scatter.2.cloned.1.call-update) | async-done | bytes 5242896 | tf_op jit(solution)/shard_map/reduce_scatter | solution.py:73
  408.2 5.5 all-to-all-start
  413.8 0.1 reduce_sum.33
  413.9 0.0 copy-done
  414.0 0.1 copy.23
  414.1 0.0 copy-done.1
  414.1 0.1 copy.29
  414.3 116.1 %all-to-all-done = bf16[8,10,16,2048]{3,2,1,0:T(8,128)(2,1)} async-done(((bf16[8,10,16,2048]{3,2,1,0:T(8,128)(2,1)}), bf16[8,10,16,2048]{3,2,1,0:T(8,128)(2,1)}, u32[]{:S(2)}, u32[]{:S(2)}) %all-to-all-start) | async-done | bytes 5242912 | tf_op jit(solution)/shard_map/all_to_all | solution.py:75
  530.4 12.0 %gather_fusion.1 = bf16[1024,2048]{1,0:T(8,128)(2,1)} fusion(bf16[1280,2048]{1,0:T(8,128)(2,1)} %bitcast.15, s32[1024]{0:T(1024)S(1)} %broadcast_clamp_fusion.1), kind=kCustom, calls=%fused_computation.1 | custom fusion | bytes 8392704 | tf_op jit(solution)/shard_map/jit(_take)/gather | solution.py:78
  542.4 3.5 fusion.2
  545.9 1.1 copy.34
  (17 shorter events, 0.3 us)
Async XLA Ops:
  6.5 133.2 %all-gather.2.cloned.1.call-start = ((), (), s32[]{:S(2)}) async-start(), calls=%async_computation.2 | async-start | bytes 18382848 | tf_op jit(solution)/shard_map/all_gather | solution.py:54
  17.1 391.2 %reduce-scatter.2.cloned.1.call-start = ((), (), s32[]{:S(2)}) async-start(), calls=%async_computation.3 | async-start | bytes 26214400 | tf_op jit(solution)/shard_map/reduce_scatter | solution.py:73
  256.8 157.1 %copy-start = (s32[128,8]{0,1:T(8,128)S(1)}, s32[128,8]{0,1:T(8,128)}, u32[]{:S(2)}) copy-start(s32[128,8]{0,1:T(8,128)} %param.10) | copy-start | bytes 12292
  256.8 157.3 %copy-start.1 = (f32[128,8]{0,1:T(8,128)S(1)}, f32[128,8]{0,1:T(8,128)}, u32[]{:S(2)}) copy-start(f32[128,8]{0,1:T(8,128)} %param.11) | copy-start | bytes 12292
  408.2 122.1 %all-to-all-start = ((bf16[8,10,16,2048]{3,2,1,0:T(8,128)(2,1)}), bf16[8,10,16,2048]{3,2,1,0:T(8,128)(2,1)}, u32[]{:S(2)}, u32[]{:S(2)}) async-start(bf16[8,10,16,2048]{3,2,1,0:T(8,128)(2,1)} %reduce-scatter.2.cloned.1.call-done), calls=%async_computation.1 | async-start | bytes 10485760 | tf_op jit(solution)/shard_map/all_to_all | solution.py:75
Sparse Core Ops, SparseCore 0:
  17.2 122.5 all-gather.1
  256.9 151.2 reduce-scatter.1

commit v3 on v2

--- a/solution.py
+++ b/solution.py
@@ -1,9 +1,12 @@
+import math
+
 import jax
 import jax.numpy as jnp
 from jax import lax
 from jax.sharding import PartitionSpec as P
 
 CAP = 10
+PIECES = 2
 
 
 EPSILON = 1e-06
@@ -59,22 +62,35 @@
     ).astype(jnp.int32)
     rows = tables + (jnp.arange(devices, dtype=jnp.int32) * stride)[:, None]
     rows = rows.reshape(owners, tok_count, holding, CAP).transpose(2, 1, 0, 3).reshape(-1)
-    picked = jnp.take(every, rows, axis=0, mode="clip")
-    picked = picked.reshape(holding, tok_count * owners * CAP, features)
-
-    both = jnp.einsum(
-        "jrd,jgfd->jrgf", picked, gate_up_weight, preferred_element_type=jnp.float32
+    rows = rows.reshape(holding, -1)
+    pieces = math.gcd(holding, PIECES)
+    width = holding // pieces
+    returned = []
+    sums = []
+    for piece in range(pieces):
+        span = slice(piece * width, (piece + 1) * width)
+        picked = jnp.take(every, rows[span].reshape(-1), axis=0, mode="clip")
+        picked = picked.reshape(width, tok_count * owners * CAP, features)
+        both = jnp.einsum(
+            "jrd,jgfd->jrgf", picked, gate_up_weight[span], preferred_element_type=jnp.float32
+        )
+        hidden = (jax.nn.silu(both[:, :, 0, :]) * both[:, :, 1, :]).astype(jnp.bfloat16)
+        partial = jnp.einsum(
+            "jrf,jfd->jrd", hidden, down_weight[span], preferred_element_type=jnp.float32
+        )
+        partial = partial.astype(jnp.bfloat16).reshape(width, tok_count * owners, CAP, features)
+        partial = partial.transpose(1, 2, 0, 3).reshape(tok_count * owners, CAP * width, features)
+        if sums:
+            partial, _ = lax.optimization_barrier((partial, sums[-1]))
+        sums.append(lax.psum_scatter(partial, "tok", scatter_dimension=0, tiled=True))
+        returned.append(
+            lax.all_to_all(sums[-1], ("row", "col"), split_axis=0, concat_axis=0, tiled=True)
+        )
+    returned = jnp.concatenate(returned, axis=1)
+    expert = target // CAP
+    back = (
+        (expert // width) * (CAP * width) + (target % CAP) * width + expert % width
     )
-    hidden = (jax.nn.silu(both[:, :, 0, :]) * both[:, :, 1, :]).astype(jnp.bfloat16)
-    partial = jnp.einsum(
-        "jrf,jfd->rjd", hidden, down_weight, preferred_element_type=jnp.float32
-    )
-    partial = partial.astype(jnp.bfloat16).reshape(tok_count * owners, CAP, holding, features)
-    summed = lax.psum_scatter(partial, "tok", scatter_dimension=0, tiled=True)
-
-    returned = lax.all_to_all(summed, ("row", "col"), split_axis=0, concat_axis=0, tiled=True)
-    expert = target // CAP
-    back = (expert // holding) * (CAP * holding) + (target % CAP) * holding + expert % holding
     picked_back = jnp.take(returned.reshape(experts * CAP, features), back, axis=0)
     picked_back = picked_back.reshape(count, chosen, features)
     mixed = jnp.einsum("tk,tkd->td", gates, picked_back.astype(jnp.float32))

time: 555 us -> 484 us (0.87); the launches traced: 554 us -> 475 us
  waiting for transfers between devices: 390 us -> 209 us
  blocking collectives: 0 us -> 66 us
  local copies, waits for them, and re-layouts: 91.6 us -> 118 us
    reduce_scatter x1 -> x2, waiting for transfers between devices: 151 us -> 26.9 us  [local(): lax.psum_scatter(partial, 'tok', scatter_dimension=0, tiled=True)]
    all_to_all x0 -> x1, blocking collectives: none -> 66 us  [local(): lax.all_to_all(sums[-1], ('row', 'col'), split_axis=0, concat_axis=0, til...]
    all_to_all x1, waiting for transfers between devices: 116 us -> 59.9 us  [local(): lax.all_to_all(sums[-1], ('row', 'col'), split_axis=0, concat_axis=0, til...]
    gather x1 -> x2, local copies, waits for them, and re-layouts: 47.2 us -> 68.8 us  [local(): picked = jnp.take(every, rows[span].reshape(-1), axis=0, mode='clip')]
    convert_element_type x1 -> x2, local copies, waits for them, and re-layouts: 22.7 us -> 27.6 us  [local(): partial.astype(jnp.bfloat16)]
    dot_general x2 -> x4, matrix products: 44.6 us -> 49.1 us  [the longest x2 26.6 us: local(): jnp.einsum('jrd,jgfd->jrgf', picked, gate_up_weight[span], preferred_elem...]
  transfers between devices with their start and end apart: 3 -> 4, of which waited for: 3 -> 4; matrix products, arithmetic and copies ran while one was open for 0% -> 17% of each run, Pallas kernels for 0% -> 0%
where the time goes in v3:
time: 484 us; the launch traced here: 475 us
  waiting for transfers between devices  209 us (43%)
  local copies, waits for them, and re-layouts  118 us (24%)
  blocking collectives  66 us (14%)
  matrix products  52.6 us (11%)
  between operations  13.6 us (3%)
  other arithmetic  9.76 us (2%)
  starting transfers between devices  5.86 us (1%)
    all_gather x1, waiting for transfers between devices, local(): every = lax.all_gather(packed, ALL, axis=0, tiled=True)  123 us
    gather x2, local copies, waits for them, and re-layouts, local(): picked = jnp.take(every, rows[span].reshape(-1), axis=0, mode='clip')  68.8 us
    all_to_all x1, blocking collectives, local(): lax.all_to_all(sums[-1], ('row', 'col'), split_axis=0, concat_axis=0, til...  66 us
    all_to_all x1, waiting for transfers between devices, local(): lax.all_to_all(sums[-1], ('row', 'col'), split_axis=0, concat_axis=0, til...  59.9 us
    convert_element_type x2, local copies, waits for them, and re-layouts, local(): partial.astype(jnp.bfloat16)  27.6 us
    reduce_scatter x2, waiting for transfers between devices, local(): lax.psum_scatter(partial, 'tok', scatter_dimension=0, tiled=True)  26.9 us
    dot_general x2, matrix products, local(): jnp.einsum('jrd,jgfd->jrgf', picked, gate_up_weight[span], preferred_elem...  26.6 us
    dot_general x2, matrix products, local(): jnp.einsum('jrf,jfd->jrd', hidden, down_weight[span], preferred_element_t...  22.5 us
  transfers between devices with their start and end apart: 4, of which 4 were waited for; matrix products, arithmetic and copies ran while one was open for 17% of the time, Pallas kernels for 0%

profile of v3, /device:TPU:0, one launch (start us, length us, event | category | flops | bytes accessed | tf_op | source)
XLA Modules:
  0.0 475.4 jit_solution(18255009470042115266)
XLA Ops:
  6.5 0.7 broadcast_multiply_fusion
  7.2 0.8 copy.23
  8.0 0.1 eq.29
  8.1 0.1 reshape.268
  8.2 1.2 fusion.25
  9.4 0.1 copy.29
  9.5 0.1 mul.124
  9.6 0.1 copy.25
  9.7 0.2 fusion.30
  10.0 0.1 copy.26
  10.2 0.4 fusion.29
  10.5 0.1 compare_select_fusion
  10.6 4.3 scatter_custom_fusion
  15.0 1.2 fusion.27
  16.2 0.9 pad_maximum_fusion.1
  17.1 0.0 all-gather.2.cloned.1.call-update
  17.1 0.0 reduce-scatter.3.cloned.1.call-start
  17.2 122.6 %all-gather.2.cloned.1.call-done = bf16[4352,2048]{1,0:T(8,128)(2,1)} async-done(((bf16[136,2048]{1,0:T(8,128)(2,1)}), bf16[4352,2048]{1,0:T(8,128)(2,1)}) %all-gather.2.cloned.1.call-update) | async-done | bytes 17825808 | tf_op jit(solution)/shard_map/all_gather | solution.py:57
  139.8 1.3 slice.77
  141.1 0.6 copy.43
  141.7 0.1 convert_add_fusion
  141.8 0.2 reshape.273
  142.0 0.1 copy.30
  142.1 0.1 reshape.283
  142.3 28.5 %gather_fusion = bf16[2560,2048]{1,0:T(8,128)(2,1)} fusion(bf16[4352,2048]{1,0:T(8,128)(2,1)} %all-gather.2.cloned.1.call-done, s32[3072]{0:T(1024)S(1)} %pad_clamp_fusion.1), kind=kCustom, calls=%fused_computation | custom fusion | bytes 20981760 | tf_op jit(solution)/shard_map/jit(_take)/gather | solution.py:72
  170.8 13.6 %fusion.2 = f32[8,320,2,192]{1,3,2,0:T(8,128)} fusion(bf16[8,320,2048,1]{2,1,3,0:T(8,128)(2,1)} %bitcast.83, bf16[16,2,192,2048]{3,2,1,0:T(8,128)(2,1)} %param.12), kind=kOutput, calls=%fused_computation.6 | convolution fusion | flops 4026531840 | bytes 27000832 | tf_op jit(solution)/shard_map/jrd,jgfd->jrgf/dot_general | solution.py:74
  184.4 11.2 %fusion.8 = bf16[8,320,2048]{2,1,0:T(8,128)(2,1)} fusion(bf16[16,192,2048]{2,1,0:T(8,128)(2,1)} %param.13, f32[8,320,2,192]{1,3,2,0:T(8,128)} %fusion.2), kind=kOutput, calls=%fused_computation.12 | convolution fusion | flops 2021457920 | bytes 21495808 | tf_op jit(solution)/shard_map/jrf,jfd->jrd/dot_general | solution.py:78
  195.6 13.8 %copy.32 = bf16[8,320,2048]{2,0,1:T(8,128)(2,1)} copy(bf16[8,320,2048]{2,1,0:T(8,128)(2,1)} %fusion.8) | data formatting | bytes 20971520 | tf_op jit(solution)/shard_map/convert_element_type | solution.py:81
  209.4 0.0 reduce-scatter.3.cloned.1.call-update
  209.4 0.0 reduce-scatter.5.cloned.1.call-start
  209.5 0.1 copy.33
  209.6 0.1 reshape.291
  209.7 40.2 %gather_fusion.1 = bf16[2560,2048]{1,0:T(8,128)(2,1)} fusion(bf16[4352,2048]{1,0:T(8,128)(2,1)} %all-gather.2.cloned.1.call-done, s32[3072]{0:T(1024)S(1)} %pad_clamp_fusion), kind=kCustom, calls=%fused_computation.1 | custom fusion | bytes 20981760 | tf_op jit(solution)/shard_map/jit(_take)/gather | solution.py:72
  250.0 12.9 %fusion = f32[8,320,2,192]{1,3,0,2:T(8,128)} fusion(bf16[8,320,2048,1]{2,1,0,3:T(8,128)(2,1)} %bitcast.82, bf16[16,2,192,2048]{3,2,1,0:T(8,128)(2,1)} %param.12), kind=kOutput, calls=%fused_computation.4 | convolution fusion | flops 4026531840 | bytes 27000832 | tf_op jit(solution)/shard_map/jrd,jgfd->jrgf/dot_general | solution.py:74
  262.9 11.4 %fusion.11 = bf16[8,320,2048]{2,1,0:T(8,128)(2,1)} fusion(bf16[16,192,2048]{2,1,0:T(8,128)(2,1)} %param.13, f32[8,320,2,192]{1,3,0,2:T(8,128)} %fusion), kind=kOutput, calls=%fused_computation.13 | convolution fusion | flops 2021457920 | bytes 21495808 | tf_op jit(solution)/shard_map/jrf,jfd->jrd/dot_general | solution.py:78
  274.3 13.8 %copy.36 = bf16[8,320,2048]{2,0,1:T(8,128)(2,1)} copy(bf16[8,320,2048]{2,1,0:T(8,128)(2,1)} %fusion.11) | data formatting | bytes 20971520 | tf_op jit(solution)/shard_map/convert_element_type | solution.py:81
  288.1 5.0 %reduce-scatter.3.cloned.1.call-done = bf16[8,80,2048]{2,1,0:T(8,128)(2,1)} async-done(((bf16[32,80,2048]{2,1,0:T(8,128)(2,1)}), bf16[8,80,2048]{2,1,0:T(8,128)(2,1)}) %reduce-scatter.3.cloned.1.call-update) | async-done | bytes 2621456 | tf_op jit(solution)/shard_map/reduce_scatter | solution.py:85
  293.1 66.0 %all_to_all.10 = bf16[8,80,2048]{2,1,0:T(8,128)(2,1)S(1)} all-to-all(bf16[8,80,2048]{2,1,0:T(8,128)(2,1)} %reduce-scatter.3.cloned.1.call-done), channel_id=1, replica_groups=mesh['row'=2,'col'=4,'tok'=4] {'row','col'}, dimensions={0} | all-to-all | bytes 5242880 | tf_op jit(solution)/shard_map/all_to_all | solution.py:87
  359.1 21.9 %reduce-scatter.5.cloned.1.call-done = bf16[8,80,2048]{2,1,0:T(8,128)(2,1)} async-done(((bf16[32,80,2048]{2,1,0:T(8,128)(2,1)}), bf16[8,80,2048]{2,1,0:T(8,128)(2,1)}) %reduce-scatter.5.cloned.1.call-update) | async-done | bytes 2621456 | tf_op jit(solution)/shard_map/reduce_scatter | solution.py:85
  381.0 5.8 %all-to-all-start.1 = ((bf16[8,80,2048]{2,1,0:T(8,128)(2,1)}), bf16[8,80,2048]{2,1,0:T(8,128)(2,1)}, u32[]{:S(2)}, u32[]{:S(2)}) async-start(bf16[8,80,2048]{2,1,0:T(8,128)(2,1)} %reduce-scatter.5.cloned.1.call-done), calls=%async_computation.3 | async-start | bytes 5242880 | tf_op jit(solution)/shard_map/all_to_all | solution.py:87
  386.8 0.1 reduce_sum.33
  386.9 0.1 copy.40
  387.2 0.1 copy.28
  387.3 59.9 %all-to-all-done.1 = bf16[8,80,2048]{2,1,0:T(8,128)(2,1)} async-done(((bf16[8,80,2048]{2,1,0:T(8,128)(2,1)}), bf16[8,80,2048]{2,1,0:T(8,128)(2,1)}, u32[]{:S(2)}, u32[]{:S(2)}) %all-to-all-start.1) | async-done | bytes 2621472 | tf_op jit(solution)/shard_map/all_to_all | solution.py:87
  447.2 4.8 %pad_maximum_fusion = bf16[8,160,2048]{2,1,0:T(8,128)(2,1)} fusion(bf16[8,80,2048]{2,1,0:T(8,128)(2,1)} %all-to-all-done.1, bf16[8,80,2048]{2,1,0:T(8,128)(2,1)S(1)} %all_to_all.10), kind=kLoop, calls=%fused_computation.14 | loop fusion | flops 10485760 | bytes 10485760 | tf_op jit(solution)/shard_map/concatenate | solution.py:89
  452.0 12.0 %gather_fusion.2 = bf16[1024,2048]{1,0:T(8,128)(2,1)} fusion(bf16[1280,2048]{1,0:T(8,128)(2,1)} %bitcast.79, s32[1024]{0:T(1024)S(1)} %broadcast_clamp_fusion), kind=kCustom, calls=%fused_computation.2 | custom fusion | bytes 8392704 | tf_op jit(solution)/shard_map/jit(_take)/gather | solution.py:94
  464.0 3.5 fusion.14
  467.6 1.1 copy.47
  (25 shorter events, 0.3 us)
Async XLA Ops:
  6.5 133.3 %all-gather.2.cloned.1.call-start = ((), (), s32[]{:S(2)}) async-start(), calls=%async_computation.4 | async-start | bytes 18382848 | tf_op jit(solution)/shard_map/all_gather | solution.py:57
  17.1 275.9 %reduce-scatter.3.cloned.1.call-start = ((), (), s32[]{:S(2)}) async-start(), calls=%async_computation.5 | async-start | bytes 13107200 | tf_op jit(solution)/shard_map/reduce_scatter | solution.py:85
  209.4 171.6 %reduce-scatter.5.cloned.1.call-start = ((), (), s32[]{:S(2)}) async-start(), calls=%async_computation.6 | async-start | bytes 13107200 | tf_op jit(solution)/shard_map/reduce_scatter | solution.py:85
  293.1 93.8 %copy-start.1 = (f32[128,8]{0,1:T(8,128)S(1)}, f32[128,8]{0,1:T(8,128)}, u32[]{:S(2)}) copy-start(f32[128,8]{0,1:T(8,128)} %param.11) | copy-start | bytes 12292
  293.1 94.0 %copy-start = (s32[128,8]{0,1:T(8,128)S(1)}, s32[128,8]{0,1:T(8,128)}, u32[]{:S(2)}) copy-start(s32[128,8]{0,1:T(8,128)} %param.10) | copy-start | bytes 12292
  381.0 66.1 %all-to-all-start.1 = ((bf16[8,80,2048]{2,1,0:T(8,128)(2,1)}), bf16[8,80,2048]{2,1,0:T(8,128)(2,1)}, u32[]{:S(2)}, u32[]{:S(2)}) async-start(bf16[8,80,2048]{2,1,0:T(8,128)(2,1)} %reduce-scatter.5.cloned.1.call-done), calls=%async_computation.3 | async-start | bytes 5242880 | tf_op jit(solution)/shard_map/all_to_all | solution.py:87
Sparse Core Ops, SparseCore 0:
  17.2 122.5 all-gather.1
  209.6 83.4 reduce-scatter.2
  295.7 85.2 reduce-scatter.4

commit v4 on v3

--- a/solution.py
+++ b/solution.py
@@ -53,10 +53,11 @@
     stride = count + extra
     table_rows = jnp.zeros((extra * features,), jnp.bfloat16)
     table_rows = table_rows.at[: experts * CAP].set(source.astype(jnp.bfloat16))
+    lanes = features // 128
     packed = jnp.concatenate([normed, table_rows.reshape(extra, features)], axis=0)
-    every = lax.all_gather(packed, ALL, axis=0, tiled=True)
+    every = lax.all_gather(packed.reshape(stride, lanes, 128), ALL, axis=0, tiled=True)
 
-    tables = every.reshape(devices, stride, features)[:, count:, :].reshape(devices, -1)
+    tables = every.reshape(devices, stride, lanes, 128)[:, count:].reshape(devices, -1)
     tables = lax.dynamic_slice_in_dim(
         tables[:, : experts * CAP], owner * holding * CAP, holding * CAP, axis=1
     ).astype(jnp.int32)

time: 484 us -> 491 us (1.014); the launches traced: 475 us -> 488 us
  matrix products: 52.6 us -> 62.2 us
  waiting for transfers between devices: 209 us -> 217 us
  local copies, waits for them, and re-layouts: 118 us -> 113 us
    gather x2, local copies, waits for them, and re-layouts: 68.8 us -> 30.7 us  [local(): picked = jnp.take(every, rows[span].reshape(-1), axis=0, mode='clip')]
    reshape x1 -> x2, local copies, waits for them, and re-layouts: 0.02 us -> 32.8 us  [local(): picked = picked.reshape(width, tok_count * owners * CAP, features)]
    dot_general x2, matrix products: 26.6 us -> 36 us  [local(): jnp.einsum('jrd,jgfd->jrgf', picked, gate_up_weight[span], preferred_elem...]
    reduce_scatter x2, waiting for transfers between devices: 26.9 us -> 34.2 us  [local(): lax.psum_scatter(partial, 'tok', scatter_dimension=0, tiled=True)]
  transfers between devices with their start and end apart: 4 -> 4, of which waited for: 4 -> 4; matrix products, arithmetic and copies ran while one was open for 17% -> 15% of each run, Pallas kernels for 0% -> 0%
where the time goes in v4:
time: 491 us; the launch traced here: 488 us
  waiting for transfers between devices  217 us (44%)
  local copies, waits for them, and re-layouts  113 us (23%)
  blocking collectives  66 us (13%)
  matrix products  62.2 us (13%)
  between operations  13.8 us (3%)
  other arithmetic  9.77 us (2%)
  starting transfers between devices  5.9 us (1%)
    all_gather x1, waiting for transfers between devices, local(): lax.all_gather(packed.reshape(stride, lanes, 128), ALL, axis=0, tiled=True)  123 us
    all_to_all x1, blocking collectives, local(): lax.all_to_all(sums[-1], ('row', 'col'), split_axis=0, concat_axis=0, til...  66 us
    all_to_all x1, waiting for transfers between devices, local(): lax.all_to_all(sums[-1], ('row', 'col'), split_axis=0, concat_axis=0, til...  59.9 us
    dot_general x2, matrix products, local(): jnp.einsum('jrd,jgfd->jrgf', picked, gate_up_weight[span], preferred_elem...  36 us
    reduce_scatter x2, waiting for transfers between devices, local(): lax.psum_scatter(partial, 'tok', scatter_dimension=0, tiled=True)  34.2 us
    reshape x2, local copies, waits for them, and re-layouts, local(): picked = picked.reshape(width, tok_count * owners * CAP, features)  32.8 us
    gather x2, local copies, waits for them, and re-layouts, local(): picked = jnp.take(every, rows[span].reshape(-1), axis=0, mode='clip')  30.7 us
    convert_element_type x2, local copies, waits for them, and re-layouts, local(): partial.astype(jnp.bfloat16)  27.6 us
  transfers between devices with their start and end apart: 4, of which 4 were waited for; matrix products, arithmetic and copies ran while one was open for 15% of the time, Pallas kernels for 0%

profile of v4, /device:TPU:0, one launch (start us, length us, event | category | flops | bytes accessed | tf_op | source)
XLA Modules:
  0.0 487.5 jit_solution(10421784051581495837)
XLA Ops:
  6.5 0.7 broadcast_multiply_fusion
  7.2 0.8 copy.35
  8.0 0.1 eq.29
  8.1 0.1 reshape.270
  8.2 1.2 fusion.26
  9.4 0.1 copy.41
  9.5 0.1 mul.124
  9.6 0.1 copy.37
  9.7 0.2 fusion.32
  10.0 0.1 copy.38
  10.2 0.4 fusion.31
  10.5 0.1 compare_select_fusion
  10.6 4.3 scatter_custom_fusion
  14.9 1.3 fusion.29
  16.2 0.1 copy.55
  16.3 0.9 pad_maximum_fusion.1
  17.3 122.6 %all-gather.2.cloned.1.call-done = bf16[4352,16,128]{2,1,0:T(8,128)(2,1)} async-done(((bf16[136,16,128]{2,1,0:T(8,128)(2,1)}), bf16[4352,16,128]{2,1,0:T(8,128)(2,1)}) %all-gather.2.cloned.1.call-update) | async-done | bytes 17825808 | tf_op jit(solution)/shard_map/all_gather | solution.py:58
  139.9 1.4 slice.77
  141.3 0.7 copy.61
  142.0 0.1 convert_add_fusion
  142.1 0.2 reshape.274
  142.3 0.1 copy.42
  142.4 0.1 reshape.284
  142.6 14.4 %gather_fusion = bf16[2560,16,128]{2,1,0:T(8,128)(2,1)} fusion(bf16[4352,16,128]{2,1,0:T(8,128)(2,1)} %all-gather.2.cloned.1.call-done, s32[3072]{0:T(1024)S(1)} %pad_clamp_fusion.1), kind=kCustom, calls=%fused_computation | custom fusion | bytes 20981760 | tf_op jit(solution)/shard_map/jit(_take)/gather | solution.py:73
  157.0 16.3 %reshape.316 = bf16[8,320,2048,1]{2,1,0,3:T(8,128)(2,1)} reshape(bf16[2560,16,128]{2,1,0:T(8,128)(2,1)} %gather_fusion) | data formatting | bytes 20971520 | tf_op jit(solution)/shard_map/reshape | solution.py:74
  173.3 23.0 %fusion.2 = f32[8,320,2,192]{1,3,2,0:T(8,128)} fusion(bf16[16,2,192,2048]{3,2,1,0:T(8,128)(2,1)} %param.12, bf16[8,320,2048,1]{2,1,0,3:T(8,128)(2,1)} %reshape.316), kind=kOutput, calls=%fused_computation.6 | convolution fusion | flops 4026531840 | bytes 27000832 | tf_op jit(solution)/shard_map/jrd,jgfd->jrgf/dot_general | solution.py:75
  196.3 11.2 %fusion.9 = bf16[8,320,2048]{2,1,0:T(8,128)(2,1)} fusion(bf16[16,192,2048]{2,1,0:T(8,128)(2,1)} %param.13, f32[8,320,2,192]{1,3,2,0:T(8,128)} %fusion.2), kind=kOutput, calls=%fused_computation.13 | convolution fusion | flops 2021457920 | bytes 21495808 | tf_op jit(solution)/shard_map/jrf,jfd->jrd/dot_general | solution.py:79
  207.5 13.8 %copy.44 = bf16[8,320,2048]{2,0,1:T(8,128)(2,1)} copy(bf16[8,320,2048]{2,1,0:T(8,128)(2,1)} %fusion.9) | data formatting | bytes 20971520 | tf_op jit(solution)/shard_map/convert_element_type | solution.py:82
  221.3 0.0 reduce-scatter.5.cloned.1.call-start
  221.4 0.1 copy.45
  221.5 0.1 reshape.292
  221.6 16.3 %gather_fusion.1 = bf16[2560,16,128]{2,1,0:T(8,128)(2,1)} fusion(bf16[4352,16,128]{2,1,0:T(8,128)(2,1)} %all-gather.2.cloned.1.call-done, s32[3072]{0:T(1024)S(1)} %pad_clamp_fusion), kind=kCustom, calls=%fused_computation.1 | custom fusion | bytes 20981760 | tf_op jit(solution)/shard_map/jit(_take)/gather | solution.py:73
  237.9 16.5 %reshape.317 = bf16[8,320,2048,1]{2,1,0,3:T(8,128)(2,1)} reshape(bf16[2560,16,128]{2,1,0:T(8,128)(2,1)} %gather_fusion.1) | data formatting | bytes 20971520 | tf_op jit(solution)/shard_map/reshape | solution.py:74
  254.4 13.0 %fusion = f32[8,320,2,192]{1,3,0,2:T(8,128)} fusion(bf16[8,320,2048,1]{2,1,0,3:T(8,128)(2,1)} %reshape.317, bf16[16,2,192,2048]{3,2,1,0:T(8,128)(2,1)} %param.12), kind=kOutput, calls=%fused_computation.4 | convolution fusion | flops 4026531840 | bytes 27000832 | tf_op jit(solution)/shard_map/jrd,jgfd->jrgf/dot_general | solution.py:75
  267.4 11.5 %fusion.12 = bf16[8,320,2048]{2,1,0:T(8,128)(2,1)} fusion(bf16[16,192,2048]{2,1,0:T(8,128)(2,1)} %param.13, f32[8,320,2,192]{1,3,0,2:T(8,128)} %fusion), kind=kOutput, calls=%fused_computation.14 | convolution fusion | flops 2021457920 | bytes 21495808 | tf_op jit(solution)/shard_map/jrf,jfd->jrd/dot_general | solution.py:79
  278.9 13.8 %copy.48 = bf16[8,320,2048]{2,0,1:T(8,128)(2,1)} copy(bf16[8,320,2048]{2,1,0:T(8,128)(2,1)} %fusion.12) | data formatting | bytes 20971520 | tf_op jit(solution)/shard_map/convert_element_type | solution.py:82
  292.7 12.3 %reduce-scatter.3.cloned.1.call-done = bf16[8,80,2048]{2,1,0:T(8,128)(2,1)} async-done(((bf16[32,80,2048]{2,1,0:T(8,128)(2,1)}), bf16[8,80,2048]{2,1,0:T(8,128)(2,1)}) %reduce-scatter.3.cloned.1.call-update) | async-done | bytes 2621456 | tf_op jit(solution)/shard_map/reduce_scatter | solution.py:86
  305.0 66.0 %all_to_all.10 = bf16[8,80,2048]{2,1,0:T(8,128)(2,1)S(1)} all-to-all(bf16[8,80,2048]{2,1,0:T(8,128)(2,1)} %reduce-scatter.3.cloned.1.call-done), channel_id=1, replica_groups=mesh['row'=2,'col'=4,'tok'=4] {'row','col'}, dimensions={0} | all-to-all | bytes 5242880 | tf_op jit(solution)/shard_map/all_to_all | solution.py:88
  371.0 21.9 %reduce-scatter.5.cloned.1.call-done = bf16[8,80,2048]{2,1,0:T(8,128)(2,1)} async-done(((bf16[32,80,2048]{2,1,0:T(8,128)(2,1)}), bf16[8,80,2048]{2,1,0:T(8,128)(2,1)}) %reduce-scatter.5.cloned.1.call-update) | async-done | bytes 2621456 | tf_op jit(solution)/shard_map/reduce_scatter | solution.py:86
  392.9 5.8 %all-to-all-start.1 = ((bf16[8,80,2048]{2,1,0:T(8,128)(2,1)}), bf16[8,80,2048]{2,1,0:T(8,128)(2,1)}, u32[]{:S(2)}, u32[]{:S(2)}) async-start(bf16[8,80,2048]{2,1,0:T(8,128)(2,1)} %reduce-scatter.5.cloned.1.call-done), calls=%async_computation.3 | async-start | bytes 5242880 | tf_op jit(solution)/shard_map/all_to_all | solution.py:88
  398.7 0.1 reduce_sum.33
  398.8 0.1 copy.52
  399.1 0.1 copy.40
  399.2 59.9 %all-to-all-done.1 = bf16[8,80,2048]{2,1,0:T(8,128)(2,1)} async-done(((bf16[8,80,2048]{2,1,0:T(8,128)(2,1)}), bf16[8,80,2048]{2,1,0:T(8,128)(2,1)}, u32[]{:S(2)}, u32[]{:S(2)}) %all-to-all-start.1) | async-done | bytes 2621472 | tf_op jit(solution)/shard_map/all_to_all | solution.py:88
  459.1 4.8 pad_maximum_fusion
  463.9 12.0 %gather_fusion.2 = bf16[1024,2048]{1,0:T(8,128)(2,1)} fusion(bf16[1280,2048]{1,0:T(8,128)(2,1)} %bitcast.79, s32[1024]{0:T(1024)S(1)} %broadcast_clamp_fusion), kind=kCustom, calls=%fused_computation.2 | custom fusion | bytes 8392704 | tf_op jit(solution)/shard_map/jit(_take)/gather | solution.py:95
  476.0 3.5 fusion.15
  479.5 1.1 copy.62
  (27 shorter events, 0.4 us)
Async XLA Ops:
  6.5 133.4 %all-gather.2.cloned.1.call-start = ((), (), s32[]{:S(2)}) async-start(), calls=%async_computation.4 | async-start | bytes 18382848 | tf_op jit(solution)/shard_map/all_gather | solution.py:58
  17.2 287.7 %reduce-scatter.3.cloned.1.call-start = ((), (), s32[]{:S(2)}) async-start(), calls=%async_computation.5 | async-start | bytes 13107200 | tf_op jit(solution)/shard_map/reduce_scatter | solution.py:86
  221.3 171.6 %reduce-scatter.5.cloned.1.call-start = ((), (), s32[]{:S(2)}) async-start(), calls=%async_computation.6 | async-start | bytes 13107200 | tf_op jit(solution)/shard_map/reduce_scatter | solution.py:86
  305.0 93.8 %copy-start.1 = (f32[128,8]{0,1:T(8,128)S(1)}, f32[128,8]{0,1:T(8,128)}, u32[]{:S(2)}) copy-start(f32[128,8]{0,1:T(8,128)} %param.11) | copy-start | bytes 12292
  305.0 94.0 %copy-start = (s32[128,8]{0,1:T(8,128)S(1)}, s32[128,8]{0,1:T(8,128)}, u32[]{:S(2)}) copy-start(s32[128,8]{0,1:T(8,128)} %param.10) | copy-start | bytes 12292
  392.9 66.2 %all-to-all-start.1 = ((bf16[8,80,2048]{2,1,0:T(8,128)(2,1)}), bf16[8,80,2048]{2,1,0:T(8,128)(2,1)}, u32[]{:S(2)}, u32[]{:S(2)}) async-start(bf16[8,80,2048]{2,1,0:T(8,128)(2,1)} %reduce-scatter.5.cloned.1.call-done), calls=%async_computation.3 | async-start | bytes 5242880 | tf_op jit(solution)/shard_map/all_to_all | solution.py:88
Sparse Core Ops, SparseCore 0:
  17.3 122.5 all-gather.1
  221.5 83.4 reduce-scatter.2
  307.6 85.2 reduce-scatter.4

commit v5 on v3

--- a/solution.py
+++ b/solution.py
@@ -26,6 +26,31 @@
     values = activations.astype(jnp.float32)
     scale = lax.rsqrt(jnp.mean(values * values, axis=-1, keepdims=True) + EPSILON)
     return (values * scale * norm_gain).astype(jnp.bfloat16)
+
+
+def reduce_over_tok(partial, tok_count):
+    if tok_count % 2:
+        return lax.psum_scatter(partial, "tok", scatter_dimension=0, tiled=True)
+    halves = tok_count // 2
+    t = lax.axis_index("tok")
+    core = t % 2
+    upper = t // 2
+    blocks = partial.reshape(halves, 2, -1, *partial.shape[2:])
+    kept = lax.dynamic_index_in_dim(blocks, core, axis=1, keepdims=False)
+    sent = lax.dynamic_index_in_dim(blocks, 1 - core, axis=1, keepdims=False)
+    swap_core = [(i, i ^ 1) for i in range(tok_count)]
+    got = lax.ppermute(sent, "tok", swap_core)
+    pairs = kept.astype(jnp.float32) + got.astype(jnp.float32)
+    if halves == 1:
+        return pairs[0]
+    if halves != 2:
+        pairs = pairs.astype(jnp.bfloat16)
+        return lax.psum_scatter(pairs, "tok", scatter_dimension=0, tiled=True)
+    kept = lax.dynamic_index_in_dim(pairs, upper, axis=0, keepdims=False)
+    sent = lax.dynamic_index_in_dim(pairs, 1 - upper, axis=0, keepdims=False)
+    swap_upper = [(i, i ^ 2) for i in range(tok_count)]
+    got = lax.ppermute(sent.astype(jnp.bfloat16), "tok", swap_upper)
+    return (kept + got.astype(jnp.float32)).astype(jnp.bfloat16)
 
 
 def local(activations, norm_gain, routes, route_weights, gate_up_weight, down_weight):
@@ -80,9 +105,7 @@
         )
         partial = partial.astype(jnp.bfloat16).reshape(width, tok_count * owners, CAP, features)
         partial = partial.transpose(1, 2, 0, 3).reshape(tok_count * owners, CAP * width, features)
-        if sums:
-            partial, _ = lax.optimization_barrier((partial, sums[-1]))
-        sums.append(lax.psum_scatter(partial, "tok", scatter_dimension=0, tiled=True))
+        sums.append(reduce_over_tok(partial, tok_count).reshape(owners, CAP * width, features))
         returned.append(
             lax.all_to_all(sums[-1], ("row", "col"), split_axis=0, concat_axis=0, tiled=True)
         )

time: 484 us -> 548 us (1.13)
  waiting for transfers between devices: 209 us -> 295 us
  blocking collectives: 66 us -> 0 us
  other arithmetic: 9.76 us -> 31.1 us
  local copies, waits for them, and re-layouts: 118 us -> 135 us
  starting transfers between devices: 5.86 us -> 13 us
    ppermute x0 -> x4, waiting for transfers between devices: none -> 114 us  [the longest x2 114 us: reduce_over_tok(): got = lax.ppermute(sent.astype(jnp.bfloat16), 'tok', swap_upper)]
    all_to_all x1 -> x0, blocking collectives: 66 us -> none  [local(): lax.all_to_all(sums[-1], ('row', 'col'), split_axis=0, concat_axis=0, til...]
    reduce_scatter x2 -> x0, waiting for transfers between devices: 26.9 us -> none  [local(): lax.psum_scatter(partial, 'tok', scatter_dimension=0, tiled=True)]
    add x0 -> x2, other arithmetic: none -> 13.1 us  [reduce_over_tok(): pairs = kept.astype(jnp.float32) + got.astype(jnp.float32)]
    squeeze x0 -> x2, local copies, waits for them, and re-layouts: none -> 11.5 us  [reduce_over_tok(): sent = lax.dynamic_index_in_dim(blocks, 1 - core, axis=1, keepdims=False)]
    convert_element_type x0 -> x2, other arithmetic: none -> 8.27 us  [reduce_over_tok(): return (kept + got.astype(jnp.float32)).astype(jnp.bfloat16)]
    all_to_all x1 -> x2, waiting for transfers between devices: 59.9 us -> 58.2 us  [local(): lax.all_to_all(sums[-1], ('row', 'col'), split_axis=0, concat_axis=0, til...]
  transfers between devices with their start and end apart: 4 -> 7, of which waited for: 4 -> 4; matrix products, arithmetic and copies ran while one was open for 17% -> 20% of each run, Pallas kernels for 0% -> 0%
where the time goes in v5:
time: 548 us; the launch traced here: 540 us
  waiting for transfers between devices  295 us (54%)
  local copies, waits for them, and re-layouts  135 us (25%)
  matrix products  52 us (9%)
  other arithmetic  31.1 us (6%)
  between operations  14.1 us (3%)
  starting transfers between devices  13 us (2%)
    all_gather x1, waiting for transfers between devices, local(): every = lax.all_gather(packed, ALL, axis=0, tiled=True)  123 us
    ppermute x2, waiting for transfers between devices, reduce_over_tok(): got = lax.ppermute(sent.astype(jnp.bfloat16), 'tok', swap_upper)  114 us
    gather x2, local copies, waits for them, and re-layouts, local(): picked = jnp.take(every, rows[span].reshape(-1), axis=0, mode='clip')  68.9 us
    all_to_all x2, waiting for transfers between devices, local(): lax.all_to_all(sums[-1], ('row', 'col'), split_axis=0, concat_axis=0, til...  58.2 us
    convert_element_type x2, local copies, waits for them, and re-layouts, local(): partial.astype(jnp.bfloat16)  27.6 us
    dot_general x2, matrix products, local(): jnp.einsum('jrd,jgfd->jrgf', picked, gate_up_weight[span], preferred_elem...  26.2 us
    dot_general x2, matrix products, local(): jnp.einsum('jrf,jfd->jrd', hidden, down_weight[span], preferred_element_t...  22.3 us
    add x2, other arithmetic, reduce_over_tok(): pairs = kept.astype(jnp.float32) + got.astype(jnp.float32)  13.1 us
  transfers between devices with their start and end apart: 7, of which 4 were waited for; matrix products, arithmetic and copies ran while one was open for 20% of the time, Pallas kernels for 0%

profile of v5, /device:TPU:0, one launch (start us, length us, event | category | flops | bytes accessed | tf_op | source)
XLA Modules:
  0.0 539.9 jit_solution(12946763559005142108)
XLA Ops:
  6.5 0.7 broadcast_multiply_fusion
  7.2 0.8 copy.23
  8.2 1.2 fusion.29
  9.5 0.1 mul.124
  9.7 0.2 fusion.34
  10.0 0.1 copy.26
  10.2 0.4 fusion.33
  10.6 4.3 scatter_custom_fusion
  15.0 1.2 fusion.31
  16.2 0.9 pad_maximum_fusion.1
  17.2 122.7 %all-gather.2.cloned.1.call-done = bf16[4352,2048]{1,0:T(8,128)(2,1)} async-done(((bf16[136,2048]{1,0:T(8,128)(2,1)}), bf16[4352,2048]{1,0:T(8,128)(2,1)}) %all-gather.2.cloned.1.call-update) | async-done | bytes 17825808 | tf_op jit(solution)/shard_map/all_gather | solution.py:82
  139.8 1.3 slice.77
  141.1 0.6 copy.43
  141.8 0.2 reshape.279
  142.1 0.1 reshape.299
  142.3 28.5 %gather_fusion.1 = bf16[2560,2048]{1,0:T(8,128)(2,1)} fusion(bf16[4352,2048]{1,0:T(8,128)(2,1)} %all-gather.2.cloned.1.call-done, s32[3072]{0:T(1024)S(1)} %pad_clamp_fusion), kind=kCustom, calls=%fused_computation.1 | custom fusion | bytes 20981760 | tf_op jit(solution)/shard_map/jit(_take)/gather | solution.py:97
  170.8 12.8 %fusion = f32[8,320,2,192]{1,3,0,2:T(8,128)} fusion(bf16[8,320,2048,1]{2,1,0,3:T(8,128)(2,1)} %bitcast.109, bf16[16,2,192,2048]{3,2,1,0:T(8,128)(2,1)} %param.12), kind=kOutput, calls=%fused_computation.4 | convolution fusion | flops 4026531840 | bytes 27000832 | tf_op jit(solution)/shard_map/jrd,jgfd->jrgf/dot_general | solution.py:99
  183.6 11.2 %fusion.11 = bf16[8,320,2048]{2,1,0:T(8,128)(2,1)} fusion(bf16[16,192,2048]{2,1,0:T(8,128)(2,1)} %param.13, f32[8,320,2,192]{1,3,0,2:T(8,128)} %fusion), kind=kOutput, calls=%fused_computation.15 | convolution fusion | flops 2021457920 | bytes 21495808 | tf_op jit(solution)/shard_map/jrf,jfd->jrd/dot_general | solution.py:103
  194.8 13.8 %copy.36 = bf16[8,320,2048]{2,0,1:T(8,128)(2,1)} copy(bf16[8,320,2048]{2,1,0:T(8,128)(2,1)} %fusion.11) | data formatting | bytes 20971520 | tf_op jit(solution)/shard_map/convert_element_type | solution.py:106
  208.6 5.8 %dynamic-slice_bitcast_fusion = bf16[2,640,2048]{2,1,0:T(8,128)(2,1)} fusion(bf16[2,2,640,2048]{3,2,1,0:T(8,128)(2,1)} %bitcast.106, s32[]{:T(128)S(6)} %select_n.145), kind=kLoop, calls=%fused_computation.22 | loop fusion | bytes 10485764 | tf_op jit(solution)/shard_map/jit(dynamic_index_in_dim)/squeeze | solution.py:40
  214.4 0.2 collective-permute-start.2
  214.6 0.1 reshape.291
  214.8 40.4 %gather_fusion = bf16[2560,2048]{1,0:T(8,128)(2,1)} fusion(bf16[4352,2048]{1,0:T(8,128)(2,1)} %all-gather.2.cloned.1.call-done, s32[3072]{0:T(1024)S(1)} %pad_clamp_fusion.1), kind=kCustom, calls=%fused_computation | custom fusion | bytes 20981760 | tf_op jit(solution)/shard_map/jit(_take)/gather | solution.py:97
  255.2 13.3 %fusion.2 = f32[8,320,2,192]{1,3,2,0:T(8,128)} fusion(bf16[8,320,2048,1]{2,1,3,0:T(8,128)(2,1)} %bitcast.108, bf16[16,2,192,2048]{3,2,1,0:T(8,128)(2,1)} %param.12), kind=kOutput, calls=%fused_computation.6 | convolution fusion | flops 4026531840 | bytes 27000832 | tf_op jit(solution)/shard_map/jrd,jgfd->jrgf/dot_general | solution.py:99
  268.5 11.2 %fusion.8 = bf16[8,320,2048]{2,1,0:T(8,128)(2,1)} fusion(bf16[16,192,2048]{2,1,0:T(8,128)(2,1)} %param.13, f32[8,320,2,192]{1,3,2,0:T(8,128)} %fusion.2), kind=kOutput, calls=%fused_computation.14 | convolution fusion | flops 2021457920 | bytes 21495808 | tf_op jit(solution)/shard_map/jrf,jfd->jrd/dot_general | solution.py:103
  279.7 13.8 %copy.32 = bf16[8,320,2048]{2,0,1:T(8,128)(2,1)} copy(bf16[8,320,2048]{2,1,0:T(8,128)(2,1)} %fusion.8) | data formatting | bytes 20971520 | tf_op jit(solution)/shard_map/convert_element_type | solution.py:106
  293.5 5.7 %dynamic-slice_bitcast_fusion.1 = bf16[2,640,2048]{2,1,0:T(8,128)(2,1)} fusion(bf16[2,2,640,2048]{3,2,1,0:T(8,128)(2,1)} %bitcast.104, s32[]{:T(128)S(6)} %select_n.145), kind=kLoop, calls=%fused_computation.24 | loop fusion | bytes 10485764 | tf_op jit(solution)/shard_map/jit(dynamic_index_in_dim)/squeeze | solution.py:40
  299.2 0.3 collective-permute-start
  299.5 6.5 %convert_add_fusion = f32[2,640,2048]{2,1,0:T(8,128)S(1)} fusion(bf16[2,640,2048]{2,1,0:T(8,128)(2,1)} %collective-permute-done.2, bf16[2,2,640,2048]{3,2,1,0:T(8,128)(2,1)} %bitcast.107, s32[]{:T(128)S(6)} %select_n.144), kind=kLoop, calls=%fused_computation.8 | loop fusion | flops 7864320 | bytes 20971524 | tf_op jit(solution)/shard_map/add | solution.py:43
  306.1 3.8 copy-done
  309.9 0.6 fusion.19
  310.5 1.5 collective-permute-start.3
  312.0 57.6 %collective-permute-done.3 = bf16[640,2048]{1,0:T(8,128)(2,1)} collective-permute-done((bf16[640,2048]{1,0:T(8,128)(2,1)S(1)}, bf16[640,2048]{1,0:T(8,128)(2,1)}, u32[]{:S(2)}, u32[]{:S(2)}) %collective-permute-start.3) | collective-permute-done | bytes 2621472 | tf_op jit(solution)/shard_map/ppermute | solution.py:52
  369.6 5.8 %fusion.14 = bf16[640,2048]{1,0:T(8,128)(2,1)} fusion(bf16[640,2048]{1,0:T(8,128)(2,1)} %collective-permute-done.3, f32[2,640,2048]{2,1,0:T(8,128)} %copy-done, s32[]{:T(128)S(6)} %select_n.147), kind=kLoop, calls=%fused_computation.18 | loop fusion | flops 3932160 | bytes 10485764 | tf_op jit(solution)/shard_map/convert_element_type | solution.py:53
  375.4 3.6 all-to-all-start.1
  379.1 6.5 %convert_add_fusion.1 = f32[2,640,2048]{2,1,0:T(8,128)S(1)} fusion(bf16[2,640,2048]{2,1,0:T(8,128)(2,1)} %collective-permute-done, bf16[2,2,640,2048]{3,2,1,0:T(8,128)(2,1)} %bitcast.105, s32[]{:T(128)S(6)} %select_n.144), kind=kLoop, calls=%fused_computation.9 | loop fusion | flops 7864320 | bytes 20971524 | tf_op jit(solution)/shard_map/add | solution.py:43
  385.6 0.4 fusion.18
  386.0 1.5 collective-permute-start.1
  387.5 56.7 %collective-permute-done.1 = bf16[640,2048]{1,0:T(8,128)(2,1)S(1)} collective-permute-done((bf16[640,2048]{1,0:T(8,128)(2,1)S(1)}, bf16[640,2048]{1,0:T(8,128)(2,1)S(1)}, u32[]{:S(2)}, u32[]{:S(2)}) %collective-permute-start.1) | collective-permute-done | bytes 2621472 | tf_op jit(solution)/shard_map/ppermute | solution.py:52
  444.2 2.5 fusion.15
  446.7 5.8 %all-to-all-start = ((bf16[8,80,2048]{2,1,0:T(8,128)(2,1)}), bf16[8,80,2048]{2,1,0:T(8,128)(2,1)}, u32[]{:S(2)}, u32[]{:S(2)}) async-start(bf16[8,80,2048]{2,1,0:T(8,128)(2,1)} %bitcast.110), calls=%async_computation | async-start | bytes 5242880 | tf_op jit(solution)/shard_map/all_to_all | solution.py:110
  452.6 0.1 copy.40
  452.8 0.1 copy.28
  453.0 58.2 %all-to-all-done = bf16[8,80,2048]{2,1,0:T(8,128)(2,1)} async-done(((bf16[8,80,2048]{2,1,0:T(8,128)(2,1)}), bf16[8,80,2048]{2,1,0:T(8,128)(2,1)}, u32[]{:S(2)}, u32[]{:S(2)}) %all-to-all-start) | async-done | bytes 2621472 | tf_op jit(solution)/shard_map/all_to_all | solution.py:110
  511.2 4.8 pad_maximum_fusion
  516.0 12.0 %gather_fusion.2 = bf16[1024,2048]{1,0:T(8,128)(2,1)} fusion(bf16[1280,2048]{1,0:T(8,128)(2,1)} %bitcast.103, s32[1024]{0:T(1024)S(1)} %broadcast_clamp_fusion), kind=kCustom, calls=%fused_computation.2 | custom fusion | bytes 8392704 | tf_op jit(solution)/shard_map/jit(_take)/gather | solution.py:117
  528.0 3.5 fusion.16
  531.6 1.1 copy.47
  (38 shorter events, 1.1 us)
Async XLA Ops:
  6.5 133.3 %all-gather.2.cloned.1.call-start = ((), (), s32[]{:S(2)}) async-start(), calls=%async_computation.2 | async-start | bytes 18382848 | tf_op jit(solution)/shard_map/all_gather | solution.py:82
  214.4 85.1 %collective-permute-start.2 = (bf16[2,640,2048]{2,1,0:T(8,128)(2,1)}, bf16[2,640,2048]{2,1,0:T(8,128)(2,1)}, u32[]{:S(2)}, u32[]{:S(2)}) collective-permute-start(bf16[2,640,2048]{2,1,0:T(8,128)(2,1)} %dynamic-slice_bitcast_fusion), channel_id=1, source_target_pairs={{0,1},{1,0},{2,3},{3,2},{4,5},{5,4},{6,7},{7,6},{8,9},{9,8},{10,11... | collective-permute-start | bytes 15728648 | tf_op jit(solution)/shard_map/ppermute | solution.py:42
  299.2 79.9 %collective-permute-start = (bf16[2,640,2048]{2,1,0:T(8,128)(2,1)}, bf16[2,640,2048]{2,1,0:T(8,128)(2,1)}, u32[]{:S(2)}, u32[]{:S(2)}) collective-permute-start(bf16[2,640,2048]{2,1,0:T(8,128)(2,1)} %dynamic-slice_bitcast_fusion.1), channel_id=1, source_target_pairs={{0,1},{1,0},{2,3},{3,2},{4,5},{5,4},{6,7},{7,6},{8,9},{9,8},{10,11... | collective-permute-start | bytes 15728648 | tf_op jit(solution)/shard_map/ppermute | solution.py:42
  306.0 3.8 copy-start
  310.5 59.1 %collective-permute-start.3 = (bf16[640,2048]{1,0:T(8,128)(2,1)S(1)}, bf16[640,2048]{1,0:T(8,128)(2,1)}, u32[]{:S(2)}, u32[]{:S(2)}) collective-permute-start(bf16[640,2048]{1,0:T(8,128)(2,1)S(1)} %fusion.19), channel_id=1, source_target_pairs={{0,2},{1,3},{2,0},{3,1},{4,6},{5,7},{6,4},{7,5},{8,10},{9,11},{10,... | collective-permute-start | bytes 7864328 | tf_op jit(solution)/shard_map/ppermute | solution.py:52
  375.4 71.3 %all-to-all-start.1 = ((bf16[8,80,2048]{2,1,0:T(8,128)(2,1)}), bf16[8,80,2048]{2,1,0:T(8,128)(2,1)S(1)}, u32[]{:S(2)}, u32[]{:S(2)}) async-start(bf16[8,80,2048]{2,1,0:T(8,128)(2,1)} %bitcast.111), calls=%async_computation.1 | async-start | bytes 5242880 | tf_op jit(solution)/shard_map/all_to_all | solution.py:110
  386.0 58.2 %collective-permute-start.1 = (bf16[640,2048]{1,0:T(8,128)(2,1)S(1)}, bf16[640,2048]{1,0:T(8,128)(2,1)S(1)}, u32[]{:S(2)}, u32[]{:S(2)}) collective-permute-start(bf16[640,2048]{1,0:T(8,128)(2,1)S(1)} %fusion.18), channel_id=1, source_target_pairs={{0,2},{1,3},{2,0},{3,1},{4,6},{5,7},{6,4},{7,5},{8,10},{9,11},{10,... | collective-permute-start | bytes 7864328 | tf_op jit(solution)/shard_map/ppermute | solution.py:52
  446.7 5.9 %copy-start.2 = (f32[128,8]{0,1:T(8,128)S(1)}, f32[128,8]{0,1:T(8,128)}, u32[]{:S(2)}) copy-start(f32[128,8]{0,1:T(8,128)} %param.11) | copy-start | bytes 12292
  446.7 6.1 %copy-start.1 = (s32[128,8]{0,1:T(8,128)S(1)}, s32[128,8]{0,1:T(8,128)}, u32[]{:S(2)}) copy-start(s32[128,8]{0,1:T(8,128)} %param.10) | copy-start | bytes 12292
  446.7 64.5 %all-to-all-start = ((bf16[8,80,2048]{2,1,0:T(8,128)(2,1)}), bf16[8,80,2048]{2,1,0:T(8,128)(2,1)}, u32[]{:S(2)}, u32[]{:S(2)}) async-start(bf16[8,80,2048]{2,1,0:T(8,128)(2,1)} %bitcast.110), calls=%async_computation | async-start | bytes 5242880 | tf_op jit(solution)/shard_map/all_to_all | solution.py:110
Sparse Core Ops, SparseCore 0:
  17.2 122.5 all-gather.1

commit v6 on v3

--- a/solution.py
+++ b/solution.py
@@ -78,20 +78,17 @@
         partial = jnp.einsum(
             "jrf,jfd->jrd", hidden, down_weight[span], preferred_element_type=jnp.float32
         )
-        partial = partial.astype(jnp.bfloat16).reshape(width, tok_count * owners, CAP, features)
-        partial = partial.transpose(1, 2, 0, 3).reshape(tok_count * owners, CAP * width, features)
+        partial = partial.astype(jnp.bfloat16)
         if sums:
             partial, _ = lax.optimization_barrier((partial, sums[-1]))
-        sums.append(lax.psum_scatter(partial, "tok", scatter_dimension=0, tiled=True))
+        sums.append(lax.psum_scatter(partial, "tok", scatter_dimension=1, tiled=True))
+        summed = sums[-1].reshape(width, owners, CAP, features).transpose(1, 0, 2, 3)
+        summed = summed.reshape(owners, width * CAP, features)
         returned.append(
-            lax.all_to_all(sums[-1], ("row", "col"), split_axis=0, concat_axis=0, tiled=True)
+            lax.all_to_all(summed, ("row", "col"), split_axis=0, concat_axis=0, tiled=True)
         )
     returned = jnp.concatenate(returned, axis=1)
-    expert = target // CAP
-    back = (
-        (expert // width) * (CAP * width) + (target % CAP) * width + expert % width
-    )
-    picked_back = jnp.take(returned.reshape(experts * CAP, features), back, axis=0)
+    picked_back = jnp.take(returned.reshape(experts * CAP, features), target, axis=0)
     picked_back = picked_back.reshape(count, chosen, features)
     mixed = jnp.einsum("tk,tkd->td", gates, picked_back.astype(jnp.float32))
     return mixed.astype(jnp.bfloat16)

time: 484 us -> 472 us (0.975); the launches traced: 475 us -> 469 us
  waiting for transfers between devices: 209 us -> 286 us
  blocking collectives: 66 us -> 0 us
  local copies, waits for them, and re-layouts: 118 us -> 95.8 us
  starting transfers between devices: 5.86 us -> 11.7 us
    reduce_scatter x2, waiting for transfers between devices: 26.9 us -> 103 us  [local(): lax.psum_scatter(partial, 'tok', scatter_dimension=1, tiled=True)]
    all_to_all x1 -> x0, blocking collectives: 66 us -> none  [local(): lax.all_to_all(sums[-1], ('row', 'col'), split_axis=0, concat_axis=0, til...]
    convert_element_type x2 -> x0, local copies, waits for them, and re-layouts: 27.6 us -> none  [local(): partial.astype(jnp.bfloat16)]
    gather x2, local copies, waits for them, and re-layouts: 68.8 us -> 59 us  [local(): picked = jnp.take(every, rows[span].reshape(-1), axis=0, mode='clip')]
    reshape x0 -> x2, local copies, waits for them, and re-layouts: none -> 5.85 us  [local(): summed = summed.reshape(owners, width * CAP, features)]
    all_to_all x1 -> x2, starting transfers between devices: 5.77 us -> 11.3 us  [local(): lax.all_to_all(summed, ('row', 'col'), split_axis=0, concat_axis=0, tiled...]
    all_to_all x1 -> x2, waiting for transfers between devices: 59.9 us -> 60 us  [local(): lax.all_to_all(summed, ('row', 'col'), split_axis=0, concat_axis=0, tiled...]
  transfers between devices with their start and end apart: 4 -> 5, of which waited for: 4 -> 4; matrix products, arithmetic and copies ran while one was open for 17% -> 15% of each run, Pallas kernels for 0% -> 0%
where the time goes in v6:
time: 472 us; the launch traced here: 469 us
  waiting for transfers between devices  286 us (61%)
  local copies, waits for them, and re-layouts  95.8 us (20%)
  matrix products  52.2 us (11%)
  between operations  13.8 us (3%)
  starting transfers between devices  11.7 us (2%)
  other arithmetic  9.66 us (2%)
    all_gather x1, waiting for transfers between devices, local(): every = lax.all_gather(packed, ALL, axis=0, tiled=True)  122 us
    reduce_scatter x2, waiting for transfers between devices, local(): lax.psum_scatter(partial, 'tok', scatter_dimension=1, tiled=True)  103 us
    all_to_all x2, waiting for transfers between devices, local(): lax.all_to_all(summed, ('row', 'col'), split_axis=0, concat_axis=0, tiled...  60 us
    gather x2, local copies, waits for them, and re-layouts, local(): picked = jnp.take(every, rows[span].reshape(-1), axis=0, mode='clip')  59 us
    dot_general x2, matrix products, local(): jnp.einsum('jrd,jgfd->jrgf', picked, gate_up_weight[span], preferred_elem...  26.2 us
    dot_general x2, matrix products, local(): jnp.einsum('jrf,jfd->jrd', hidden, down_weight[span], preferred_element_t...  22.4 us
    gather x1, local copies, waits for them, and re-layouts, local(): jnp.take(returned.reshape(experts * CAP, features), target, axis=0)  12 us
    all_to_all x2, starting transfers between devices, local(): lax.all_to_all(summed, ('row', 'col'), split_axis=0, concat_axis=0, tiled...  11.3 us
  transfers between devices with their start and end apart: 5, of which 4 were waited for; matrix products, arithmetic and copies ran while one was open for 15% of the time, Pallas kernels for 0%

profile of v6, /device:TPU:0, one launch (start us, length us, event | category | flops | bytes accessed | tf_op | source)
XLA Modules:
  0.0 468.9 jit_solution(8036707304032116973)
XLA Ops:
  6.5 0.8 copy.42
  7.3 0.1 eq.26
  7.4 0.1 reshape.139
  7.5 0.7 broadcast_multiply_fusion
  8.2 0.1 copy.44
  8.3 0.2 fusion.30
  8.6 0.1 copy.45
  8.7 0.1 copy.48
  8.8 0.1 mul.79
  8.9 0.4 fusion.29
  9.3 4.3 scatter_custom_fusion
  13.7 1.2 fusion.25
  14.9 1.2 fusion.27
  16.2 0.9 pad_maximum_fusion.1
  17.0 0.2 reduce-scatter.3.cloned.1.call-start
  17.3 122.5 %all-gather.2.cloned.1.call-done = bf16[4352,2048]{1,0:T(8,128)(2,1)} async-done(((bf16[136,2048]{1,0:T(8,128)(2,1)}), bf16[4352,2048]{1,0:T(8,128)(2,1)}) %all-gather.2.cloned.1.call-update) | async-done | bytes 17825808 | tf_op jit(solution)/shard_map/all_gather | solution.py:57
  139.7 1.3 slice.77
  141.0 0.6 copy.66
  141.7 0.1 convert_add_fusion
  141.7 0.2 reshape.144
  141.9 0.1 copy.49
  142.0 0.1 reshape.154
  142.2 28.5 %gather_fusion = bf16[2560,2048]{1,0:T(8,128)(2,1)} fusion(bf16[4352,2048]{1,0:T(8,128)(2,1)} %all-gather.2.cloned.1.call-done, s32[3072]{0:T(1024)S(1)} %pad_clamp_fusion.1), kind=kCustom, calls=%fused_computation | custom fusion | bytes 20981760 | tf_op jit(solution)/shard_map/jit(_take)/gather | solution.py:72
  170.7 13.4 %fusion.2 = f32[8,320,2,192]{1,3,2,0:T(8,128)} fusion(bf16[8,320,2048,1]{2,1,3,0:T(8,128)(2,1)} %bitcast.77, bf16[16,2,192,2048]{3,2,1,0:T(8,128)(2,1)} %param.12), kind=kOutput, calls=%fused_computation.6 | convolution fusion | flops 4026531840 | bytes 27000832 | tf_op jit(solution)/shard_map/jrd,jgfd->jrgf/dot_general | solution.py:74
  184.1 11.2 %fusion.8 = bf16[8,320,2048]{2,1,0:T(8,128)(2,1)} fusion(bf16[16,192,2048]{2,1,0:T(8,128)(2,1)} %param.13, f32[8,320,2,192]{1,3,2,0:T(8,128)} %fusion.2), kind=kOutput, calls=%fused_computation.12 | convolution fusion | flops 2021457920 | bytes 21495808 | tf_op jit(solution)/shard_map/jrf,jfd->jrd/dot_general | solution.py:78
  195.3 0.3 reduce-scatter.5.cloned.1.call-start
  195.7 0.1 reshape.162
  195.8 30.4 %gather_fusion.1 = bf16[2560,2048]{1,0:T(8,128)(2,1)} fusion(bf16[4352,2048]{1,0:T(8,128)(2,1)} %all-gather.2.cloned.1.call-done, s32[3072]{0:T(1024)S(1)} %pad_clamp_fusion), kind=kCustom, calls=%fused_computation.1 | custom fusion | bytes 20981760 | tf_op jit(solution)/shard_map/jit(_take)/gather | solution.py:72
  226.3 12.9 %fusion = f32[8,320,2,192]{1,3,0,2:T(8,128)} fusion(bf16[8,320,2048,1]{2,1,0,3:T(8,128)(2,1)} %bitcast.76, bf16[16,2,192,2048]{3,2,1,0:T(8,128)(2,1)} %param.12), kind=kOutput, calls=%fused_computation.4 | convolution fusion | flops 4026531840 | bytes 27000832 | tf_op jit(solution)/shard_map/jrd,jgfd->jrgf/dot_general | solution.py:74
  239.1 11.2 %fusion.11 = bf16[8,320,2048]{2,1,0:T(8,128)(2,1)} fusion(bf16[16,192,2048]{2,1,0:T(8,128)(2,1)} %param.13, f32[8,320,2,192]{1,3,0,2:T(8,128)} %fusion), kind=kOutput, calls=%fused_computation.13 | convolution fusion | flops 2021457920 | bytes 21495808 | tf_op jit(solution)/shard_map/jrf,jfd->jrd/dot_general | solution.py:78
  250.3 28.6 %reduce-scatter.3.cloned.1.call-done = bf16[8,80,2048]{2,1,0:T(8,128)(2,1)} async-done(((bf16[8,320,2048]{2,1,0:T(8,128)(2,1)}), bf16[8,80,2048]{2,1,0:T(8,128)(2,1)}) %reduce-scatter.3.cloned.1.call-update) | async-done | bytes 2621456 | tf_op jit(solution)/shard_map/reduce_scatter | solution.py:84
  279.0 1.7 copy-done
  280.7 1.4 copy.51
  282.1 1.4 copy.52
  283.6 2.9 copy.53
  286.5 5.7 %all-to-all-start = ((bf16[8,80,2048]{2,1,0:T(8,128)(2,1)}), bf16[8,80,2048]{2,1,0:T(8,128)(2,1)S(1)}, u32[]{:S(2)}, u32[]{:S(2)}) async-start(bf16[8,80,2048]{2,1,0:T(8,128)(2,1)} %copy.53), calls=%async_computation.1 | async-start | bytes 5242880 | tf_op jit(solution)/shard_map/all_to_all | solution.py:88
  292.2 74.7 %reduce-scatter.5.cloned.1.call-done = bf16[8,80,2048]{2,1,0:T(8,128)(2,1)} async-done(((bf16[8,320,2048]{2,1,0:T(8,128)(2,1)}), bf16[8,80,2048]{2,1,0:T(8,128)(2,1)}) %reduce-scatter.5.cloned.1.call-update) | async-done | bytes 2621456 | tf_op jit(solution)/shard_map/reduce_scatter | solution.py:84
  366.9 3.2 copy.57
  370.1 1.4 copy.58
  371.5 2.9 copy.59
  374.5 5.5 %all-to-all-start.1 = ((bf16[8,80,2048]{2,1,0:T(8,128)(2,1)}), bf16[8,80,2048]{2,1,0:T(8,128)(2,1)}, u32[]{:S(2)}, u32[]{:S(2)}) async-start(bf16[8,80,2048]{2,1,0:T(8,128)(2,1)} %copy.59), calls=%async_computation.3 | async-start | bytes 5242880 | tf_op jit(solution)/shard_map/all_to_all | solution.py:88
  380.2 0.1 copy.47
  380.3 0.1 copy.63
  380.5 60.0 %all-to-all-done.1 = bf16[8,80,2048]{2,1,0:T(8,128)(2,1)} async-done(((bf16[8,80,2048]{2,1,0:T(8,128)(2,1)}), bf16[8,80,2048]{2,1,0:T(8,128)(2,1)}, u32[]{:S(2)}, u32[]{:S(2)}) %all-to-all-start.1) | async-done | bytes 2621472 | tf_op jit(solution)/shard_map/all_to_all | solution.py:88
  440.4 4.8 %pad_maximum_fusion = bf16[8,160,2048]{2,1,0:T(8,128)(2,1)} fusion(bf16[8,80,2048]{2,1,0:T(8,128)(2,1)} %all-to-all-done.1, bf16[8,80,2048]{2,1,0:T(8,128)(2,1)S(1)} %all-to-all-done), kind=kLoop, calls=%fused_computation.14 | loop fusion | flops 10485760 | bytes 10485760 | tf_op jit(solution)/shard_map/concatenate | solution.py:90
  445.2 12.0 %gather_fusion.2 = bf16[1024,2048]{1,0:T(8,128)(2,1)} fusion(bf16[1280,2048]{1,0:T(8,128)(2,1)} %bitcast.75, s32[1024]{0:T(1024)S(1)} %broadcast_clamp_fusion), kind=kCustom, calls=%fused_computation.2 | custom fusion | bytes 8392704 | tf_op jit(solution)/shard_map/jit(_take)/gather | solution.py:91
  457.3 3.5 fusion.14
  460.8 1.1 copy.70
  (32 shorter events, 0.5 us)
Async XLA Ops:
  6.5 133.2 %all-gather.2.cloned.1.call-start = ((), (), s32[]{:S(2)}) async-start(), calls=%async_computation.4 | async-start | bytes 18382848 | tf_op jit(solution)/shard_map/all_gather | solution.py:57
  17.0 261.9 %reduce-scatter.3.cloned.1.call-start = ((), (), s32[]{:S(2)}) async-start(), calls=%async_computation.5 | async-start | bytes 13107200 | tf_op jit(solution)/shard_map/reduce_scatter | solution.py:84
  195.3 171.6 %reduce-scatter.5.cloned.1.call-start = ((), (), s32[]{:S(2)}) async-start(), calls=%async_computation.6 | async-start | bytes 13107200 | tf_op jit(solution)/shard_map/reduce_scatter | solution.py:84
  278.9 1.7 copy-start
  286.5 88.0 %all-to-all-start = ((bf16[8,80,2048]{2,1,0:T(8,128)(2,1)}), bf16[8,80,2048]{2,1,0:T(8,128)(2,1)S(1)}, u32[]{:S(2)}, u32[]{:S(2)}) async-start(bf16[8,80,2048]{2,1,0:T(8,128)(2,1)} %copy.53), calls=%async_computation.1 | async-start | bytes 5242880 | tf_op jit(solution)/shard_map/all_to_all | solution.py:88
  371.5 8.6 %copy-start.1 = (s32[128,8]{0,1:T(8,128)S(1)}, s32[128,8]{0,1:T(8,128)}, u32[]{:S(2)}) copy-start(s32[128,8]{0,1:T(8,128)} %param.10) | copy-start | bytes 12292
  371.5 8.8 %copy-start.2 = (f32[128,8]{0,1:T(8,128)S(1)}, f32[128,8]{0,1:T(8,128)}, u32[]{:S(2)}) copy-start(f32[128,8]{0,1:T(8,128)} %param.11) | copy-start | bytes 12292
  374.5 66.0 %all-to-all-start.1 = ((bf16[8,80,2048]{2,1,0:T(8,128)(2,1)}), bf16[8,80,2048]{2,1,0:T(8,128)(2,1)}, u32[]{:S(2)}, u32[]{:S(2)}) async-start(bf16[8,80,2048]{2,1,0:T(8,128)(2,1)} %copy.59), calls=%async_computation.3 | async-start | bytes 5242880 | tf_op jit(solution)/shard_map/all_to_all | solution.py:88
Sparse Core Ops, SparseCore 0:
  17.2 122.5 all-gather.1
  195.4 83.4 reduce-scatter.2
  281.5 85.2 reduce-scatter.4

commit v7 on v6

--- a/solution.py
+++ b/solution.py
@@ -6,7 +6,7 @@
 from jax.sharding import PartitionSpec as P
 
 CAP = 10
-PIECES = 2
+PIECES = 4
 
 
 EPSILON = 1e-06

time: 472 us -> 516 us (1.093); the launches traced: 469 us -> 507 us
  local copies, waits for them, and re-layouts: 95.8 us -> 133 us
  waiting for transfers between devices: 286 us -> 271 us
  starting transfers between devices: 11.7 us -> 19.3 us
  matrix products: 52.2 us -> 59.4 us
    reduce_scatter x2 -> x4, waiting for transfers between devices: 103 us -> 38.9 us  [local(): lax.psum_scatter(partial, 'tok', scatter_dimension=1, tiled=True)]
    all_to_all x2 -> x4, waiting for transfers between devices: 60 us -> 110 us  [local(): lax.all_to_all(summed, ('row', 'col'), split_axis=0, concat_axis=0, tiled...]
    gather x2 -> x4, local copies, waits for them, and re-layouts: 59 us -> 77.7 us  [local(): picked = jnp.take(every, rows[span].reshape(-1), axis=0, mode='clip')]
    slice x0 -> x1, local copies, waits for them, and re-layouts: none -> 16.3 us  [local(): gate_up_weight[span]]
    all_to_all x2 -> x4, starting transfers between devices: 11.3 us -> 18.1 us  [local(): lax.all_to_all(summed, ('row', 'col'), split_axis=0, concat_axis=0, tiled...]
    dot_general x2 -> x4, matrix products: 26.2 us -> 32.8 us  [local(): jnp.einsum('jrd,jgfd->jrgf', picked, gate_up_weight[span], preferred_elem...]
    dot_general x2 -> x4, matrix products: 22.4 us -> 23.1 us  [local(): jnp.einsum('jrf,jfd->jrd', hidden, down_weight[span], preferred_element_t...]
  transfers between devices with their start and end apart: 5 -> 9, of which waited for: 4 -> 7; matrix products, arithmetic and copies ran while one was open for 15% -> 27% of each run, Pallas kernels for 0% -> 0%
where the time goes in v7:
time: 516 us; the launch traced here: 507 us
  waiting for transfers between devices  271 us (53%)
  local copies, waits for them, and re-layouts  133 us (26%)
  matrix products  59.4 us (12%)
  starting transfers between devices  19.3 us (4%)
  between operations  13.8 us (3%)
  other arithmetic  9.89 us (2%)
    all_gather x1, waiting for transfers between devices, local(): every = lax.all_gather(packed, ALL, axis=0, tiled=True)  123 us
    all_to_all x4, waiting for transfers between devices, local(): lax.all_to_all(summed, ('row', 'col'), split_axis=0, concat_axis=0, tiled...  110 us
    gather x4, local copies, waits for them, and re-layouts, local(): picked = jnp.take(every, rows[span].reshape(-1), axis=0, mode='clip')  77.7 us
    reduce_scatter x4, waiting for transfers between devices, local(): lax.psum_scatter(partial, 'tok', scatter_dimension=1, tiled=True)  38.9 us
    dot_general x4, matrix products, local(): jnp.einsum('jrd,jgfd->jrgf', picked, gate_up_weight[span], preferred_elem...  32.8 us
    dot_general x4, matrix products, local(): jnp.einsum('jrf,jfd->jrd', hidden, down_weight[span], preferred_element_t...  23.1 us
    all_to_all x4, starting transfers between devices, local(): lax.all_to_all(summed, ('row', 'col'), split_axis=0, concat_axis=0, tiled...  18.1 us
    slice x1, local copies, waits for them, and re-layouts, local(): gate_up_weight[span]  16.3 us
  transfers between devices with their start and end apart: 9, of which 7 were waited for; matrix products, arithmetic and copies ran while one was open for 27% of the time, Pallas kernels for 0%

profile of v7, /device:TPU:0, one launch (start us, length us, event | category | flops | bytes accessed | tf_op | source)
XLA Modules:
  0.0 506.6 jit_solution(9325426834161170466)
XLA Ops:
  6.5 0.7 broadcast_multiply_fusion
  7.3 0.8 copy.68
  8.3 1.2 fusion.23
  10.6 4.3 scatter_custom_fusion
  15.2 0.9 pad_maximum_fusion.1
  16.2 122.6 %all-gather.2.cloned.1.call-done = bf16[4352,2048]{1,0:T(8,128)(2,1)} async-done(((bf16[136,2048]{1,0:T(8,128)(2,1)}), bf16[4352,2048]{1,0:T(8,128)(2,1)}) %all-gather.2.cloned.1.call-update) | async-done | bytes 17825808 | tf_op jit(solution)/shard_map/all_gather | solution.py:57
  138.8 1.3 slice.123
  140.1 0.6 copy.108
  141.2 19.2 %gather_fusion = bf16[1280,2048]{1,0:T(8,128)(2,1)} fusion(bf16[4352,2048]{1,0:T(8,128)(2,1)} %all-gather.2.cloned.1.call-done, s32[2048]{0:T(1024)S(1)} %pad_clamp_fusion.3), kind=kCustom, calls=%fused_computation | custom fusion | bytes 10490880 | tf_op jit(solution)/shard_map/jit(_take)/gather | solution.py:72
  160.4 7.8 %fusion.6 = f32[4,320,2,192]{1,3,2,0:T(8,128)S(1)} fusion(bf16[4,320,2048,1]{2,1,3,0:T(8,128)(2,1)} %bitcast.124, bf16[16,2,192,2048]{3,2,1,0:T(8,128)(2,1)} %param.12), kind=kOutput, calls=%fused_computation.12 | convolution fusion | flops 2013265920 | bytes 13500416 | tf_op jit(solution)/shard_map/jrd,jgfd->jrgf/dot_general | solution.py:74
  168.2 5.8 %convolution_convert_fusion.3 = bf16[4,320,2048]{2,1,0:T(8,128)(2,1)} fusion(bf16[16,192,2048]{2,1,0:T(8,128)(2,1)} %param.13, f32[4,320,2,192]{1,3,2,0:T(8,128)S(1)} %fusion.6), kind=kOutput, calls=%fused_computation.21 | convolution fusion | flops 1010728960 | bytes 10354688 | tf_op jit(solution)/shard_map/jrf,jfd->jrd/dot_general | solution.py:78
  174.3 16.3 %fusion.49 = (bf16[4,2,192,2048]{3,2,1,0:T(8,128)(2,1)}, bf16[4,2,192,2048]{3,2,1,0:T(8,128)(2,1)}, bf16[4,2,192,2048]{3,2,1,0:T(8,128)(2,1)}) fusion(bf16[16,2,192,2048]{3,2,1,0:T(8,128)(2,1)} %param.12), kind=kLoop, calls=%fused_computation.91 | loop fusion | bytes 37748736 | tf_op jit(solution)/shard_map/slice | solution.py:75
  190.8 20.0 %gather_fusion.1 = bf16[1280,2048]{1,0:T(8,128)(2,1)} fusion(bf16[4352,2048]{1,0:T(8,128)(2,1)} %all-gather.2.cloned.1.call-done, s32[2048]{0:T(1024)S(1)} %pad_clamp_fusion.2), kind=kCustom, calls=%fused_computation.1 | custom fusion | bytes 10490880 | tf_op jit(solution)/shard_map/jit(_take)/gather | solution.py:72
  210.9 7.8 %fusion.4 = f32[4,320,2,192]{1,3,0,2:T(8,128)S(1)} fusion(bf16[4,320,2048,1]{2,1,0,3:T(8,128)(2,1)} %bitcast.122, bf16[4,2,192,2048]{3,2,1,0:T(8,128)(2,1)} %get-tuple-element.23), kind=kOutput, calls=%fused_computation.10 | convolution fusion | flops 2013265920 | bytes 13500416 | tf_op jit(solution)/shard_map/jrd,jgfd->jrgf/dot_general | solution.py:74
  218.6 5.8 %convolution_convert_fusion.2 = bf16[4,320,2048]{2,1,0:T(8,128)(2,1)} fusion(bf16[16,192,2048]{2,1,0:T(8,128)(2,1)} %param.13, f32[4,320,2,192]{1,3,0,2:T(8,128)S(1)} %fusion.4), kind=kOutput, calls=%fused_computation.20 | convolution fusion | flops 1010728960 | bytes 10354688 | tf_op jit(solution)/shard_map/jrf,jfd->jrd/dot_general | solution.py:78
  224.4 0.6 reduce-scatter.9.cloned.1.call-start
  225.2 19.2 %gather_fusion.2 = bf16[1280,2048]{1,0:T(8,128)(2,1)} fusion(bf16[4352,2048]{1,0:T(8,128)(2,1)} %all-gather.2.cloned.1.call-done, s32[2048]{0:T(1024)S(1)} %pad_clamp_fusion.1), kind=kCustom, calls=%fused_computation.2 | custom fusion | bytes 10490880 | tf_op jit(solution)/shard_map/jit(_take)/gather | solution.py:72
  244.4 8.7 %fusion.2 = f32[4,320,2,192]{1,3,0,2:T(8,128)S(1)} fusion(bf16[4,320,2048,1]{2,1,0,3:T(8,128)(2,1)} %bitcast.123, bf16[4,2,192,2048]{3,2,1,0:T(8,128)(2,1)} %get-tuple-element.25), kind=kOutput, calls=%fused_computation.8 | convolution fusion | flops 2013265920 | bytes 13500416 | tf_op jit(solution)/shard_map/jrd,jgfd->jrgf/dot_general | solution.py:74
  253.1 5.8 %convolution_convert_fusion.1 = bf16[4,320,2048]{2,1,0:T(8,128)(2,1)} fusion(bf16[16,192,2048]{2,1,0:T(8,128)(2,1)} %param.13, f32[4,320,2,192]{1,3,0,2:T(8,128)S(1)} %fusion.2), kind=kOutput, calls=%fused_computation.19 | convolution fusion | flops 1010728960 | bytes 10354688 | tf_op jit(solution)/shard_map/jrf,jfd->jrd/dot_general | solution.py:78
  258.8 19.0 %reduce-scatter.7.cloned.1.call-done = bf16[4,80,2048]{2,1,0:T(8,128)(2,1)} async-done(((bf16[4,320,2048]{2,1,0:T(8,128)(2,1)}), bf16[4,80,2048]{2,1,0:T(8,128)(2,1)}) %reduce-scatter.7.cloned.1.call-update) | async-done | bytes 1310736 | tf_op jit(solution)/shard_map/reduce_scatter | solution.py:84
  278.3 19.2 %gather_fusion.3 = bf16[1280,2048]{1,0:T(8,128)(2,1)} fusion(bf16[4352,2048]{1,0:T(8,128)(2,1)} %all-gather.2.cloned.1.call-done, s32[2048]{0:T(1024)S(1)} %pad_clamp_fusion), kind=kCustom, calls=%fused_computation.3 | custom fusion | bytes 10490880 | tf_op jit(solution)/shard_map/jit(_take)/gather | solution.py:72
  297.5 8.6 %fusion = f32[4,320,2,192]{1,3,0,2:T(8,128)S(1)} fusion(bf16[4,320,2048,1]{2,1,0,3:T(8,128)(2,1)} %bitcast.121, bf16[4,2,192,2048]{3,2,1,0:T(8,128)(2,1)} %get-tuple-element.24), kind=kOutput, calls=%fused_computation.6 | convolution fusion | flops 2013265920 | bytes 13500416 | tf_op jit(solution)/shard_map/jrd,jgfd->jrgf/dot_general | solution.py:74
  306.0 5.8 %convolution_convert_fusion = bf16[4,320,2048]{2,1,0:T(8,128)(2,1)} fusion(bf16[16,192,2048]{2,1,0:T(8,128)(2,1)} %param.13, f32[4,320,2,192]{1,3,0,2:T(8,128)S(1)} %fusion), kind=kOutput, calls=%fused_computation.18 | convolution fusion | flops 1010728960 | bytes 10354688 | tf_op jit(solution)/shard_map/jrf,jfd->jrd/dot_general | solution.py:78
  311.8 19.8 %reduce-scatter.9.cloned.1.call-done = bf16[4,80,2048]{2,1,0:T(8,128)(2,1)} async-done(((bf16[4,320,2048]{2,1,0:T(8,128)(2,1)}), bf16[4,80,2048]{2,1,0:T(8,128)(2,1)}) %reduce-scatter.9.cloned.1.call-update) | async-done | bytes 1310736 | tf_op jit(solution)/shard_map/reduce_scatter | solution.py:84
  331.7 1.0 copy.77
  332.7 0.7 copy.78
  333.5 1.8 copy.79
  335.2 5.7 %all-to-all-start = ((bf16[8,40,2048]{2,1,0:T(8,128)(2,1)}), bf16[8,40,2048]{2,1,0:T(8,128)(2,1)S(1)}, u32[]{:S(2)}, u32[]{:S(2)}) async-start(bf16[8,40,2048]{2,1,0:T(8,128)(2,1)} %copy.79), calls=%async_computation.1 | async-start | bytes 2621440 | tf_op jit(solution)/shard_map/all_to_all | solution.py:88
  341.0 1.0 copy.83
  342.0 0.7 copy.84
  342.8 1.8 copy.85
  344.6 28.6 %all-to-all-done = bf16[8,40,2048]{2,1,0:T(8,128)(2,1)S(1)} async-done(((bf16[8,40,2048]{2,1,0:T(8,128)(2,1)}), bf16[8,40,2048]{2,1,0:T(8,128)(2,1)S(1)}, u32[]{:S(2)}, u32[]{:S(2)}) %all-to-all-start) | async-done | bytes 1310752 | tf_op jit(solution)/shard_map/all_to_all | solution.py:88
  373.2 3.6 all-to-all-start.1
  376.8 2.3 copy.89
  379.1 0.7 copy.90
  379.8 1.8 copy.91
  381.6 26.4 %all-to-all-done.1 = bf16[8,40,2048]{2,1,0:T(8,128)(2,1)S(1)} async-done(((bf16[8,40,2048]{2,1,0:T(8,128)(2,1)}), bf16[8,40,2048]{2,1,0:T(8,128)(2,1)S(1)}, u32[]{:S(2)}, u32[]{:S(2)}) %all-to-all-start.1) | async-done | bytes 1310752 | tf_op jit(solution)/shard_map/all_to_all | solution.py:88
  408.0 4.3 all-to-all-start.2
  412.3 2.3 copy.95
  414.7 0.7 copy.96
  415.4 1.8 copy.97
  417.2 25.3 %all-to-all-done.2 = bf16[8,40,2048]{2,1,0:T(8,128)(2,1)} async-done(((bf16[8,40,2048]{2,1,0:T(8,128)(2,1)}), bf16[8,40,2048]{2,1,0:T(8,128)(2,1)}, u32[]{:S(2)}, u32[]{:S(2)}) %all-to-all-start.2) | async-done | bytes 1310752 | tf_op jit(solution)/shard_map/all_to_all | solution.py:88
  442.5 4.5 all-to-all-start.3
  447.5 29.7 %all-to-all-done.3 = bf16[8,40,2048]{2,1,0:T(8,128)(2,1)} async-done(((bf16[8,40,2048]{2,1,0:T(8,128)(2,1)}), bf16[8,40,2048]{2,1,0:T(8,128)(2,1)}, u32[]{:S(2)}, u32[]{:S(2)}) %all-to-all-start.3) | async-done | bytes 1310752 | tf_op jit(solution)/shard_map/all_to_all | solution.py:88
  477.2 6.0 %pad_maximum_fusion = bf16[8,160,2048]{2,1,0:T(8,128)(2,1)} fusion(bf16[8,40,2048]{2,1,0:T(8,128)(2,1)} %all-to-all-done.3, bf16[8,40,2048]{2,1,0:T(8,128)(2,1)} %all-to-all-done.2, bf16[8,40,2048]{2,1,0:T(8,128)(2,1)S(1)} %all-to-all-done.1, bf16[8,40,2048]{2,1,0:T(8,128)(2,1)S(1)} %all-to-all-done), kind=kLoop, calls=%fused_computation.14 | loop fusion | flops 20971520 | bytes 10485760 | tf_op jit(solution)/shard_map/concatenate | solution.py:90
  483.2 12.0 %gather_fusion.4 = bf16[1024,2048]{1,0:T(8,128)(2,1)} fusion(bf16[1280,2048]{1,0:T(8,128)(2,1)} %bitcast.120, s32[1024]{0:T(1024)S(1)} %broadcast_clamp_fusion), kind=kCustom, calls=%fused_computation.4 | custom fusion | bytes 8392704 | tf_op jit(solution)/shard_map/jit(_take)/gather | solution.py:91
  495.2 3.5 fusion.8
  498.7 1.1 copy.116
  (67 shorter events, 3.6 us)
Async XLA Ops:
  6.5 8.4 %copy-start = (bf16[128,2048]{1,0:T(8,128)(2,1)S(1)}, bf16[128,2048]{1,0:T(8,128)(2,1)}, u32[]{:S(2)}) copy-start(bf16[128,2048]{1,0:T(8,128)(2,1)} %param.8) | copy-start | bytes 1572868
  6.5 8.5 %copy-start.5 = (f32[2048]{0:T(1024)S(1)}, f32[2048]{0:T(1024)}, u32[]{:S(2)}) copy-start(f32[2048]{0:T(1024)} %param.9) | copy-start | bytes 24580
  6.5 132.2 %all-gather.2.cloned.1.call-start = ((), (), s32[]{:S(2)}) async-start(), calls=%async_computation.8 | async-start | bytes 18382848 | tf_op jit(solution)/shard_map/all_gather | solution.py:57
  16.1 208.3 %reduce-scatter.5.cloned.1.call-start = ((), (), s32[]{:S(2)}) async-start(), calls=%async_computation.9 | async-start | bytes 6553600 | tf_op jit(solution)/shard_map/reduce_scatter | solution.py:84
  174.0 103.9 %reduce-scatter.7.cloned.1.call-start = ((), (), s32[]{:S(2)}) async-start(), calls=%async_computation.10 | async-start | bytes 6553600 | tf_op jit(solution)/shard_map/reduce_scatter | solution.py:84
  224.4 107.2 %reduce-scatter.9.cloned.1.call-start = ((), (), s32[]{:S(2)}) async-start(), calls=%async_computation.11 | async-start | bytes 6553600 | tf_op jit(solution)/shard_map/reduce_scatter | solution.py:84
  277.9 134.4 %reduce-scatter.11.cloned.1.call-start = ((), (), s32[]{:S(2)}) async-start(), calls=%async_computation.12 | async-start | bytes 6553600 | tf_op jit(solution)/shard_map/reduce_scatter | solution.py:84
  311.8 19.9 %copy-start.1 = (bf16[4,80,2048]{2,1,0:T(8,128)(2,1)S(1)}, bf16[4,80,2048]{2,1,0:T(8,128)(2,1)}, u32[]{:S(2)}) copy-start(bf16[4,80,2048]{2,1,0:T(8,128)(2,1)} %reduce-scatter.5.cloned.1.call-done) | copy-start | bytes 3932164
  332.7 8.3 %copy-start.2 = (bf16[4,80,2048]{2,1,0:T(8,128)(2,1)S(1)}, bf16[4,80,2048]{2,1,0:T(8,128)(2,1)}, u32[]{:S(2)}) copy-start(bf16[4,80,2048]{2,1,0:T(8,128)(2,1)} %reduce-scatter.7.cloned.1.call-done) | copy-start | bytes 3932164
  335.2 37.9 %all-to-all-start = ((bf16[8,40,2048]{2,1,0:T(8,128)(2,1)}), bf16[8,40,2048]{2,1,0:T(8,128)(2,1)S(1)}, u32[]{:S(2)}, u32[]{:S(2)}) async-start(bf16[8,40,2048]{2,1,0:T(8,128)(2,1)} %copy.79), calls=%async_computation.1 | async-start | bytes 2621440 | tf_op jit(solution)/shard_map/all_to_all | solution.py:88
  373.2 34.8 %all-to-all-start.1 = ((bf16[8,40,2048]{2,1,0:T(8,128)(2,1)}), bf16[8,40,2048]{2,1,0:T(8,128)(2,1)S(1)}, u32[]{:S(2)}, u32[]{:S(2)}) async-start(bf16[8,40,2048]{2,1,0:T(8,128)(2,1)} %copy.85), calls=%async_computation.3 | async-start | bytes 2621440 | tf_op jit(solution)/shard_map/all_to_all | solution.py:88
  408.0 34.4 %all-to-all-start.2 = ((bf16[8,40,2048]{2,1,0:T(8,128)(2,1)}), bf16[8,40,2048]{2,1,0:T(8,128)(2,1)}, u32[]{:S(2)}, u32[]{:S(2)}) async-start(bf16[8,40,2048]{2,1,0:T(8,128)(2,1)} %copy.91), calls=%async_computation.5 | async-start | bytes 2621440 | tf_op jit(solution)/shard_map/all_to_all | solution.py:88
  414.7 32.4 %copy-start.4 = (f32[128,8]{0,1:T(8,128)S(1)}, f32[128,8]{0,1:T(8,128)}, u32[]{:S(2)}) copy-start(f32[128,8]{0,1:T(8,128)} %param.11) | copy-start | bytes 12292
  414.7 32.6 %copy-start.3 = (s32[128,8]{0,1:T(8,128)S(1)}, s32[128,8]{0,1:T(8,128)}, u32[]{:S(2)}) copy-start(s32[128,8]{0,1:T(8,128)} %param.10) | copy-start | bytes 12292
  442.5 34.7 %all-to-all-start.3 = ((bf16[8,40,2048]{2,1,0:T(8,128)(2,1)}), bf16[8,40,2048]{2,1,0:T(8,128)(2,1)}, u32[]{:S(2)}, u32[]{:S(2)}) async-start(bf16[8,40,2048]{2,1,0:T(8,128)(2,1)} %copy.97), calls=%async_computation.7 | async-start | bytes 2621440 | tf_op jit(solution)/shard_map/all_to_all | solution.py:88
Sparse Core Ops, SparseCore 0:
  16.2 122.5 all-gather.1
  174.1 49.5 reduce-scatter.4
  226.4 51.3 reduce-scatter.6
  280.2 51.3 reduce-scatter.8
  334.2 51.3 reduce-scatter.10

commit v8 on v7

--- a/solution.py
+++ b/solution.py
@@ -80,7 +80,7 @@
         )
         partial = partial.astype(jnp.bfloat16)
         if sums:
-            partial, _ = lax.optimization_barrier((partial, sums[-1]))
+            partial, _ = lax.optimization_barrier((partial, (sums[-1], returned[:-1])))
         sums.append(lax.psum_scatter(partial, "tok", scatter_dimension=1, tiled=True))
         summed = sums[-1].reshape(width, owners, CAP, features).transpose(1, 0, 2, 3)
         summed = summed.reshape(owners, width * CAP, features)

time: 516 us -> 467 us (0.905)
  waiting for transfers between devices: 271 us -> 216 us
    all_to_all x4, waiting for transfers between devices: 110 us -> 31.9 us  [local(): lax.all_to_all(summed, ('row', 'col'), split_axis=0, concat_axis=0, tiled...]
    reduce_scatter x4, waiting for transfers between devices: 38.9 us -> 61.2 us  [local(): lax.psum_scatter(partial, 'tok', scatter_dimension=1, tiled=True)]
  transfers between devices with their start and end apart: 9 -> 9, of which waited for: 7 -> 5; matrix products, arithmetic and copies ran while one was open for 27% -> 30% of each run, Pallas kernels for 0% -> 0%
where the time goes in v8:
time: 467 us; the launch traced here: 458 us
  waiting for transfers between devices  216 us (46%)
  local copies, waits for them, and re-layouts  138 us (30%)
  matrix products  58.2 us (12%)
  starting transfers between devices  22.6 us (5%)
  between operations  14 us (3%)
  other arithmetic  9.89 us (2%)
    all_gather x1, waiting for transfers between devices, local(): every = lax.all_gather(packed, ALL, axis=0, tiled=True)  123 us
    gather x4, local copies, waits for them, and re-layouts, local(): picked = jnp.take(every, rows[span].reshape(-1), axis=0, mode='clip')  80 us
    reduce_scatter x4, waiting for transfers between devices, local(): lax.psum_scatter(partial, 'tok', scatter_dimension=1, tiled=True)  61.2 us
    all_to_all x4, waiting for transfers between devices, local(): lax.all_to_all(summed, ('row', 'col'), split_axis=0, concat_axis=0, tiled...  31.9 us
    dot_general x4, matrix products, local(): jnp.einsum('jrd,jgfd->jrgf', picked, gate_up_weight[span], preferred_elem...  31.4 us
    dot_general x4, matrix products, local(): jnp.einsum('jrf,jfd->jrd', hidden, down_weight[span], preferred_element_t...  23.3 us
    all_to_all x4, starting transfers between devices, local(): lax.all_to_all(summed, ('row', 'col'), split_axis=0, concat_axis=0, tiled...  21.5 us
    slice x1, local copies, waits for them, and re-layouts, local(): gate_up_weight[span]  16.2 us
  transfers between devices with their start and end apart: 9, of which 5 were waited for; matrix products, arithmetic and copies ran while one was open for 30% of the time, Pallas kernels for 0%

profile of v8, /device:TPU:0, one launch (start us, length us, event | category | flops | bytes accessed | tf_op | source)
XLA Modules:
  0.0 458.0 jit_solution(16420601011597710427)
XLA Ops:
  6.5 0.7 broadcast_multiply_fusion
  7.3 0.8 copy.68
  8.3 1.2 fusion.23
  10.6 4.3 scatter_custom_fusion
  15.2 0.9 pad_maximum_fusion.1
  16.2 122.6 %all-gather.2.cloned.1.call-done = bf16[4352,2048]{1,0:T(8,128)(2,1)} async-done(((bf16[136,2048]{1,0:T(8,128)(2,1)}), bf16[4352,2048]{1,0:T(8,128)(2,1)}) %all-gather.2.cloned.1.call-update) | async-done | bytes 17825808 | tf_op jit(solution)/shard_map/all_gather | solution.py:57
  138.8 1.3 slice.123
  140.1 0.6 copy.108
  141.2 19.2 %gather_fusion = bf16[1280,2048]{1,0:T(8,128)(2,1)} fusion(bf16[4352,2048]{1,0:T(8,128)(2,1)} %all-gather.2.cloned.1.call-done, s32[2048]{0:T(1024)S(1)} %pad_clamp_fusion.3), kind=kCustom, calls=%fused_computation | custom fusion | bytes 10490880 | tf_op jit(solution)/shard_map/jit(_take)/gather | solution.py:72
  160.4 7.8 %fusion.6 = f32[4,320,2,192]{1,3,2,0:T(8,128)S(1)} fusion(bf16[4,320,2048,1]{2,1,3,0:T(8,128)(2,1)} %bitcast.124, bf16[16,2,192,2048]{3,2,1,0:T(8,128)(2,1)} %param.12), kind=kOutput, calls=%fused_computation.12 | convolution fusion | flops 2013265920 | bytes 13500416 | tf_op jit(solution)/shard_map/jrd,jgfd->jrgf/dot_general | solution.py:74
  168.2 5.8 %convolution_convert_fusion.3 = bf16[4,320,2048]{2,1,0:T(8,128)(2,1)} fusion(bf16[16,192,2048]{2,1,0:T(8,128)(2,1)} %param.13, f32[4,320,2,192]{1,3,2,0:T(8,128)S(1)} %fusion.6), kind=kOutput, calls=%fused_computation.21 | convolution fusion | flops 1010728960 | bytes 10354688 | tf_op jit(solution)/shard_map/jrf,jfd->jrd/dot_general | solution.py:78
  174.0 0.5 reduce-scatter.7.cloned.1.call-start
  174.5 16.2 %fusion.49 = (bf16[4,2,192,2048]{3,2,1,0:T(8,128)(2,1)}, bf16[4,2,192,2048]{3,2,1,0:T(8,128)(2,1)}, bf16[4,2,192,2048]{3,2,1,0:T(8,128)(2,1)}) fusion(bf16[16,2,192,2048]{3,2,1,0:T(8,128)(2,1)} %param.12), kind=kLoop, calls=%fused_computation.91 | loop fusion | bytes 37748736 | tf_op jit(solution)/shard_map/slice | solution.py:75
  190.9 20.0 %gather_fusion.1 = bf16[1280,2048]{1,0:T(8,128)(2,1)} fusion(bf16[4352,2048]{1,0:T(8,128)(2,1)} %all-gather.2.cloned.1.call-done, s32[2048]{0:T(1024)S(1)} %pad_clamp_fusion.2), kind=kCustom, calls=%fused_computation.1 | custom fusion | bytes 10490880 | tf_op jit(solution)/shard_map/jit(_take)/gather | solution.py:72
  210.9 7.8 %fusion.4 = f32[4,320,2,192]{1,3,0,2:T(8,128)S(1)} fusion(bf16[4,320,2048,1]{2,1,0,3:T(8,128)(2,1)} %bitcast.122, bf16[4,2,192,2048]{3,2,1,0:T(8,128)(2,1)} %get-tuple-element.23), kind=kOutput, calls=%fused_computation.10 | convolution fusion | flops 2013265920 | bytes 13500416 | tf_op jit(solution)/shard_map/jrd,jgfd->jrgf/dot_general | solution.py:74
  218.7 5.8 %convolution_convert_fusion.2 = bf16[4,320,2048]{2,1,0:T(8,128)(2,1)} fusion(bf16[16,192,2048]{2,1,0:T(8,128)(2,1)} %param.13, f32[4,320,2,192]{1,3,0,2:T(8,128)S(1)} %fusion.4), kind=kOutput, calls=%fused_computation.20 | convolution fusion | flops 1010728960 | bytes 10354688 | tf_op jit(solution)/shard_map/jrf,jfd->jrd/dot_general | solution.py:78
  224.5 1.3 copy-done.2
  225.8 1.0 copy.77
  226.8 0.7 copy.78
  227.5 1.8 copy.79
  229.3 4.7 %all-to-all-start = ((bf16[8,40,2048]{2,1,0:T(8,128)(2,1)}), bf16[8,40,2048]{2,1,0:T(8,128)(2,1)S(1)}, u32[]{:S(2)}, u32[]{:S(2)}) async-start(bf16[8,40,2048]{2,1,0:T(8,128)(2,1)} %copy.79), calls=%async_computation.1 | async-start | bytes 2621440 | tf_op jit(solution)/shard_map/all_to_all | solution.py:88
  234.5 20.5 %gather_fusion.2 = bf16[1280,2048]{1,0:T(8,128)(2,1)} fusion(bf16[4352,2048]{1,0:T(8,128)(2,1)} %all-gather.2.cloned.1.call-done, s32[2048]{0:T(1024)S(1)} %pad_clamp_fusion.1), kind=kCustom, calls=%fused_computation.2 | custom fusion | bytes 10490880 | tf_op jit(solution)/shard_map/jit(_take)/gather | solution.py:72
  254.9 7.9 %fusion.2 = f32[4,320,2,192]{1,3,0,2:T(8,128)S(1)} fusion(bf16[4,320,2048,1]{2,1,0,3:T(8,128)(2,1)} %bitcast.123, bf16[4,2,192,2048]{3,2,1,0:T(8,128)(2,1)} %get-tuple-element.25), kind=kOutput, calls=%fused_computation.8 | convolution fusion | flops 2013265920 | bytes 13500416 | tf_op jit(solution)/shard_map/jrd,jgfd->jrgf/dot_general | solution.py:74
  262.9 5.9 %convolution_convert_fusion.1 = bf16[4,320,2048]{2,1,0:T(8,128)(2,1)} fusion(bf16[16,192,2048]{2,1,0:T(8,128)(2,1)} %param.13, f32[4,320,2,192]{1,3,0,2:T(8,128)S(1)} %fusion.2), kind=kOutput, calls=%fused_computation.19 | convolution fusion | flops 1010728960 | bytes 10354688 | tf_op jit(solution)/shard_map/jrf,jfd->jrd/dot_general | solution.py:78
  268.8 9.1 %reduce-scatter.7.cloned.1.call-done = bf16[4,80,2048]{2,1,0:T(8,128)(2,1)} async-done(((bf16[4,320,2048]{2,1,0:T(8,128)(2,1)}), bf16[4,80,2048]{2,1,0:T(8,128)(2,1)}) %reduce-scatter.7.cloned.1.call-update) | async-done | bytes 1310736 | tf_op jit(solution)/shard_map/reduce_scatter | solution.py:84
  277.9 1.3 copy-done.1
  279.2 1.0 copy.83
  280.2 0.7 copy.84
  280.9 1.8 copy.85
  282.7 5.5 %all-to-all-start.1 = ((bf16[8,40,2048]{2,1,0:T(8,128)(2,1)}), bf16[8,40,2048]{2,1,0:T(8,128)(2,1)S(1)}, u32[]{:S(2)}, u32[]{:S(2)}) async-start(bf16[8,40,2048]{2,1,0:T(8,128)(2,1)} %copy.85), calls=%async_computation.3 | async-start | bytes 2621440 | tf_op jit(solution)/shard_map/all_to_all | solution.py:88
  288.6 20.3 %gather_fusion.3 = bf16[1280,2048]{1,0:T(8,128)(2,1)} fusion(bf16[4352,2048]{1,0:T(8,128)(2,1)} %all-gather.2.cloned.1.call-done, s32[2048]{0:T(1024)S(1)} %pad_clamp_fusion), kind=kCustom, calls=%fused_computation.3 | custom fusion | bytes 10490880 | tf_op jit(solution)/shard_map/jit(_take)/gather | solution.py:72
  308.9 7.9 %fusion = f32[4,320,2,192]{1,3,0,2:T(8,128)S(1)} fusion(bf16[4,320,2048,1]{2,1,0,3:T(8,128)(2,1)} %bitcast.121, bf16[4,2,192,2048]{3,2,1,0:T(8,128)(2,1)} %get-tuple-element.24), kind=kOutput, calls=%fused_computation.6 | convolution fusion | flops 2013265920 | bytes 13500416 | tf_op jit(solution)/shard_map/jrd,jgfd->jrgf/dot_general | solution.py:74
  316.8 5.9 %convolution_convert_fusion = bf16[4,320,2048]{2,1,0:T(8,128)(2,1)} fusion(bf16[16,192,2048]{2,1,0:T(8,128)(2,1)} %param.13, f32[4,320,2,192]{1,3,0,2:T(8,128)S(1)} %fusion), kind=kOutput, calls=%fused_computation.18 | convolution fusion | flops 1010728960 | bytes 10354688 | tf_op jit(solution)/shard_map/jrf,jfd->jrd/dot_general | solution.py:78
  322.7 8.9 %reduce-scatter.9.cloned.1.call-done = bf16[4,80,2048]{2,1,0:T(8,128)(2,1)} async-done(((bf16[4,320,2048]{2,1,0:T(8,128)(2,1)}), bf16[4,80,2048]{2,1,0:T(8,128)(2,1)}) %reduce-scatter.9.cloned.1.call-update) | async-done | bytes 1310736 | tf_op jit(solution)/shard_map/reduce_scatter | solution.py:84
  331.7 2.3 copy.89
  334.0 0.7 copy.90
  334.7 1.9 copy.91
  336.6 5.8 %all-to-all-start.2 = ((bf16[8,40,2048]{2,1,0:T(8,128)(2,1)}), bf16[8,40,2048]{2,1,0:T(8,128)(2,1)}, u32[]{:S(2)}, u32[]{:S(2)}) async-start(bf16[8,40,2048]{2,1,0:T(8,128)(2,1)} %copy.91), calls=%async_computation.5 | async-start | bytes 2621440 | tf_op jit(solution)/shard_map/all_to_all | solution.py:88
  342.4 43.2 %reduce-scatter.11.cloned.1.call-done = bf16[4,80,2048]{2,1,0:T(8,128)(2,1)} async-done(((bf16[4,320,2048]{2,1,0:T(8,128)(2,1)}), bf16[4,80,2048]{2,1,0:T(8,128)(2,1)}) %reduce-scatter.11.cloned.1.call-update) | async-done | bytes 1310736 | tf_op jit(solution)/shard_map/reduce_scatter | solution.py:84
  385.6 2.3 copy.95
  388.0 0.7 copy.96
  388.7 1.8 copy.97
  390.5 5.5 %all-to-all-start.3 = ((bf16[8,40,2048]{2,1,0:T(8,128)(2,1)}), bf16[8,40,2048]{2,1,0:T(8,128)(2,1)}, u32[]{:S(2)}, u32[]{:S(2)}) async-start(bf16[8,40,2048]{2,1,0:T(8,128)(2,1)} %copy.97), calls=%async_computation.7 | async-start | bytes 2621440 | tf_op jit(solution)/shard_map/all_to_all | solution.py:88
  396.5 31.9 %all-to-all-done.3 = bf16[8,40,2048]{2,1,0:T(8,128)(2,1)} async-done(((bf16[8,40,2048]{2,1,0:T(8,128)(2,1)}), bf16[8,40,2048]{2,1,0:T(8,128)(2,1)}, u32[]{:S(2)}, u32[]{:S(2)}) %all-to-all-start.3) | async-done | bytes 1310752 | tf_op jit(solution)/shard_map/all_to_all | solution.py:88
  428.3 6.0 %pad_maximum_fusion = bf16[8,160,2048]{2,1,0:T(8,128)(2,1)} fusion(bf16[8,40,2048]{2,1,0:T(8,128)(2,1)} %all-to-all-done.3, bf16[8,40,2048]{2,1,0:T(8,128)(2,1)} %all-to-all-done.2, bf16[8,40,2048]{2,1,0:T(8,128)(2,1)S(1)} %all-to-all-done.1, bf16[8,40,2048]{2,1,0:T(8,128)(2,1)S(1)} %all-to-all-done), kind=kLoop, calls=%fused_computation.14 | loop fusion | flops 20971520 | bytes 10485760 | tf_op jit(solution)/shard_map/concatenate | solution.py:90
  434.4 12.0 %gather_fusion.4 = bf16[1024,2048]{1,0:T(8,128)(2,1)} fusion(bf16[1280,2048]{1,0:T(8,128)(2,1)} %bitcast.120, s32[1024]{0:T(1024)S(1)} %broadcast_clamp_fusion), kind=kCustom, calls=%fused_computation.4 | custom fusion | bytes 8392704 | tf_op jit(solution)/shard_map/jit(_take)/gather | solution.py:91
  446.4 3.5 fusion.8
  449.9 1.1 copy.116
  (67 shorter events, 3.5 us)
Async XLA Ops:
  6.5 8.4 %copy-start = (bf16[128,2048]{1,0:T(8,128)(2,1)S(1)}, bf16[128,2048]{1,0:T(8,128)(2,1)}, u32[]{:S(2)}) copy-start(bf16[128,2048]{1,0:T(8,128)(2,1)} %param.8) | copy-start | bytes 1572868
  6.5 8.5 %copy-start.5 = (f32[2048]{0:T(1024)S(1)}, f32[2048]{0:T(1024)}, u32[]{:S(2)}) copy-start(f32[2048]{0:T(1024)} %param.9) | copy-start | bytes 24580
  6.5 132.2 %all-gather.2.cloned.1.call-start = ((), (), s32[]{:S(2)}) async-start(), calls=%async_computation.8 | async-start | bytes 18382848 | tf_op jit(solution)/shard_map/all_gather | solution.py:57
  16.1 208.4 %reduce-scatter.5.cloned.1.call-start = ((), (), s32[]{:S(2)}) async-start(), calls=%async_computation.9 | async-start | bytes 6553600 | tf_op jit(solution)/shard_map/reduce_scatter | solution.py:84
  174.0 103.9 %reduce-scatter.7.cloned.1.call-start = ((), (), s32[]{:S(2)}) async-start(), calls=%async_computation.10 | async-start | bytes 6553600 | tf_op jit(solution)/shard_map/reduce_scatter | solution.py:84
  224.5 1.3 copy-start.2
  229.3 39.4 %all-to-all-start = ((bf16[8,40,2048]{2,1,0:T(8,128)(2,1)}), bf16[8,40,2048]{2,1,0:T(8,128)(2,1)S(1)}, u32[]{:S(2)}, u32[]{:S(2)}) async-start(bf16[8,40,2048]{2,1,0:T(8,128)(2,1)} %copy.79), calls=%async_computation.1 | async-start | bytes 2621440 | tf_op jit(solution)/shard_map/all_to_all | solution.py:88
  234.1 97.6 %reduce-scatter.9.cloned.1.call-start = ((), (), s32[]{:S(2)}) async-start(), calls=%async_computation.11 | async-start | bytes 6553600 | tf_op jit(solution)/shard_map/reduce_scatter | solution.py:84
  277.8 1.3 copy-start.1
  282.7 40.0 %all-to-all-start.1 = ((bf16[8,40,2048]{2,1,0:T(8,128)(2,1)}), bf16[8,40,2048]{2,1,0:T(8,128)(2,1)S(1)}, u32[]{:S(2)}, u32[]{:S(2)}) async-start(bf16[8,40,2048]{2,1,0:T(8,128)(2,1)} %copy.85), calls=%async_computation.3 | async-start | bytes 2621440 | tf_op jit(solution)/shard_map/all_to_all | solution.py:88
  288.2 97.4 %reduce-scatter.11.cloned.1.call-start = ((), (), s32[]{:S(2)}) async-start(), calls=%async_computation.12 | async-start | bytes 6553600 | tf_op jit(solution)/shard_map/reduce_scatter | solution.py:84
  336.6 53.9 %all-to-all-start.2 = ((bf16[8,40,2048]{2,1,0:T(8,128)(2,1)}), bf16[8,40,2048]{2,1,0:T(8,128)(2,1)}, u32[]{:S(2)}, u32[]{:S(2)}) async-start(bf16[8,40,2048]{2,1,0:T(8,128)(2,1)} %copy.91), calls=%async_computation.5 | async-start | bytes 2621440 | tf_op jit(solution)/shard_map/all_to_all | solution.py:88
  387.9 8.1 %copy-start.4 = (f32[128,8]{0,1:T(8,128)S(1)}, f32[128,8]{0,1:T(8,128)}, u32[]{:S(2)}) copy-start(f32[128,8]{0,1:T(8,128)} %param.11) | copy-start | bytes 12292
  388.0 8.3 %copy-start.3 = (s32[128,8]{0,1:T(8,128)S(1)}, s32[128,8]{0,1:T(8,128)}, u32[]{:S(2)}) copy-start(s32[128,8]{0,1:T(8,128)} %param.10) | copy-start | bytes 12292
  390.5 37.9 %all-to-all-start.3 = ((bf16[8,40,2048]{2,1,0:T(8,128)(2,1)}), bf16[8,40,2048]{2,1,0:T(8,128)(2,1)}, u32[]{:S(2)}, u32[]{:S(2)}) async-start(bf16[8,40,2048]{2,1,0:T(8,128)(2,1)} %copy.97), calls=%async_computation.7 | async-start | bytes 2621440 | tf_op jit(solution)/shard_map/all_to_all | solution.py:88
Sparse Core Ops, SparseCore 0:
  16.2 122.5 all-gather.1
  174.1 49.5 reduce-scatter.4
  226.4 51.3 reduce-scatter.6
  280.2 51.3 reduce-scatter.8
  334.2 51.3 reduce-scatter.10

commit v9 on v8

--- a/solution.py
+++ b/solution.py
@@ -54,7 +54,8 @@
     table_rows = jnp.zeros((extra * features,), jnp.bfloat16)
     table_rows = table_rows.at[: experts * CAP].set(source.astype(jnp.bfloat16))
     packed = jnp.concatenate([normed, table_rows.reshape(extra, features)], axis=0)
-    every = lax.all_gather(packed, ALL, axis=0, tiled=True)
+    every = lax.all_gather(packed, "tok", axis=0, tiled=True)
+    every = lax.all_gather(every, ("row", "col"), axis=0, tiled=True)
 
     tables = every.reshape(devices, stride, features)[:, count:, :].reshape(devices, -1)
     tables = lax.dynamic_slice_in_dim(

time: 467 us -> 718 us (1.54)
  waiting for transfers between devices: 216 us -> 466 us
    all_gather x1 -> x2, waiting for transfers between devices: 123 us -> 370 us  [the longest x1 344 us: local(): every = lax.all_gather(every, ('row', 'col'), axis=0, tiled=True)]
  transfers between devices with their start and end apart: 9 -> 10, of which waited for: 5 -> 7; matrix products, arithmetic and copies ran while one was open for 30% -> 19% of each run, Pallas kernels for 0% -> 0%
where the time goes in v9:
time: 718 us; the launch traced here: 709 us
  waiting for transfers between devices  466 us (65%)
  local copies, waits for them, and re-layouts  137 us (19%)
  matrix products  58.4 us (8%)
  starting transfers between devices  23.3 us (3%)
  between operations  14.3 us (2%)
  other arithmetic  9.89 us (1%)
    all_gather x1, waiting for transfers between devices, local(): every = lax.all_gather(every, ('row', 'col'), axis=0, tiled=True)  344 us
    gather x4, local copies, waits for them, and re-layouts, local(): picked = jnp.take(every, rows[span].reshape(-1), axis=0, mode='clip')  79.9 us
    reduce_scatter x4, waiting for transfers between devices, local(): lax.psum_scatter(partial, 'tok', scatter_dimension=1, tiled=True)  63.9 us
    all_to_all x4, waiting for transfers between devices, local(): lax.all_to_all(summed, ('row', 'col'), split_axis=0, concat_axis=0, tiled...  31.9 us
    dot_general x4, matrix products, local(): jnp.einsum('jrd,jgfd->jrgf', picked, gate_up_weight[span], preferred_elem...  31.5 us
    all_gather x1, waiting for transfers between devices, local(): every = lax.all_gather(packed, 'tok', axis=0, tiled=True)  26.1 us
    dot_general x4, matrix products, local(): jnp.einsum('jrf,jfd->jrd', hidden, down_weight[span], preferred_element_t...  23.4 us
    all_to_all x4, starting transfers between devices, local(): lax.all_to_all(summed, ('row', 'col'), split_axis=0, concat_axis=0, tiled...  22.3 us
  transfers between devices with their start and end apart: 10, of which 7 were waited for; matrix products, arithmetic and copies ran while one was open for 19% of the time, Pallas kernels for 0%

profile of v9, /device:TPU:0, one launch (start us, length us, event | category | flops | bytes accessed | tf_op | source)
XLA Modules:
  0.0 708.9 jit_solution(1709486326164848802)
XLA Ops:
  6.5 0.7 broadcast_multiply_fusion
  7.3 0.8 copy.68
  8.3 1.2 fusion.23
  10.6 4.3 scatter_custom_fusion
  15.2 0.9 pad_maximum_fusion.1
  16.1 26.1 %all-gather.3.cloned.1.call-done = bf16[544,2048]{1,0:T(8,128)(2,1)} async-done(((bf16[136,2048]{1,0:T(8,128)(2,1)}), bf16[544,2048]{1,0:T(8,128)(2,1)}) %all-gather.3.cloned.1.call-update) | async-done | bytes 2228240 | tf_op jit(solution)/shard_map/all_gather | solution.py:57
  42.4 344.2 %all-gather.5.cloned.1.call-done = bf16[4352,2048]{1,0:T(8,128)(2,1)} async-done(((bf16[544,2048]{1,0:T(8,128)(2,1)}), bf16[4352,2048]{1,0:T(8,128)(2,1)}) %all-gather.5.cloned.1.call-update) | async-done | bytes 17825808 | tf_op jit(solution)/shard_map/all_gather | solution.py:58
  386.6 1.3 slice.123
  389.0 19.2 %gather_fusion = bf16[1280,2048]{1,0:T(8,128)(2,1)} fusion(bf16[4352,2048]{1,0:T(8,128)(2,1)} %all-gather.5.cloned.1.call-done, s32[2048]{0:T(1024)S(1)} %pad_clamp_fusion.3), kind=kCustom, calls=%fused_computation | custom fusion | bytes 10490880 | tf_op jit(solution)/shard_map/jit(_take)/gather | solution.py:73
  408.2 7.8 %fusion.6 = f32[4,320,2,192]{1,3,2,0:T(8,128)S(1)} fusion(bf16[4,320,2048,1]{2,1,3,0:T(8,128)(2,1)} %bitcast.124, bf16[16,2,192,2048]{3,2,1,0:T(8,128)(2,1)} %param.12), kind=kOutput, calls=%fused_computation.12 | convolution fusion | flops 2013265920 | bytes 13500416 | tf_op jit(solution)/shard_map/jrd,jgfd->jrgf/dot_general | solution.py:75
  416.0 5.8 convolution_convert_fusion.3
  422.3 15.6 %fusion.49 = (bf16[4,2,192,2048]{3,2,1,0:T(8,128)(2,1)}, bf16[4,2,192,2048]{3,2,1,0:T(8,128)(2,1)}, bf16[4,2,192,2048]{3,2,1,0:T(8,128)(2,1)}) fusion(bf16[16,2,192,2048]{3,2,1,0:T(8,128)(2,1)} %param.12), kind=kLoop, calls=%fused_computation.91 | loop fusion | bytes 37748736 | tf_op jit(solution)/shard_map/slice | solution.py:76
  438.1 20.0 %gather_fusion.1 = bf16[1280,2048]{1,0:T(8,128)(2,1)} fusion(bf16[4352,2048]{1,0:T(8,128)(2,1)} %all-gather.5.cloned.1.call-done, s32[2048]{0:T(1024)S(1)} %pad_clamp_fusion.2), kind=kCustom, calls=%fused_computation.1 | custom fusion | bytes 10490880 | tf_op jit(solution)/shard_map/jit(_take)/gather | solution.py:73
  458.2 7.9 %fusion.4 = f32[4,320,2,192]{1,3,0,2:T(8,128)S(1)} fusion(bf16[4,320,2048,1]{2,1,0,3:T(8,128)(2,1)} %bitcast.122, bf16[4,2,192,2048]{3,2,1,0:T(8,128)(2,1)} %get-tuple-element.23), kind=kOutput, calls=%fused_computation.10 | convolution fusion | flops 2013265920 | bytes 13500416 | tf_op jit(solution)/shard_map/jrd,jgfd->jrgf/dot_general | solution.py:75
  466.1 5.8 convolution_convert_fusion.2
  471.9 2.7 reduce-scatter.5.cloned.1.call-done
  474.6 1.3 copy-done.2
  475.9 1.0 copy.77
  476.9 0.7 copy.78
  477.6 1.8 copy.79
  479.4 5.5 all-to-all-start
  485.3 20.4 %gather_fusion.2 = bf16[1280,2048]{1,0:T(8,128)(2,1)} fusion(bf16[4352,2048]{1,0:T(8,128)(2,1)} %all-gather.5.cloned.1.call-done, s32[2048]{0:T(1024)S(1)} %pad_clamp_fusion.1), kind=kCustom, calls=%fused_computation.2 | custom fusion | bytes 10490880 | tf_op jit(solution)/shard_map/jit(_take)/gather | solution.py:73
  505.7 7.9 %fusion.2 = f32[4,320,2,192]{1,3,0,2:T(8,128)S(1)} fusion(bf16[4,320,2048,1]{2,1,0,3:T(8,128)(2,1)} %bitcast.123, bf16[4,2,192,2048]{3,2,1,0:T(8,128)(2,1)} %get-tuple-element.25), kind=kOutput, calls=%fused_computation.8 | convolution fusion | flops 2013265920 | bytes 13500416 | tf_op jit(solution)/shard_map/jrd,jgfd->jrgf/dot_general | solution.py:75
  513.6 5.9 convolution_convert_fusion.1
  519.5 9.0 %reduce-scatter.7.cloned.1.call-done = bf16[4,80,2048]{2,1,0:T(8,128)(2,1)} async-done(((bf16[4,320,2048]{2,1,0:T(8,128)(2,1)}), bf16[4,80,2048]{2,1,0:T(8,128)(2,1)}) %reduce-scatter.7.cloned.1.call-update) | async-done | bytes 1310736 | tf_op jit(solution)/shard_map/reduce_scatter | solution.py:85
  528.5 1.3 copy-done.1
  529.8 1.0 copy.83
  530.8 0.7 copy.84
  531.6 1.8 copy.85
  533.4 5.5 all-to-all-start.1
  539.3 20.2 %gather_fusion.3 = bf16[1280,2048]{1,0:T(8,128)(2,1)} fusion(bf16[4352,2048]{1,0:T(8,128)(2,1)} %all-gather.5.cloned.1.call-done, s32[2048]{0:T(1024)S(1)} %pad_clamp_fusion), kind=kCustom, calls=%fused_computation.3 | custom fusion | bytes 10490880 | tf_op jit(solution)/shard_map/jit(_take)/gather | solution.py:73
  559.5 7.9 %fusion = f32[4,320,2,192]{1,3,0,2:T(8,128)S(1)} fusion(bf16[4,320,2048,1]{2,1,0,3:T(8,128)(2,1)} %bitcast.121, bf16[4,2,192,2048]{3,2,1,0:T(8,128)(2,1)} %get-tuple-element.24), kind=kOutput, calls=%fused_computation.6 | convolution fusion | flops 2013265920 | bytes 13500416 | tf_op jit(solution)/shard_map/jrd,jgfd->jrgf/dot_general | solution.py:75
  567.5 5.9 convolution_convert_fusion
  573.4 9.0 %reduce-scatter.9.cloned.1.call-done = bf16[4,80,2048]{2,1,0:T(8,128)(2,1)} async-done(((bf16[4,320,2048]{2,1,0:T(8,128)(2,1)}), bf16[4,80,2048]{2,1,0:T(8,128)(2,1)}) %reduce-scatter.9.cloned.1.call-update) | async-done | bytes 1310736 | tf_op jit(solution)/shard_map/reduce_scatter | solution.py:85
  582.3 2.3 copy.89
  584.7 0.7 copy.90
  585.4 1.9 copy.91
  587.3 5.8 all-to-all-start.2
  593.1 43.2 %reduce-scatter.11.cloned.1.call-done = bf16[4,80,2048]{2,1,0:T(8,128)(2,1)} async-done(((bf16[4,320,2048]{2,1,0:T(8,128)(2,1)}), bf16[4,80,2048]{2,1,0:T(8,128)(2,1)}) %reduce-scatter.11.cloned.1.call-update) | async-done | bytes 1310736 | tf_op jit(solution)/shard_map/reduce_scatter | solution.py:85
  636.3 2.3 copy.95
  638.6 0.7 copy.96
  639.4 1.8 copy.97
  641.1 5.5 all-to-all-start.3
  647.1 31.9 %all-to-all-done.3 = bf16[8,40,2048]{2,1,0:T(8,128)(2,1)} async-done(((bf16[8,40,2048]{2,1,0:T(8,128)(2,1)}), bf16[8,40,2048]{2,1,0:T(8,128)(2,1)}, u32[]{:S(2)}, u32[]{:S(2)}) %all-to-all-start.3) | async-done | bytes 1310752 | tf_op jit(solution)/shard_map/all_to_all | solution.py:89
  679.0 6.0 pad_maximum_fusion
  685.0 12.0 %gather_fusion.4 = bf16[1024,2048]{1,0:T(8,128)(2,1)} fusion(bf16[1280,2048]{1,0:T(8,128)(2,1)} %bitcast.120, s32[1024]{0:T(1024)S(1)} %broadcast_clamp_fusion), kind=kCustom, calls=%fused_computation.4 | custom fusion | bytes 8392704 | tf_op jit(solution)/shard_map/jit(_take)/gather | solution.py:92
  697.0 3.5 fusion.8
  700.6 1.1 copy.116
  (70 shorter events, 4.6 us)
Async XLA Ops:
  6.5 8.4 %copy-start = (bf16[128,2048]{1,0:T(8,128)(2,1)S(1)}, bf16[128,2048]{1,0:T(8,128)(2,1)}, u32[]{:S(2)}) copy-start(bf16[128,2048]{1,0:T(8,128)(2,1)} %param.8) | copy-start | bytes 1572868
  6.5 8.5 %copy-start.5 = (f32[2048]{0:T(1024)S(1)}, f32[2048]{0:T(1024)}, u32[]{:S(2)}) copy-start(f32[2048]{0:T(1024)} %param.9) | copy-start | bytes 24580
  6.5 35.7 %all-gather.3.cloned.1.call-start = ((), (), s32[]{:S(2)}) async-start(), calls=%async_computation.8 | async-start | bytes 2785280 | tf_op jit(solution)/shard_map/all_gather | solution.py:57
  16.1 370.5 %all-gather.5.cloned.1.call-start = ((), (), s32[]{:S(2)}) async-start(), calls=%async_computation.9 | async-start | bytes 20054016 | tf_op jit(solution)/shard_map/all_gather | solution.py:58
  42.3 432.3 %reduce-scatter.5.cloned.1.call-start = ((), (), s32[]{:S(2)}) async-start(), calls=%async_computation.10 | async-start | bytes 6553600 | tf_op jit(solution)/shard_map/reduce_scatter | solution.py:85
  421.8 106.7 %reduce-scatter.7.cloned.1.call-start = ((), (), s32[]{:S(2)}) async-start(), calls=%async_computation.11 | async-start | bytes 6553600 | tf_op jit(solution)/shard_map/reduce_scatter | solution.py:85
  474.6 1.3 copy-start.2
  479.4 40.1 %all-to-all-start = ((bf16[8,40,2048]{2,1,0:T(8,128)(2,1)}), bf16[8,40,2048]{2,1,0:T(8,128)(2,1)S(1)}, u32[]{:S(2)}, u32[]{:S(2)}) async-start(bf16[8,40,2048]{2,1,0:T(8,128)(2,1)} %copy.79), calls=%async_computation.1 | async-start | bytes 2621440 | tf_op jit(solution)/shard_map/all_to_all | solution.py:89
  484.9 97.4 %reduce-scatter.9.cloned.1.call-start = ((), (), s32[]{:S(2)}) async-start(), calls=%async_computation.12 | async-start | bytes 6553600 | tf_op jit(solution)/shard_map/reduce_scatter | solution.py:85
  528.5 1.3 copy-start.1
  533.4 40.0 %all-to-all-start.1 = ((bf16[8,40,2048]{2,1,0:T(8,128)(2,1)}), bf16[8,40,2048]{2,1,0:T(8,128)(2,1)S(1)}, u32[]{:S(2)}, u32[]{:S(2)}) async-start(bf16[8,40,2048]{2,1,0:T(8,128)(2,1)} %copy.85), calls=%async_computation.3 | async-start | bytes 2621440 | tf_op jit(solution)/shard_map/all_to_all | solution.py:89
  538.9 97.4 %reduce-scatter.11.cloned.1.call-start = ((), (), s32[]{:S(2)}) async-start(), calls=%async_computation.13 | async-start | bytes 6553600 | tf_op jit(solution)/shard_map/reduce_scatter | solution.py:85
  587.3 53.9 %all-to-all-start.2 = ((bf16[8,40,2048]{2,1,0:T(8,128)(2,1)}), bf16[8,40,2048]{2,1,0:T(8,128)(2,1)}, u32[]{:S(2)}, u32[]{:S(2)}) async-start(bf16[8,40,2048]{2,1,0:T(8,128)(2,1)} %copy.91), calls=%async_computation.5 | async-start | bytes 2621440 | tf_op jit(solution)/shard_map/all_to_all | solution.py:89
  638.6 8.1 %copy-start.4 = (f32[128,8]{0,1:T(8,128)S(1)}, f32[128,8]{0,1:T(8,128)}, u32[]{:S(2)}) copy-start(f32[128,8]{0,1:T(8,128)} %param.11) | copy-start | bytes 12292
  638.6 8.3 %copy-start.3 = (s32[128,8]{0,1:T(8,128)S(1)}, s32[128,8]{0,1:T(8,128)}, u32[]{:S(2)}) copy-start(s32[128,8]{0,1:T(8,128)} %param.10) | copy-start | bytes 12292
  641.1 37.9 %all-to-all-start.3 = ((bf16[8,40,2048]{2,1,0:T(8,128)(2,1)}), bf16[8,40,2048]{2,1,0:T(8,128)(2,1)}, u32[]{:S(2)}, u32[]{:S(2)}) async-start(bf16[8,40,2048]{2,1,0:T(8,128)(2,1)} %copy.97), calls=%async_computation.7 | async-start | bytes 2621440 | tf_op jit(solution)/shard_map/all_to_all | solution.py:89
Sparse Core Ops, SparseCore 0:
  16.2 26.0 all-gather.2
  43.8 342.7 all-gather.4
  421.9 52.6 reduce-scatter.4
  477.1 51.3 reduce-scatter.6
  530.9 51.3 reduce-scatter.8
  584.9 51.3 reduce-scatter.10

commit v10 on v8

--- a/solution.py
+++ b/solution.py
@@ -48,15 +48,19 @@
     token_ids = jnp.arange(count * chosen, dtype=jnp.int32) // chosen
     source = jnp.full((experts * CAP,), count, jnp.int32).at[target].set(token_ids)
 
-    extra = -(-(experts * CAP) // features)
+    half = features // 2
+    extra = -(-(experts * CAP) // half)
     extra = -(-extra // 8) * 8
     stride = count + extra
-    table_rows = jnp.zeros((extra * features,), jnp.bfloat16)
+    table_rows = jnp.zeros((extra * half,), jnp.bfloat16)
     table_rows = table_rows.at[: experts * CAP].set(source.astype(jnp.bfloat16))
-    packed = jnp.concatenate([normed, table_rows.reshape(extra, features)], axis=0)
+    packed = jnp.concatenate([normed[:, :half], table_rows.reshape(extra, half)], axis=0)
     every = lax.all_gather(packed, ALL, axis=0, tiled=True)
+    later = jnp.concatenate([normed[:, half:], jnp.zeros((extra, half), jnp.bfloat16)], axis=0)
+    later, _ = lax.optimization_barrier((later, every))
+    every_later = lax.all_gather(later, ALL, axis=0, tiled=True)
 
-    tables = every.reshape(devices, stride, features)[:, count:, :].reshape(devices, -1)
+    tables = every.reshape(devices, stride, half)[:, count:, :].reshape(devices, -1)
     tables = lax.dynamic_slice_in_dim(
         tables[:, : experts * CAP], owner * holding * CAP, holding * CAP, axis=1
     ).astype(jnp.int32)
@@ -69,11 +73,16 @@
     sums = []
     for piece in range(pieces):
         span = slice(piece * width, (piece + 1) * width)
-        picked = jnp.take(every, rows[span].reshape(-1), axis=0, mode="clip")
-        picked = picked.reshape(width, tok_count * owners * CAP, features)
-        both = jnp.einsum(
-            "jrd,jgfd->jrgf", picked, gate_up_weight[span], preferred_element_type=jnp.float32
-        )
+        both = 0
+        for part, gathered in ((slice(0, half), every), (slice(half, features), every_later)):
+            picked = jnp.take(gathered, rows[span].reshape(-1), axis=0, mode="clip")
+            picked = picked.reshape(width, tok_count * owners * CAP, half)
+            both = both + jnp.einsum(
+                "jrd,jgfd->jrgf",
+                picked,
+                gate_up_weight[span][..., part],
+                preferred_element_type=jnp.float32,
+            )
         hidden = (jax.nn.silu(both[:, :, 0, :]) * both[:, :, 1, :]).astype(jnp.bfloat16)
         partial = jnp.einsum(
             "jrf,jfd->jrd", hidden, down_weight[span], preferred_element_type=jnp.float32

time: 467 us -> 493 us (1.056); the launches traced: 458 us -> 489 us
  waiting for transfers between devices: 216 us -> 239 us
  local copies, waits for them, and re-layouts: 138 us -> 149 us
    all_gather x0 -> x1, waiting for transfers between devices: none -> 68.2 us  [local(): every_later = lax.all_gather(later, ALL, axis=0, tiled=True)]
    all_gather x1, waiting for transfers between devices: 123 us -> 81.6 us  [local(): every = lax.all_gather(packed, ALL, axis=0, tiled=True)]
    gather x4 -> x8, local copies, waits for them, and re-layouts: 80 us -> 93.1 us  [local(): picked = jnp.take(gathered, rows[span].reshape(-1), axis=0, mode='clip')]
    dot_general x4 -> x8, matrix products: 31.4 us -> 27.5 us  [local(): jnp.einsum('jrd,jgfd->jrgf', picked, gate_up_weight[span][..., part], pre...]
    slice x7 -> x8, local copies, waits for them, and re-layouts: 17.7 us -> 15 us  [the longest x1 13.8 us: local(): gate_up_weight[span][..., part]]
  transfers between devices with their start and end apart: 9 -> 10, of which waited for: 5 -> 7; matrix products, arithmetic and copies ran while one was open for 30% -> 31% of each run, Pallas kernels for 0% -> 0%
where the time goes in v10:
time: 493 us; the launch traced here: 489 us
  waiting for transfers between devices  239 us (48%)
  local copies, waits for them, and re-layouts  149 us (30%)
  matrix products  54.5 us (11%)
  starting transfers between devices  23.1 us (5%)
  between operations  14.2 us (3%)
  other arithmetic  9.74 us (2%)
    gather x8, local copies, waits for them, and re-layouts, local(): picked = jnp.take(gathered, rows[span].reshape(-1), axis=0, mode='clip')  93.1 us
    all_gather x1, waiting for transfers between devices, local(): every = lax.all_gather(packed, ALL, axis=0, tiled=True)  81.6 us
    all_gather x1, waiting for transfers between devices, local(): every_later = lax.all_gather(later, ALL, axis=0, tiled=True)  68.2 us
    reduce_scatter x4, waiting for transfers between devices, local(): lax.psum_scatter(partial, 'tok', scatter_dimension=1, tiled=True)  57.5 us
    all_to_all x4, waiting for transfers between devices, local(): lax.all_to_all(summed, ('row', 'col'), split_axis=0, concat_axis=0, tiled...  31.9 us
    dot_general x8, matrix products, local(): jnp.einsum('jrd,jgfd->jrgf', picked, gate_up_weight[span][..., part], pre...  27.5 us
    dot_general x4, matrix products, local(): jnp.einsum('jrf,jfd->jrd', hidden, down_weight[span], preferred_element_t...  23.5 us
    all_to_all x4, starting transfers between devices, local(): lax.all_to_all(summed, ('row', 'col'), split_axis=0, concat_axis=0, tiled...  22.3 us
  transfers between devices with their start and end apart: 10, of which 7 were waited for; matrix products, arithmetic and copies ran while one was open for 31% of the time, Pallas kernels for 0%

profile of v10, /device:TPU:0, one launch (start us, length us, event | category | flops | bytes accessed | tf_op | source)
XLA Modules:
  0.0 489.4 jit_solution(1160113582049942953)
XLA Ops:
  8.3 1.2 fusion.43
  10.6 4.3 scatter_custom_fusion
  16.8 81.6 %all-gather.3.cloned.1.call-done = bf16[4352,1024]{1,0:T(8,128)(2,1)} async-done(((bf16[136,1024]{1,0:T(8,128)(2,1)}), bf16[4352,1024]{1,0:T(8,128)(2,1)}) %all-gather.3.cloned.1.call-update) | async-done | bytes 8912912 | tf_op jit(solution)/shard_map/all_gather | solution.py:58
  98.7 1.1 slice.176
  100.6 10.7 %gather_fusion = bf16[1280,1024]{1,0:T(8,128)(2,1)S(1)} fusion(bf16[4352,1024]{1,0:T(8,128)(2,1)} %all-gather.3.cloned.1.call-done, s32[2048]{0:T(1024)S(1)} %pad_clamp_fusion.3), kind=kCustom, calls=%fused_computation | custom fusion | bytes 5248000 | tf_op jit(solution)/shard_map/jit(_take)/gather | solution.py:78
  111.2 68.2 %all-gather.5.cloned.1.call-done = bf16[4352,1024]{1,0:T(8,128)(2,1)} async-done(((bf16[136,1024]{1,0:T(8,128)(2,1)}), bf16[4352,1024]{1,0:T(8,128)(2,1)}) %all-gather.5.cloned.1.call-update) | async-done | bytes 8912912 | tf_op jit(solution)/shard_map/all_gather | solution.py:61
  179.5 11.4 %gather_fusion.1 = bf16[1280,1024]{1,0:T(8,128)(2,1)} fusion(bf16[4352,1024]{1,0:T(8,128)(2,1)} %all-gather.5.cloned.1.call-done, s32[2048]{0:T(1024)S(1)} %pad_clamp_fusion.3), kind=kCustom, calls=%fused_computation.1 | custom fusion | bytes 5248000 | tf_op jit(solution)/shard_map/jit(_take)/gather | solution.py:78
  190.9 4.5 fusion.18
  195.3 3.8 fusion.23
  199.1 5.9 %convolution_convert_fusion.3 = bf16[4,320,2048]{2,1,0:T(8,128)(2,1)} fusion(bf16[16,192,2048]{2,1,0:T(8,128)(2,1)} %param.13, f32[4,320,2,192]{1,3,2,0:T(8,128)S(1)} %fusion.23), kind=kOutput, calls=%fused_computation.17 | convolution fusion | flops 1010728960 | bytes 10354688 | tf_op jit(solution)/shard_map/jrf,jfd->jrd/dot_general | solution.py:87
  205.3 13.8 %fusion.69 = (bf16[4,2,192,1024]{3,2,1,0:T(8,128)(2,1)S(1)}, bf16[4,2,192,1024]{3,2,1,0:T(8,128)(2,1)}, bf16[4,2,192,1024]{3,2,1,0:T(8,128)(2,1)}, bf16[4,2,192,...) fusion(bf16[16,2,192,2048]{3,2,1,0:T(8,128)(2,1)} %param.12), kind=kLoop, calls=%fused_computation.107 | loop fusion | bytes 37748736 | tf_op jit(solution)/shard_map/slice | solution.py:83
  219.3 11.4 %gather_fusion.2 = bf16[1280,1024]{1,0:T(8,128)(2,1)} fusion(bf16[4352,1024]{1,0:T(8,128)(2,1)} %all-gather.3.cloned.1.call-done, s32[2048]{0:T(1024)S(1)} %pad_clamp_fusion.2), kind=kCustom, calls=%fused_computation.2 | custom fusion | bytes 5248000 | tf_op jit(solution)/shard_map/jit(_take)/gather | solution.py:78
  230.7 11.7 %gather_fusion.3 = bf16[1280,1024]{1,0:T(8,128)(2,1)} fusion(bf16[4352,1024]{1,0:T(8,128)(2,1)} %all-gather.5.cloned.1.call-done, s32[2048]{0:T(1024)S(1)} %pad_clamp_fusion.2), kind=kCustom, calls=%fused_computation.3 | custom fusion | bytes 5248000 | tf_op jit(solution)/shard_map/jit(_take)/gather | solution.py:78
  242.4 4.6 fusion.10
  247.0 1.8 fusion.26
  248.9 5.9 %convolution_convert_fusion.2 = bf16[4,320,2048]{2,1,0:T(8,128)(2,1)} fusion(bf16[16,192,2048]{2,1,0:T(8,128)(2,1)} %param.13, f32[4,320,2,192]{1,3,0,2:T(8,128)S(1)} %fusion.26), kind=kOutput, calls=%fused_computation.16 | convolution fusion | flops 1010728960 | bytes 10354688 | tf_op jit(solution)/shard_map/jrf,jfd->jrd/dot_general | solution.py:87
  255.2 1.3 copy-done.7
  256.5 1.0 copy.77
  258.2 1.8 copy.79
  260.0 5.5 %all-to-all-start = ((bf16[8,40,2048]{2,1,0:T(8,128)(2,1)}), bf16[8,40,2048]{2,1,0:T(8,128)(2,1)S(1)}, u32[]{:S(2)}, u32[]{:S(2)}) async-start(bf16[8,40,2048]{2,1,0:T(8,128)(2,1)} %copy.79), calls=%async_computation.1 | async-start | bytes 2621440 | tf_op jit(solution)/shard_map/all_to_all | solution.py:97
  265.8 12.7 %gather_fusion.4 = bf16[1280,1024]{1,0:T(8,128)(2,1)} fusion(bf16[4352,1024]{1,0:T(8,128)(2,1)} %all-gather.3.cloned.1.call-done, s32[2048]{0:T(1024)S(1)} %pad_clamp_fusion.1), kind=kCustom, calls=%fused_computation.4 | custom fusion | bytes 5248000 | tf_op jit(solution)/shard_map/jit(_take)/gather | solution.py:78
  278.5 11.4 %gather_fusion.5 = bf16[1280,1024]{1,0:T(8,128)(2,1)} fusion(bf16[4352,1024]{1,0:T(8,128)(2,1)} %all-gather.5.cloned.1.call-done, s32[2048]{0:T(1024)S(1)} %pad_clamp_fusion.1), kind=kCustom, calls=%fused_computation.5 | custom fusion | bytes 5248000 | tf_op jit(solution)/shard_map/jit(_take)/gather | solution.py:78
  289.9 4.6 fusion.6
  294.5 1.8 fusion.29
  296.3 5.9 %convolution_convert_fusion.1 = bf16[4,320,2048]{2,1,0:T(8,128)(2,1)} fusion(bf16[16,192,2048]{2,1,0:T(8,128)(2,1)} %param.13, f32[4,320,2,192]{1,3,0,2:T(8,128)S(1)} %fusion.29), kind=kOutput, calls=%fused_computation.15 | convolution fusion | flops 1010728960 | bytes 10354688 | tf_op jit(solution)/shard_map/jrf,jfd->jrd/dot_general | solution.py:87
  302.2 6.9 %reduce-scatter.7.cloned.1.call-done = bf16[4,80,2048]{2,1,0:T(8,128)(2,1)} async-done(((bf16[4,320,2048]{2,1,0:T(8,128)(2,1)}), bf16[4,80,2048]{2,1,0:T(8,128)(2,1)}) %reduce-scatter.7.cloned.1.call-update) | async-done | bytes 1310736 | tf_op jit(solution)/shard_map/reduce_scatter | solution.py:93
  309.2 1.3 copy-done.6
  310.5 1.0 copy.83
  312.2 1.8 copy.85
  314.0 5.5 %all-to-all-start.1 = ((bf16[8,40,2048]{2,1,0:T(8,128)(2,1)}), bf16[8,40,2048]{2,1,0:T(8,128)(2,1)S(1)}, u32[]{:S(2)}, u32[]{:S(2)}) async-start(bf16[8,40,2048]{2,1,0:T(8,128)(2,1)} %copy.85), calls=%async_computation.3 | async-start | bytes 2621440 | tf_op jit(solution)/shard_map/all_to_all | solution.py:97
  320.0 12.4 %gather_fusion.6 = bf16[1280,1024]{1,0:T(8,128)(2,1)} fusion(bf16[4352,1024]{1,0:T(8,128)(2,1)} %all-gather.3.cloned.1.call-done, s32[2048]{0:T(1024)S(1)} %pad_clamp_fusion), kind=kCustom, calls=%fused_computation.6 | custom fusion | bytes 5248000 | tf_op jit(solution)/shard_map/jit(_take)/gather | solution.py:78
  332.4 11.4 %gather_fusion.7 = bf16[1280,1024]{1,0:T(8,128)(2,1)} fusion(bf16[4352,1024]{1,0:T(8,128)(2,1)} %all-gather.5.cloned.1.call-done, s32[2048]{0:T(1024)S(1)} %pad_clamp_fusion), kind=kCustom, calls=%fused_computation.7 | custom fusion | bytes 5248000 | tf_op jit(solution)/shard_map/jit(_take)/gather | solution.py:78
  343.7 4.6 fusion.2
  348.4 1.8 fusion.32
  350.2 5.8 %convolution_convert_fusion = bf16[4,320,2048]{2,1,0:T(8,128)(2,1)} fusion(bf16[16,192,2048]{2,1,0:T(8,128)(2,1)} %param.13, f32[4,320,2,192]{1,3,0,2:T(8,128)S(1)} %fusion.32), kind=kOutput, calls=%fused_computation.14 | convolution fusion | flops 1010728960 | bytes 10354688 | tf_op jit(solution)/shard_map/jrf,jfd->jrd/dot_general | solution.py:87
  356.0 7.0 %reduce-scatter.9.cloned.1.call-done = bf16[4,80,2048]{2,1,0:T(8,128)(2,1)} async-done(((bf16[4,320,2048]{2,1,0:T(8,128)(2,1)}), bf16[4,80,2048]{2,1,0:T(8,128)(2,1)}) %reduce-scatter.9.cloned.1.call-update) | async-done | bytes 1310736 | tf_op jit(solution)/shard_map/reduce_scatter | solution.py:93
  363.0 2.3 copy.89
  366.1 1.9 copy.91
  367.9 5.8 %all-to-all-start.2 = ((bf16[8,40,2048]{2,1,0:T(8,128)(2,1)}), bf16[8,40,2048]{2,1,0:T(8,128)(2,1)}, u32[]{:S(2)}, u32[]{:S(2)}) async-start(bf16[8,40,2048]{2,1,0:T(8,128)(2,1)} %copy.91), calls=%async_computation.5 | async-start | bytes 2621440 | tf_op jit(solution)/shard_map/all_to_all | solution.py:97
  373.7 43.2 %reduce-scatter.11.cloned.1.call-done = bf16[4,80,2048]{2,1,0:T(8,128)(2,1)} async-done(((bf16[4,320,2048]{2,1,0:T(8,128)(2,1)}), bf16[4,80,2048]{2,1,0:T(8,128)(2,1)}) %reduce-scatter.11.cloned.1.call-update) | async-done | bytes 1310736 | tf_op jit(solution)/shard_map/reduce_scatter | solution.py:93
  416.9 2.3 copy.95
  420.0 1.8 copy.97
  421.8 5.5 %all-to-all-start.3 = ((bf16[8,40,2048]{2,1,0:T(8,128)(2,1)}), bf16[8,40,2048]{2,1,0:T(8,128)(2,1)}, u32[]{:S(2)}, u32[]{:S(2)}) async-start(bf16[8,40,2048]{2,1,0:T(8,128)(2,1)} %copy.97), calls=%async_computation.7 | async-start | bytes 2621440 | tf_op jit(solution)/shard_map/all_to_all | solution.py:97
  427.8 31.9 %all-to-all-done.3 = bf16[8,40,2048]{2,1,0:T(8,128)(2,1)} async-done(((bf16[8,40,2048]{2,1,0:T(8,128)(2,1)}), bf16[8,40,2048]{2,1,0:T(8,128)(2,1)}, u32[]{:S(2)}, u32[]{:S(2)}) %all-to-all-start.3) | async-done | bytes 1310752 | tf_op jit(solution)/shard_map/all_to_all | solution.py:97
  459.7 6.0 %pad_maximum_fusion = bf16[8,160,2048]{2,1,0:T(8,128)(2,1)} fusion(bf16[8,40,2048]{2,1,0:T(8,128)(2,1)} %all-to-all-done.3, bf16[8,40,2048]{2,1,0:T(8,128)(2,1)} %all-to-all-done.2, bf16[8,40,2048]{2,1,0:T(8,128)(2,1)S(1)} %all-to-all-done.1, bf16[8,40,2048]{2,1,0:T(8,128)(2,1)S(1)} %all-to-all-done), kind=kLoop, calls=%fused_computation.10 | loop fusion | flops 20971520 | bytes 10485760 | tf_op jit(solution)/shard_map/concatenate | solution.py:99
  465.7 12.0 %gather_fusion.8 = bf16[1024,2048]{1,0:T(8,128)(2,1)} fusion(bf16[1280,2048]{1,0:T(8,128)(2,1)} %bitcast.138, s32[1024]{0:T(1024)S(1)} %broadcast_clamp_fusion), kind=kCustom, calls=%fused_computation.8 | custom fusion | bytes 8392704 | tf_op jit(solution)/shard_map/jit(_take)/gather | solution.py:100
  477.7 3.5 fusion
  481.2 1.1 copy.135
  (90 shorter events, 10.4 us)
Async XLA Ops:
  6.5 8.4 %copy-start.5 = (bf16[128,2048]{1,0:T(8,128)(2,1)S(1)}, bf16[128,2048]{1,0:T(8,128)(2,1)}, u32[]{:S(2)}) copy-start(bf16[128,2048]{1,0:T(8,128)(2,1)} %param.8) | copy-start | bytes 1572868
  6.5 8.4 %copy-start.10 = (f32[2048]{0:T(1024)S(1)}, f32[2048]{0:T(1024)}, u32[]{:S(2)}) copy-start(f32[2048]{0:T(1024)} %param.9) | copy-start | bytes 24580
  6.5 91.9 %all-gather.3.cloned.1.call-start = ((), (), s32[]{:S(2)}) async-start(), calls=%async_computation.8 | async-start | bytes 9191424 | tf_op jit(solution)/shard_map/all_gather | solution.py:58
  16.0 163.5 %all-gather.5.cloned.1.call-start = ((), (), s32[]{:S(2)}) async-start(), calls=%async_computation.9 | async-start | bytes 9191424 | tf_op jit(solution)/shard_map/all_gather | solution.py:61
  98.4 156.8 %reduce-scatter.5.cloned.1.call-start = ((), (), s32[]{:S(2)}) async-start(), calls=%async_computation.10 | async-start | bytes 6553600 | tf_op jit(solution)/shard_map/reduce_scatter | solution.py:93
  205.0 104.1 %reduce-scatter.7.cloned.1.call-start = ((), (), s32[]{:S(2)}) async-start(), calls=%async_computation.11 | async-start | bytes 6553600 | tf_op jit(solution)/shard_map/reduce_scatter | solution.py:93
  242.4 4.6 copy-start.3
  255.2 1.3 copy-start.7
  260.0 42.2 %all-to-all-start = ((bf16[8,40,2048]{2,1,0:T(8,128)(2,1)}), bf16[8,40,2048]{2,1,0:T(8,128)(2,1)S(1)}, u32[]{:S(2)}, u32[]{:S(2)}) async-start(bf16[8,40,2048]{2,1,0:T(8,128)(2,1)} %copy.79), calls=%async_computation.1 | async-start | bytes 2621440 | tf_op jit(solution)/shard_map/all_to_all | solution.py:97
  265.5 97.4 %reduce-scatter.9.cloned.1.call-start = ((), (), s32[]{:S(2)}) async-start(), calls=%async_computation.12 | async-start | bytes 6553600 | tf_op jit(solution)/shard_map/reduce_scatter | solution.py:93
  289.9 4.6 copy-start.1
  289.9 4.6 copy-start.4
  309.2 1.3 copy-start.6
  314.0 42.0 %all-to-all-start.1 = ((bf16[8,40,2048]{2,1,0:T(8,128)(2,1)}), bf16[8,40,2048]{2,1,0:T(8,128)(2,1)S(1)}, u32[]{:S(2)}, u32[]{:S(2)}) async-start(bf16[8,40,2048]{2,1,0:T(8,128)(2,1)} %copy.85), calls=%async_computation.3 | async-start | bytes 2621440 | tf_op jit(solution)/shard_map/all_to_all | solution.py:97
  319.5 97.4 %reduce-scatter.11.cloned.1.call-start = ((), (), s32[]{:S(2)}) async-start(), calls=%async_computation.13 | async-start | bytes 6553600 | tf_op jit(solution)/shard_map/reduce_scatter | solution.py:93
  343.7 4.6 copy-start
  343.7 4.6 copy-start.2
  367.9 53.9 %all-to-all-start.2 = ((bf16[8,40,2048]{2,1,0:T(8,128)(2,1)}), bf16[8,40,2048]{2,1,0:T(8,128)(2,1)}, u32[]{:S(2)}, u32[]{:S(2)}) async-start(bf16[8,40,2048]{2,1,0:T(8,128)(2,1)} %copy.91), calls=%async_computation.5 | async-start | bytes 2621440 | tf_op jit(solution)/shard_map/all_to_all | solution.py:97
  420.0 7.4 %copy-start.9 = (f32[128,8]{0,1:T(8,128)S(1)}, f32[128,8]{0,1:T(8,128)}, u32[]{:S(2)}) copy-start(f32[128,8]{0,1:T(8,128)} %param.11) | copy-start | bytes 12292
  420.0 7.6 %copy-start.8 = (s32[128,8]{0,1:T(8,128)S(1)}, s32[128,8]{0,1:T(8,128)}, u32[]{:S(2)}) copy-start(s32[128,8]{0,1:T(8,128)} %param.10) | copy-start | bytes 12292
  421.8 37.8 %all-to-all-start.3 = ((bf16[8,40,2048]{2,1,0:T(8,128)(2,1)}), bf16[8,40,2048]{2,1,0:T(8,128)(2,1)}, u32[]{:S(2)}, u32[]{:S(2)}) async-start(bf16[8,40,2048]{2,1,0:T(8,128)(2,1)} %copy.97), calls=%async_computation.7 | async-start | bytes 2621440 | tf_op jit(solution)/shard_map/all_to_all | solution.py:97
Sparse Core Ops, SparseCore 0:
  16.1 82.2 all-gather.2
  101.3 78.1 all-gather.4
  205.1 49.9 reduce-scatter.4
  257.7 51.3 reduce-scatter.6
  311.5 51.3 reduce-scatter.8
  365.5 51.3 reduce-scatter.10

commit v11 on v8

--- a/solution.py
+++ b/solution.py
@@ -49,14 +49,15 @@
     source = jnp.full((experts * CAP,), count, jnp.int32).at[target].set(token_ids)
 
     extra = -(-(experts * CAP) // features)
-    extra = -(-extra // 8) * 8
     stride = count + extra
     table_rows = jnp.zeros((extra * features,), jnp.bfloat16)
     table_rows = table_rows.at[: experts * CAP].set(source.astype(jnp.bfloat16))
     packed = jnp.concatenate([normed, table_rows.reshape(extra, features)], axis=0)
     every = lax.all_gather(packed, ALL, axis=0, tiled=True)
 
-    tables = every.reshape(devices, stride, features)[:, count:, :].reshape(devices, -1)
+    table_at = jnp.arange(devices, dtype=jnp.int32)[:, None] * stride + count
+    table_at = (table_at + jnp.arange(extra, dtype=jnp.int32)[None, :]).reshape(-1)
+    tables = jnp.take(every, table_at, axis=0).reshape(devices, -1)
     tables = lax.dynamic_slice_in_dim(
         tables[:, : experts * CAP], owner * holding * CAP, holding * CAP, axis=1
     ).astype(jnp.int32)

time: 467 us -> 490 us (1.049); the launches traced: 458 us -> 486 us
  local copies, waits for them, and re-layouts: 138 us -> 165 us
    unnamed x14, local copies, waits for them, and re-layouts: 3.98 us -> 25.6 us
    gather x0 -> x1, local copies, waits for them, and re-layouts: none -> 8.75 us  [local(): tables = jnp.take(every, table_at, axis=0).reshape(devices, -1)]
  transfers between devices with their start and end apart: 9 -> 9, of which waited for: 5 -> 5; matrix products, arithmetic and copies ran while one was open for 30% -> 28% of each run, Pallas kernels for 0% -> 0%
where the time goes in v11:
time: 490 us; the launch traced here: 486 us
  waiting for transfers between devices  216 us (44%)
  local copies, waits for them, and re-layouts  165 us (34%)
  matrix products  58.2 us (12%)
  starting transfers between devices  23.6 us (5%)
  between operations  13.7 us (3%)
  other arithmetic  9.92 us (2%)
    all_gather x1, waiting for transfers between devices, local(): every = lax.all_gather(packed, ALL, axis=0, tiled=True)  122 us
    gather x4, local copies, waits for them, and re-layouts, local(): picked = jnp.take(every, rows[span].reshape(-1), axis=0, mode='clip')  78.3 us
    reduce_scatter x4, waiting for transfers between devices, local(): lax.psum_scatter(partial, 'tok', scatter_dimension=1, tiled=True)  61.9 us
    all_to_all x4, waiting for transfers between devices, local(): lax.all_to_all(summed, ('row', 'col'), split_axis=0, concat_axis=0, tiled...  31.9 us
    dot_general x4, matrix products, local(): jnp.einsum('jrd,jgfd->jrgf', picked, gate_up_weight[span], preferred_elem...  31.4 us
    unnamed x14, local copies, waits for them, and re-layouts  25.6 us
    dot_general x4, matrix products, local(): jnp.einsum('jrf,jfd->jrd', hidden, down_weight[span], preferred_element_t...  23.4 us
    all_to_all x4, starting transfers between devices, local(): lax.all_to_all(summed, ('row', 'col'), split_axis=0, concat_axis=0, tiled...  22.1 us
  transfers between devices with their start and end apart: 9, of which 5 were waited for; matrix products, arithmetic and copies ran while one was open for 28% of the time, Pallas kernels for 0%

profile of v11, /device:TPU:0, one launch (start us, length us, event | category | flops | bytes accessed | tf_op | source)
XLA Modules:
  0.0 486.3 jit_solution(4744925284441448991)
XLA Ops:
  6.5 0.7 broadcast_multiply_fusion
  7.3 0.8 copy.68
  8.3 1.2 fusion.24
  10.6 4.3 scatter_custom_fusion
  15.2 0.9 fusion.36
  16.1 0.6 reduce-scatter.5.cloned.1.call-start
  16.7 122.1 %all-gather.3.cloned.1.call-done = bf16[32,129,2048]{2,1,0:T(8,128)(2,1)} async-done(((bf16[1,129,2048]{2,1,0:T(8,128)(2,1)}), bf16[32,129,2048]{2,1,0:T(8,128)(2,1)}) %all-gather.3.cloned.1.call-update) | async-done | bytes 16908304 | tf_op jit(solution)/shard_map/all_gather | solution.py:56
  138.8 22.2 %reshape.266 = bf16[4128,2048]{1,0:T(8,128)(2,1)} reshape(bf16[32,129,2048]{2,1,0:T(8,128)(2,1)} %all-gather.3.cloned.1.call-done) | data formatting | bytes 33816576
  160.9 8.7 %gather_fusion = bf16[32,2048]{1,0:T(8,128)(2,1)S(1)} fusion(bf16[4128,2048]{1,0:T(8,128)(2,1)} %reshape.266, s32[1024]{0:T(1024)S(1)} %pad_clamp_fusion.4), kind=kCustom, calls=%fused_computation | custom fusion | bytes 262272 | tf_op jit(solution)/shard_map/jit(_take)/gather | solution.py:60
  170.2 18.8 %gather_fusion.1 = bf16[1280,2048]{1,0:T(8,128)(2,1)} fusion(bf16[4128,2048]{1,0:T(8,128)(2,1)} %reshape.266, s32[2048]{0:T(1024)S(1)} %pad_clamp_fusion.3), kind=kCustom, calls=%fused_computation.1 | custom fusion | bytes 10490880 | tf_op jit(solution)/shard_map/jit(_take)/gather | solution.py:73
  189.0 7.8 %fusion.6 = f32[4,320,2,192]{1,3,2,0:T(8,128)S(1)} fusion(bf16[4,320,2048,1]{2,1,3,0:T(8,128)(2,1)} %bitcast.124, bf16[16,2,192,2048]{3,2,1,0:T(8,128)(2,1)} %param.12), kind=kOutput, calls=%fused_computation.13 | convolution fusion | flops 2013265920 | bytes 13500416 | tf_op jit(solution)/shard_map/jrd,jgfd->jrgf/dot_general | solution.py:75
  196.8 5.7 %convolution_convert_fusion.3 = bf16[4,320,2048]{2,1,0:T(8,128)(2,1)} fusion(bf16[16,192,2048]{2,1,0:T(8,128)(2,1)} %param.13, f32[4,320,2,192]{1,3,2,0:T(8,128)S(1)} %fusion.6), kind=kOutput, calls=%fused_computation.22 | convolution fusion | flops 1010728960 | bytes 10354688 | tf_op jit(solution)/shard_map/jrf,jfd->jrd/dot_general | solution.py:79
  202.8 16.2 %fusion.53 = (bf16[4,2,192,2048]{3,2,1,0:T(8,128)(2,1)}, bf16[4,2,192,2048]{3,2,1,0:T(8,128)(2,1)}, bf16[4,2,192,2048]{3,2,1,0:T(8,128)(2,1)}) fusion(bf16[16,2,192,2048]{3,2,1,0:T(8,128)(2,1)} %param.12), kind=kLoop, calls=%fused_computation.101 | loop fusion | bytes 37748736 | tf_op jit(solution)/shard_map/slice | solution.py:76
  219.2 19.7 %gather_fusion.2 = bf16[1280,2048]{1,0:T(8,128)(2,1)} fusion(bf16[4128,2048]{1,0:T(8,128)(2,1)} %reshape.266, s32[2048]{0:T(1024)S(1)} %pad_clamp_fusion.2), kind=kCustom, calls=%fused_computation.2 | custom fusion | bytes 10490880 | tf_op jit(solution)/shard_map/jit(_take)/gather | solution.py:73
  238.9 7.8 %fusion.4 = f32[4,320,2,192]{1,3,0,2:T(8,128)S(1)} fusion(bf16[4,320,2048,1]{2,1,0,3:T(8,128)(2,1)} %bitcast.122, bf16[4,2,192,2048]{3,2,1,0:T(8,128)(2,1)} %get-tuple-element.23), kind=kOutput, calls=%fused_computation.11 | convolution fusion | flops 2013265920 | bytes 13500416 | tf_op jit(solution)/shard_map/jrd,jgfd->jrgf/dot_general | solution.py:75
  246.7 5.8 %convolution_convert_fusion.2 = bf16[4,320,2048]{2,1,0:T(8,128)(2,1)} fusion(bf16[16,192,2048]{2,1,0:T(8,128)(2,1)} %param.13, f32[4,320,2,192]{1,3,0,2:T(8,128)S(1)} %fusion.4), kind=kOutput, calls=%fused_computation.21 | convolution fusion | flops 1010728960 | bytes 10354688 | tf_op jit(solution)/shard_map/jrf,jfd->jrd/dot_general | solution.py:79
  252.4 1.3 copy-done.2
  253.7 1.0 copy.77
  254.8 0.7 copy.78
  255.5 1.9 copy.79
  257.3 5.4 %all-to-all-start = ((bf16[8,40,2048]{2,1,0:T(8,128)(2,1)}), bf16[8,40,2048]{2,1,0:T(8,128)(2,1)S(1)}, u32[]{:S(2)}, u32[]{:S(2)}) async-start(bf16[8,40,2048]{2,1,0:T(8,128)(2,1)} %copy.79), calls=%async_computation.1 | async-start | bytes 2621440 | tf_op jit(solution)/shard_map/all_to_all | solution.py:89
  263.1 20.0 %gather_fusion.3 = bf16[1280,2048]{1,0:T(8,128)(2,1)} fusion(bf16[4128,2048]{1,0:T(8,128)(2,1)} %reshape.266, s32[2048]{0:T(1024)S(1)} %pad_clamp_fusion.1), kind=kCustom, calls=%fused_computation.3 | custom fusion | bytes 10490880 | tf_op jit(solution)/shard_map/jit(_take)/gather | solution.py:73
  283.1 7.9 %fusion.2 = f32[4,320,2,192]{1,3,0,2:T(8,128)S(1)} fusion(bf16[4,320,2048,1]{2,1,0,3:T(8,128)(2,1)} %bitcast.123, bf16[4,2,192,2048]{3,2,1,0:T(8,128)(2,1)} %get-tuple-element.25), kind=kOutput, calls=%fused_computation.9 | convolution fusion | flops 2013265920 | bytes 13500416 | tf_op jit(solution)/shard_map/jrd,jgfd->jrgf/dot_general | solution.py:75
  291.0 6.0 %convolution_convert_fusion.1 = bf16[4,320,2048]{2,1,0:T(8,128)(2,1)} fusion(bf16[16,192,2048]{2,1,0:T(8,128)(2,1)} %param.13, f32[4,320,2,192]{1,3,0,2:T(8,128)S(1)} %fusion.2), kind=kOutput, calls=%fused_computation.20 | convolution fusion | flops 1010728960 | bytes 10354688 | tf_op jit(solution)/shard_map/jrf,jfd->jrd/dot_general | solution.py:79
  297.0 9.4 %reduce-scatter.7.cloned.1.call-done = bf16[4,80,2048]{2,1,0:T(8,128)(2,1)} async-done(((bf16[4,320,2048]{2,1,0:T(8,128)(2,1)}), bf16[4,80,2048]{2,1,0:T(8,128)(2,1)}) %reduce-scatter.7.cloned.1.call-update) | async-done | bytes 1310736 | tf_op jit(solution)/shard_map/reduce_scatter | solution.py:85
  306.5 1.3 copy-done.1
  307.8 1.0 copy.83
  308.8 0.7 copy.84
  309.5 1.8 copy.85
  311.3 5.5 %all-to-all-start.1 = ((bf16[8,40,2048]{2,1,0:T(8,128)(2,1)}), bf16[8,40,2048]{2,1,0:T(8,128)(2,1)S(1)}, u32[]{:S(2)}, u32[]{:S(2)}) async-start(bf16[8,40,2048]{2,1,0:T(8,128)(2,1)} %copy.85), calls=%async_computation.3 | async-start | bytes 2621440 | tf_op jit(solution)/shard_map/all_to_all | solution.py:89
  317.4 19.8 %gather_fusion.4 = bf16[1280,2048]{1,0:T(8,128)(2,1)} fusion(bf16[4128,2048]{1,0:T(8,128)(2,1)} %reshape.266, s32[2048]{0:T(1024)S(1)} %pad_clamp_fusion), kind=kCustom, calls=%fused_computation.4 | custom fusion | bytes 10490880 | tf_op jit(solution)/shard_map/jit(_take)/gather | solution.py:73
  337.2 7.9 %fusion = f32[4,320,2,192]{1,3,0,2:T(8,128)S(1)} fusion(bf16[4,320,2048,1]{2,1,0,3:T(8,128)(2,1)} %bitcast.121, bf16[4,2,192,2048]{3,2,1,0:T(8,128)(2,1)} %get-tuple-element.24), kind=kOutput, calls=%fused_computation.7 | convolution fusion | flops 2013265920 | bytes 13500416 | tf_op jit(solution)/shard_map/jrd,jgfd->jrgf/dot_general | solution.py:75
  345.1 5.9 %convolution_convert_fusion = bf16[4,320,2048]{2,1,0:T(8,128)(2,1)} fusion(bf16[16,192,2048]{2,1,0:T(8,128)(2,1)} %param.13, f32[4,320,2,192]{1,3,0,2:T(8,128)S(1)} %fusion), kind=kOutput, calls=%fused_computation.19 | convolution fusion | flops 1010728960 | bytes 10354688 | tf_op jit(solution)/shard_map/jrf,jfd->jrd/dot_general | solution.py:79
  351.0 9.2 %reduce-scatter.9.cloned.1.call-done = bf16[4,80,2048]{2,1,0:T(8,128)(2,1)} async-done(((bf16[4,320,2048]{2,1,0:T(8,128)(2,1)}), bf16[4,80,2048]{2,1,0:T(8,128)(2,1)}) %reduce-scatter.9.cloned.1.call-update) | async-done | bytes 1310736 | tf_op jit(solution)/shard_map/reduce_scatter | solution.py:85
  360.2 2.3 copy.89
  362.6 0.7 copy.90
  363.3 1.9 copy.91
  365.2 5.7 %all-to-all-start.2 = ((bf16[8,40,2048]{2,1,0:T(8,128)(2,1)}), bf16[8,40,2048]{2,1,0:T(8,128)(2,1)}, u32[]{:S(2)}, u32[]{:S(2)}) async-start(bf16[8,40,2048]{2,1,0:T(8,128)(2,1)} %copy.91), calls=%async_computation.5 | async-start | bytes 2621440 | tf_op jit(solution)/shard_map/all_to_all | solution.py:89
  370.9 43.3 %reduce-scatter.11.cloned.1.call-done = bf16[4,80,2048]{2,1,0:T(8,128)(2,1)} async-done(((bf16[4,320,2048]{2,1,0:T(8,128)(2,1)}), bf16[4,80,2048]{2,1,0:T(8,128)(2,1)}) %reduce-scatter.11.cloned.1.call-update) | async-done | bytes 1310736 | tf_op jit(solution)/shard_map/reduce_scatter | solution.py:85
  414.2 2.3 copy.95
  416.5 0.7 copy.96
  417.3 1.8 copy.97
  419.1 5.5 %all-to-all-start.3 = ((bf16[8,40,2048]{2,1,0:T(8,128)(2,1)}), bf16[8,40,2048]{2,1,0:T(8,128)(2,1)}, u32[]{:S(2)}, u32[]{:S(2)}) async-start(bf16[8,40,2048]{2,1,0:T(8,128)(2,1)} %copy.97), calls=%async_computation.7 | async-start | bytes 2621440 | tf_op jit(solution)/shard_map/all_to_all | solution.py:89
  425.0 31.9 %all-to-all-done.3 = bf16[8,40,2048]{2,1,0:T(8,128)(2,1)} async-done(((bf16[8,40,2048]{2,1,0:T(8,128)(2,1)}), bf16[8,40,2048]{2,1,0:T(8,128)(2,1)}, u32[]{:S(2)}, u32[]{:S(2)}) %all-to-all-start.3) | async-done | bytes 1310752 | tf_op jit(solution)/shard_map/all_to_all | solution.py:89
  456.9 6.0 %pad_maximum_fusion = bf16[8,160,2048]{2,1,0:T(8,128)(2,1)} fusion(bf16[8,40,2048]{2,1,0:T(8,128)(2,1)} %all-to-all-done.3, bf16[8,40,2048]{2,1,0:T(8,128)(2,1)} %all-to-all-done.2, bf16[8,40,2048]{2,1,0:T(8,128)(2,1)S(1)} %all-to-all-done.1, bf16[8,40,2048]{2,1,0:T(8,128)(2,1)S(1)} %all-to-all-done), kind=kLoop, calls=%fused_computation.15 | loop fusion | flops 20971520 | bytes 10485760 | tf_op jit(solution)/shard_map/concatenate | solution.py:91
  462.9 12.0 %gather_fusion.5 = bf16[1024,2048]{1,0:T(8,128)(2,1)} fusion(bf16[1280,2048]{1,0:T(8,128)(2,1)} %bitcast.120, s32[1024]{0:T(1024)S(1)} %broadcast_clamp_fusion), kind=kCustom, calls=%fused_computation.5 | custom fusion | bytes 8392704 | tf_op jit(solution)/shard_map/jit(_take)/gather | solution.py:92
  475.0 3.5 fusion.8
  478.5 1.1 copy.115
  (69 shorter events, 3.9 us)
Async XLA Ops:
  6.5 8.4 %copy-start = (bf16[128,2048]{1,0:T(8,128)(2,1)S(1)}, bf16[128,2048]{1,0:T(8,128)(2,1)}, u32[]{:S(2)}) copy-start(bf16[128,2048]{1,0:T(8,128)(2,1)} %param.8) | copy-start | bytes 1572868
  6.5 8.4 %copy-start.5 = (f32[2048]{0:T(1024)S(1)}, f32[2048]{0:T(1024)}, u32[]{:S(2)}) copy-start(f32[2048]{0:T(1024)} %param.9) | copy-start | bytes 24580
  6.5 132.2 %all-gather.3.cloned.1.call-start = ((), (), s32[]{:S(2)}) async-start(), calls=%async_computation.12 | async-start | bytes 18382848 | tf_op jit(solution)/shard_map/all_gather | solution.py:56
  16.1 236.4 %reduce-scatter.5.cloned.1.call-start = ((), (), s32[]{:S(2)}) async-start(), calls=%async_computation.8 | async-start | bytes 6553600 | tf_op jit(solution)/shard_map/reduce_scatter | solution.py:85
  202.6 103.9 %reduce-scatter.7.cloned.1.call-start = ((), (), s32[]{:S(2)}) async-start(), calls=%async_computation.9 | async-start | bytes 6553600 | tf_op jit(solution)/shard_map/reduce_scatter | solution.py:85
  252.4 1.3 copy-start.2
  257.3 39.7 %all-to-all-start = ((bf16[8,40,2048]{2,1,0:T(8,128)(2,1)}), bf16[8,40,2048]{2,1,0:T(8,128)(2,1)S(1)}, u32[]{:S(2)}, u32[]{:S(2)}) async-start(bf16[8,40,2048]{2,1,0:T(8,128)(2,1)} %copy.79), calls=%async_computation.1 | async-start | bytes 2621440 | tf_op jit(solution)/shard_map/all_to_all | solution.py:89
  262.7 97.5 %reduce-scatter.9.cloned.1.call-start = ((), (), s32[]{:S(2)}) async-start(), calls=%async_computation.10 | async-start | bytes 6553600 | tf_op jit(solution)/shard_map/reduce_scatter | solution.py:85
  306.4 1.3 copy-start.1
  311.3 39.8 %all-to-all-start.1 = ((bf16[8,40,2048]{2,1,0:T(8,128)(2,1)}), bf16[8,40,2048]{2,1,0:T(8,128)(2,1)S(1)}, u32[]{:S(2)}, u32[]{:S(2)}) async-start(bf16[8,40,2048]{2,1,0:T(8,128)(2,1)} %copy.85), calls=%async_computation.3 | async-start | bytes 2621440 | tf_op jit(solution)/shard_map/all_to_all | solution.py:89
  316.8 97.4 %reduce-scatter.11.cloned.1.call-start = ((), (), s32[]{:S(2)}) async-start(), calls=%async_computation.11 | async-start | bytes 6553600 | tf_op jit(solution)/shard_map/reduce_scatter | solution.py:85
  365.2 53.9 %all-to-all-start.2 = ((bf16[8,40,2048]{2,1,0:T(8,128)(2,1)}), bf16[8,40,2048]{2,1,0:T(8,128)(2,1)}, u32[]{:S(2)}, u32[]{:S(2)}) async-start(bf16[8,40,2048]{2,1,0:T(8,128)(2,1)} %copy.91), calls=%async_computation.5 | async-start | bytes 2621440 | tf_op jit(solution)/shard_map/all_to_all | solution.py:89
  416.5 8.1 %copy-start.4 = (f32[128,8]{0,1:T(8,128)S(1)}, f32[128,8]{0,1:T(8,128)}, u32[]{:S(2)}) copy-start(f32[128,8]{0,1:T(8,128)} %param.11) | copy-start | bytes 12292
  416.5 8.3 %copy-start.3 = (s32[128,8]{0,1:T(8,128)S(1)}, s32[128,8]{0,1:T(8,128)}, u32[]{:S(2)}) copy-start(s32[128,8]{0,1:T(8,128)} %param.10) | copy-start | bytes 12292
  419.1 37.8 %all-to-all-start.3 = ((bf16[8,40,2048]{2,1,0:T(8,128)(2,1)}), bf16[8,40,2048]{2,1,0:T(8,128)(2,1)}, u32[]{:S(2)}, u32[]{:S(2)}) async-start(bf16[8,40,2048]{2,1,0:T(8,128)(2,1)} %copy.97), calls=%async_computation.7 | async-start | bytes 2621440 | tf_op jit(solution)/shard_map/all_to_all | solution.py:89
Sparse Core Ops, SparseCore 0:
  16.2 122.5 all-gather.2
  202.7 49.5 reduce-scatter.4
  255.0 51.4 reduce-scatter.6
  308.8 51.3 reduce-scatter.8
  362.8 51.3 reduce-scatter.10
